TPU v7x, 32 devices: a whole 2x2x4 slice. The times are simulated.
32 devices in a mesh: img: 4 (over z), gx: 4 (over x, core), gy: 2 (over y).
Axes of the slice: x: 2, y: 2, z: 4, core: 2. Of those that a mesh axis runs over, the one named last changes fastest.
Arguments:
- spins: float32 [4, 3, 128, 128, 128], P('img', None, 'gx', 'gy'), may hold values from -1 to 1, as said below
- velocity: float32 [4, 3, 128, 128, 128], P('img', None, 'gx', 'gy'), may hold values from -3 to 3
- upwind: int32 [4], P('img'), may hold values from -1 to 1
- climber: int32 [1], replicated, may hold values from 1 to 2
- coupling: float32 [3], replicated, may hold values from 0.5 to 1.5
Outputs:
- new_spins: float32 [4, 3, 128, 128, 128], P('img', None, 'gx', 'gy')
- new_velocity: float32 [4, 3, 128, 128, 128], P('img', None, 'gx', 'gy')
- spacing: float32 [4, 2], P('img')
Inputs may be any that keep to these rules, and one draw needn't show every extreme that they name: Every cell of spins is a unit vector.
All inputs are finite; a program needn't handle non-finite values.
Results may differ from a plain program's by a relative error of at most 0.0003.
Values sent between devices are 32-bit elements; how exact they have to be, the bound alone decides.
No kernel may reach another device: no remote copies, remote signals or barrier semaphores. Data moves between devices by JAX's collectives and lax.ppermute only.
A program may use at most 64 MiB of HBM per device.

v0:
```python
import jax
import jax.numpy as jnp
from jax import lax
from jax.sharding import PartitionSpec as P

TIME_STEP = 0.1
SPRING = 2.0
EPSILON = 1e-06


def extended(block, sides, width):
    for axis, dim in sides:
        count = lax.axis_size(axis)
        forward = [(i, i + 1) for i in range(count - 1)]
        forward.append((count - 1, 0))
        backward = [(target, source) for source, target in forward]
        low = lax.ppermute(
            lax.slice_in_dim(block, block.shape[dim] - width, None, axis=dim), axis, forward
        )
        high = lax.ppermute(lax.slice_in_dim(block, 0, width, axis=dim), axis, backward)
        block = jnp.concatenate([low, block, high], axis=dim)
    return block


def from_behind(value, axis, by):
    size = lax.axis_size(axis)
    pairs = [(i, i + by) for i in range(size) if 0 <= i + by < size]
    return lax.ppermute(value, axis, pairs)


def cell_dot(left, right):
    return jnp.sum(left * right, axis=1, keepdims=True)


def lattice_field(state, coupling):
    padded = extended(state, (("gx", 2), ("gy", 3)), 1)
    plus_x = padded[:, :, 2:, 1:-1]
    minus_x = padded[:, :, :-2, 1:-1]
    plus_y = padded[:, :, 1:-1, 2:]
    minus_y = padded[:, :, 1:-1, :-2]
    zpadded = jnp.pad(state, ((0, 0), (0, 0), (0, 0), (0, 0), (1, 1)))
    plus_z = zpadded[..., 2:]
    minus_z = zpadded[..., :-2]
    diff_x = plus_x - minus_x
    diff_y = plus_y - minus_y
    diff_z = plus_z - minus_z
    twist = jnp.stack(
        [diff_y[:, 2] - diff_z[:, 1], diff_z[:, 0] - diff_x[:, 2], diff_x[:, 1] - diff_y[:, 0]], 1
    )
    neighbours = plus_x + minus_x + plus_y + minus_y + plus_z + minus_z
    lift = jnp.array([0.0, 0.0, 1.0], jnp.float32).reshape(1, 3, 1, 1, 1)
    return coupling[0] * neighbours + coupling[1] * twist + coupling[2] * lift


def per_device(spins, velocity, upwind, climber, coupling):
    count = spins.shape[0]
    total = count * lax.axis_size("img")
    cells = (
        spins.shape[2] * spins.shape[3] * spins.shape[4] * lax.axis_size("gx") * lax.axis_size("gy")
    )
    root_cells = jnp.sqrt(jnp.asarray(cells, jnp.float32))
    indices = lax.axis_index("img") * count + jnp.arange(count, dtype=jnp.int32)
    axes_all = (1, 2, 3, 4)
    ahead = from_behind(spins, "img", -1)
    after = jnp.concatenate([spins[1:], ahead], 0)
    forward = after - spins
    forward_part = jnp.sum(forward * forward, axis=axes_all)
    behind = from_behind(spins, "img", 1)
    before = jnp.concatenate([behind, spins[:-1]], 0)
    backward = spins - before
    backward_part = jnp.sum(backward * backward, axis=axes_all)
    field = lattice_field(spins, coupling)
    perp_field = field - cell_dot(field, spins) * spins
    direction = upwind.reshape(count, 1, 1, 1, 1)
    raw = jnp.where(direction > 0, forward, jnp.where(direction < 0, backward, forward + backward))
    tangent_perp = raw - cell_dot(raw, spins) * spins
    tangent_part = jnp.sum(tangent_perp * tangent_perp, axis=axes_all)
    norm_t, next_sq, prev_sq = lax.psum((tangent_part, forward_part, backward_part), ("gx", "gy"))
    scale = 1.0 / jnp.sqrt(norm_t + EPSILON)
    tau = tangent_perp * scale.reshape(count, 1, 1, 1, 1)
    along = lax.psum(jnp.sum(perp_field * tau, axis=axes_all), ("gx", "gy"))
    dist_next = jnp.sqrt(next_sq + EPSILON)
    dist_prev = jnp.sqrt(prev_sq + EPSILON)
    spacing = jnp.stack([dist_next, dist_prev], 1) / root_cells
    climbing = indices == climber[0]
    ending = (indices == 0) | (indices == total - 1)
    weight = jnp.where(climbing, 2.0 * along, along - SPRING * (dist_next - dist_prev))
    force = perp_field - weight.reshape(count, 1, 1, 1, 1) * tau
    force = jnp.where(ending.reshape(count, 1, 1, 1, 1), jnp.zeros_like(force), force)
    projected = (
        jnp.maximum(cell_dot(velocity, force), 0.0)
        / jnp.maximum(cell_dot(force, force), 1.0)
        * force
    )
    speed_new = projected + TIME_STEP * force
    moved = spins + TIME_STEP * speed_new
    return (moved / jnp.sqrt(cell_dot(moved, moved)), speed_new, spacing)


def solution(mesh):
    return jax.shard_map(
        per_device,
        mesh=mesh,
        in_specs=(
            P("img", None, "gx", "gy", None),
            P("img", None, "gx", "gy", None),
            P("img"),
            P(),
            P(),
        ),
        out_specs=(
            P("img", None, "gx", "gy", None),
            P("img", None, "gx", "gy", None),
            P("img", None),
        ),
        check_vma=False,
    )
```

profile of v0, /device:TPU:16, one launch (start us, length us, event | category | flops | bytes accessed | tf_op | source)
XLA Modules:
  0.0 138.6 jit_solution(8237169492378314667)
XLA Ops:
  0.6 2.4 %collective-permute-start.4 = (f32[1,3,32,64,128]{4,3,2,1,0:T(8,128)}, f32[1,3,32,64,128]{4,3,2,1,0:T(8,128)}, u32[]{:S(2)}, u32[]{:S(2)}) collective-permute-start(f32[1,3,32,64,128]{4,3,2,1,0:T(8,128)} %param.6), channel_id=1, source_target_pairs={{8,0},{16,8},{24,16},{9,1},{17,9},{25,17},{10,2},{18,10},{26,18},{... | collective-permute-start | bytes 9437192 | tf_op jit(solution)/shard_map/ppermute | solution.py:28
  3.0 5.2 %collective-permute-start.5 = (f32[1,3,32,64,128]{4,3,2,1,0:T(8,128)}, f32[1,3,32,64,128]{4,3,2,1,0:T(8,128)}, u32[]{:S(2)}, u32[]{:S(2)}) collective-permute-start(f32[1,3,32,64,128]{4,3,2,1,0:T(8,128)} %param.6), channel_id=1, source_target_pairs={{0,8},{8,16},{16,24},{1,9},{9,17},{17,25},{2,10},{10,18},{18,26},{... | collective-permute-start | bytes 9437192 | tf_op jit(solution)/shard_map/ppermute | solution.py:28
  8.2 1.0 fusion.8
  9.2 0.1 collective-permute-start.1
  9.2 1.7 %collective-permute-start = (f32[1,3,1,64,128]{4,3,2,1,0:T(8,128)S(1)}, f32[1,3,1,64,128]{4,3,2,1,0:T(8,128)S(1)}, u32[]{:S(2)}, u32[]{:S(2)}) collective-permute-start(f32[1,3,1,64,128]{4,3,2,1,0:T(8,128)S(1)} %get-tuple-element.26), channel_id=1, source_target_pairs={{2,0},{4,2},{6,4},{0,6},{3,1},{5,3},{7,5},{1,7},{10,8},{12,10},{14... | collective-permute-start | bytes 294920 | tf_op jit(solution)/shard_map/ppermute | solution.py:20
  11.0 1.4 %fusion.9 = (f32[1]{0:T(128)}, f32[1]{0:T(128)}, f32[1]{0:T(128)}) fusion(f32[3]{0:T(128)} %param.10), kind=kLoop, calls=%fused_computation.40 | loop fusion | bytes 24 | tf_op jit(solution)/shard_map/slice | solution.py:52
  12.4 0.9 collective-permute-done.1
  13.3 0.0 copy-start.6
  13.3 0.0 collective-permute-done
  13.3 9.6 %fusion.3 = (f32[1,3,32,64,128]{4,3,2,1,0:T(8,128)}, f32[1,3,34,64,128]{4,3,2,1,0:T(8,128)S(1)}, f32[1,3,32,64,128]{4,3,2,1,0:T(8,128)}) fusion(f32[1,3,32,64,128]{4,3,2,1,0:T(8,128)} %param.6, f32[1,3,34,64,128]{4,3,2,1,0:T(8,128)S(1)} %constant_dynamic-update-slice_fusion.2, f32[1,3,1,64,128]{4,3,2,1,0:T(8,128)S(1)} %collective-permute-done.1, ...), kind=kLoop, calls=%fused_computation.24 | loop fusion | flops 3145728 | bytes 12779520 | tf_op jit(solution)/shard_map/sub | solution.py:46
  23.0 0.8 fusion.7
  23.8 1.5 %collective-permute-start.2 = (f32[1,3,34,1,128]{4,3,2,1,0:T(1,128)}, f32[1,3,34,1,128]{4,3,2,1,0:T(1,128)}, u32[]{:S(2)}, u32[]{:S(2)}) collective-permute-start(f32[1,3,34,1,128]{4,3,2,1,0:T(1,128)} %get-tuple-element.19), channel_id=1, source_target_pairs={{1,0},{0,1},{3,2},{2,3},{5,4},{4,5},{7,6},{6,7},{9,8},{8,9},{11,10... | collective-permute-start | bytes 156680 | tf_op jit(solution)/shard_map/ppermute | solution.py:20
  25.3 0.5 collective-permute-start.3
  25.8 0.6 broadcast_multiply_fusion.1
  27.8 0.0 copy-start.4
  27.8 0.4 collective-permute-done.2
  28.2 1.5 %collective-permute-done.3 = f32[1,3,34,1,128]{4,3,2,1,0:T(1,128)} collective-permute-done((f32[1,3,34,1,128]{4,3,2,1,0:T(1,128)}, f32[1,3,34,1,128]{4,3,2,1,0:T(1,128)}, u32[]{:S(2)}, u32[]{:S(2)}) %collective-permute-start.3) | collective-permute-done | bytes 52256 | tf_op jit(solution)/shard_map/ppermute | solution.py:17
  29.8 1.6 %fusion.5 = f32[1,3,32,64,128]{4,3,2,1,0:T(8,128)S(1)} fusion(f32[1,3,34,1,128]{4,3,2,1,0:T(1,128)} %collective-permute-done.2, f32[1,3,34,64,128]{4,3,2,1,0:T(8,128)S(1)} %constant_dynamic-update-slice_fusion, f32[1,3,34,1,128]{4,3,2,1,0:T(1,128)} %collective-permute-done.3), kind=kLoop, calls=%fused_computation.26 | loop fusion | flops 2359296 | bytes 6592512 | tf_op jit(solution)/shard_map/sub | solution.py:45
  31.5 2.1 %slice_subtract_fusion.2 = (f32[1,1,32,64,128]{4,3,2,1,0:T(8,128)S(1)}, f32[1,1,32,64,128]{4,3,2,1,0:T(8,128)}, f32[1,1,32,64,128]{4,3,2,1,0:T(8,128)}) fusion(f32[1,3,32,64,128]{4,3,2,1,0:T(8,128)S(1)} %copy-done.4, f32[1,3,32,64,128]{4,3,2,1,0:T(8,128)S(1)} %fusion.5, f32[1,3,32,64,128]{4,3,2,1,0:T(8,128)S(1)} %copy-done.5), kind=kLoop, calls=%fused_computation.31 | loop fusion | flops 786432 | bytes 9437184 | tf_op jit(solution)/shard_map/sub | solution.py:48
  33.5 39.1 %collective-permute-done.4 = f32[1,3,32,64,128]{4,3,2,1,0:T(8,128)} collective-permute-done((f32[1,3,32,64,128]{4,3,2,1,0:T(8,128)}, f32[1,3,32,64,128]{4,3,2,1,0:T(8,128)}, u32[]{:S(2)}, u32[]{:S(2)}) %collective-permute-start.4) | collective-permute-done | bytes 3145760 | tf_op jit(solution)/shard_map/ppermute | solution.py:28
  72.7 2.9 %collective-permute-done.5 = f32[1,3,32,64,128]{4,3,2,1,0:T(8,128)} collective-permute-done((f32[1,3,32,64,128]{4,3,2,1,0:T(8,128)}, f32[1,3,32,64,128]{4,3,2,1,0:T(8,128)}, u32[]{:S(2)}, u32[]{:S(2)}) %collective-permute-start.5) | collective-permute-done | bytes 3145760 | tf_op jit(solution)/shard_map/ppermute | solution.py:28
  75.6 10.3 %multiply_reduce_fusion.3 = (f32[]{:T(128)}, f32[32,64,128]{2,1,0:T(8,128)S(1)}, f32[]{:T(128)}, f32[32,64,128]{2,1,0:T(8,128)}, f32[1,3,32,64,128]{4,3,2,1,0:T(8,128)}) fusion(f32[1,3,32,64,128]{4,3,2,1,0:T(8,128)S(1)} %copy-done, f32[1,3,32,64,128]{4,3,2,1,0:T(8,128)} %collective-permute-done.5, pred[]{:T(512)} %bitcast.6, ...), kind=kLoop, calls=%fused_computation.16 | loop fusion | flops 21495806 | bytes 21469214 | tf_op jit(solution)/shard_map/reduce_sum | solution.py:71
  85.8 6.3 %multiply_reduce_fusion.6 = (f32[]{:T(128)}, f32[1,3,32,64,128]{4,3,2,1,0:T(8,128)}) fusion(f32[1,3,32,64,128]{4,3,2,1,0:T(8,128)S(1)} %copy-done, f32[32,64,128]{2,1,0:T(8,128)S(1)} %get-tuple-element.4, f32[1,3,32,64,128]{4,3,2,1,0:T(8,128)} %collective-permute-done.5, pred[]{:T(512)} %bitcast.6, f32[1,3,32,64,128]{4,3,2,1,0:T(8,128)} %collective-permute-done.4, ...), kind=kLoop, calls=%fused_computation.19 | loop fusion | flops 7077887 | bytes 13631494 | tf_op jit(solution)/shard_map/reduce_sum | solution.py:77
  92.2 14.1 %psum.28 = f32[1]{0:T(128)} all-reduce(f32[1]{0:T(128)} %bitcast.7), channel_id=1, replica_groups=mesh['img'=4,'gx'=4,'gy'=2] {'gx','gy'}, use_global_device_ids=true, to_apply=%region_3.4 | all-reduce | flops 1 | bytes 8 | tf_op jit(solution)/shard_map/psum | solution.py:78
  106.9 4.5 %multiply_reduce_fusion.5 = f32[]{:T(128)} fusion(f32[1,3,32,64,128]{4,3,2,1,0:T(8,128)} %get-tuple-element.16, f32[]{:T(128)} %bitcast.8, f32[1,3,32,64,128]{4,3,2,1,0:T(8,128)} %get-tuple-element.17, f32[1,3,32,64,128]{4,3,2,1,0:T(8,128)S(1)} %copy-done, f32[32,64,128]{2,1,0:T(8,128)} %get-tuple-element.8), kind=kLoop, calls=%fused_computation.18 | loop fusion | flops 3932159 | bytes 10485768 | tf_op jit(solution)/shard_map/reduce_sum | solution.py:81
  111.5 13.6 %all-reduce.1 = (f32[1]{0:T(128)}, f32[1]{0:T(128)}, f32[1]{0:T(128)}) all-reduce(f32[1]{0:T(128)} %bitcast.9, f32[1]{0:T(128)} %bitcast.10, f32[1]{0:T(128)} %bitcast.11), channel_id=1, replica_groups=mesh['img'=4,'gx'=4,'gy'=2] {'gx','gy'}, use_global_device_ids=true, to_apply=%region_5.6 | all-reduce | flops 3 | bytes 24 | tf_op jit(solution)/shard_map/psum | solution.py:81
  127.7 6.1 %multiply_reduce_fusion.2 = (f32[32,64,128]{2,1,0:T(8,128)S(1)}, f32[32,64,128]{2,1,0:T(8,128)S(1)}, f32[1,3,32,64,128]{4,3,2,1,0:T(8,128)S(1)}) fusion(f32[1,3,32,64,128]{4,3,2,1,0:T(8,128)} %param.7, f32[1,3,32,64,128]{4,3,2,1,0:T(8,128)} %get-tuple-element.16, f32[]{:T(128)} %bitcast.8, f32[]{:T(128)} %bitcast.12, ...), kind=kLoop, calls=%fused_computation.14 | loop fusion | flops 7340032 | bytes 18874376 | tf_op jit(solution)/shard_map/reduce_sum | solution.py:32
  133.8 0.3 divide_add_fusion
  134.1 1.0 multiply_reduce_fusion
  135.0 0.2 sqrt.20
  135.3 0.8 maximum_multiply_fusion.1
  136.1 2.5 %broadcast_divide_fusion = f32[1,3,32,64,128]{4,3,2,1,0:T(8,128)} fusion(f32[32,64,128]{2,1,0:T(8,128)S(1)} %sqrt.20, f32[1,3,32,64,128]{4,3,2,1,0:T(8,128)S(1)} %copy-done, f32[1,3,32,64,128]{4,3,2,1,0:T(8,128)S(1)} %get-tuple-element.13), kind=kLoop, calls=%fused_computation.28 | loop fusion | flops 2359296 | bytes 10485760 | tf_op jit(solution)/shard_map/div | solution.py:97
  (14 shorter events, 0.0 us)
Async XLA Ops:
  0.6 72.1 %collective-permute-start.4 = (f32[1,3,32,64,128]{4,3,2,1,0:T(8,128)}, f32[1,3,32,64,128]{4,3,2,1,0:T(8,128)}, u32[]{:S(2)}, u32[]{:S(2)}) collective-permute-start(f32[1,3,32,64,128]{4,3,2,1,0:T(8,128)} %param.6), channel_id=1, source_target_pairs={{8,0},{16,8},{24,16},{9,1},{17,9},{25,17},{10,2},{18,10},{26,18},{... | collective-permute-start | bytes 9437192 | tf_op jit(solution)/shard_map/ppermute | solution.py:28
  3.0 72.6 %collective-permute-start.5 = (f32[1,3,32,64,128]{4,3,2,1,0:T(8,128)}, f32[1,3,32,64,128]{4,3,2,1,0:T(8,128)}, u32[]{:S(2)}, u32[]{:S(2)}) collective-permute-start(f32[1,3,32,64,128]{4,3,2,1,0:T(8,128)} %param.6), channel_id=1, source_target_pairs={{0,8},{8,16},{16,24},{1,9},{9,17},{17,25},{2,10},{10,18},{18,26},{... | collective-permute-start | bytes 9437192 | tf_op jit(solution)/shard_map/ppermute | solution.py:28
  9.2 4.1 %collective-permute-start.1 = (f32[1,3,1,64,128]{4,3,2,1,0:T(8,128)S(1)}, f32[1,3,1,64,128]{4,3,2,1,0:T(8,128)S(1)}, u32[]{:S(2)}, u32[]{:S(2)}) collective-permute-start(f32[1,3,1,64,128]{4,3,2,1,0:T(8,128)S(1)} %get-tuple-element.27), channel_id=1, source_target_pairs={{0,2},{2,4},{4,6},{6,0},{1,3},{3,5},{5,7},{7,1},{8,10},{10,12},{12... | collective-permute-start | bytes 294920 | tf_op jit(solution)/shard_map/ppermute | solution.py:17
  9.2 4.1 %collective-permute-start = (f32[1,3,1,64,128]{4,3,2,1,0:T(8,128)S(1)}, f32[1,3,1,64,128]{4,3,2,1,0:T(8,128)S(1)}, u32[]{:S(2)}, u32[]{:S(2)}) collective-permute-start(f32[1,3,1,64,128]{4,3,2,1,0:T(8,128)S(1)} %get-tuple-element.26), channel_id=1, source_target_pairs={{2,0},{4,2},{6,4},{0,6},{3,1},{5,3},{7,5},{1,7},{10,8},{12,10},{14... | collective-permute-start | bytes 294920 | tf_op jit(solution)/shard_map/ppermute | solution.py:20
  13.3 12.6 %copy-start.6 = (f32[3]{0:T(128)S(1)}, f32[3]{0:T(128)}, u32[]{:S(2)}) copy-start(f32[3]{0:T(128)} %constant.32.clone) | copy-start | bytes 40
  23.0 8.5 %copy-start.1 = (f32[1,3,34,64,128]{4,3,2,1,0:T(8,128)}, f32[1,3,34,64,128]{4,3,2,1,0:T(8,128)S(1)}, u32[]{:S(2)}) copy-start(f32[1,3,34,64,128]{4,3,2,1,0:T(8,128)S(1)} %constant_dynamic-update-slice_fusion) | copy-start | bytes 10027012
  23.8 4.4 %collective-permute-start.2 = (f32[1,3,34,1,128]{4,3,2,1,0:T(1,128)}, f32[1,3,34,1,128]{4,3,2,1,0:T(1,128)}, u32[]{:S(2)}, u32[]{:S(2)}) collective-permute-start(f32[1,3,34,1,128]{4,3,2,1,0:T(1,128)} %get-tuple-element.19), channel_id=1, source_target_pairs={{1,0},{0,1},{3,2},{2,3},{5,4},{4,5},{7,6},{6,7},{9,8},{8,9},{11,10... | collective-permute-start | bytes 156680 | tf_op jit(solution)/shard_map/ppermute | solution.py:20
  25.3 4.5 %collective-permute-start.3 = (f32[1,3,34,1,128]{4,3,2,1,0:T(1,128)}, f32[1,3,34,1,128]{4,3,2,1,0:T(1,128)}, u32[]{:S(2)}, u32[]{:S(2)}) collective-permute-start(f32[1,3,34,1,128]{4,3,2,1,0:T(1,128)} %get-tuple-element.18), channel_id=1, source_target_pairs={{0,1},{1,0},{2,3},{3,2},{4,5},{5,4},{6,7},{7,6},{8,9},{9,8},{10,11... | collective-permute-start | bytes 156680 | tf_op jit(solution)/shard_map/ppermute | solution.py:17
  27.8 3.7 %copy-start.4 = (f32[1,3,32,64,128]{4,3,2,1,0:T(8,128)S(1)}, f32[1,3,32,64,128]{4,3,2,1,0:T(8,128)}, u32[]{:S(2)}) copy-start(f32[1,3,32,64,128]{4,3,2,1,0:T(8,128)} %get-tuple-element.23) | copy-start | bytes 9437188
  27.8 3.7 %copy-start.5 = (f32[1,3,32,64,128]{4,3,2,1,0:T(8,128)S(1)}, f32[1,3,32,64,128]{4,3,2,1,0:T(8,128)}, u32[]{:S(2)}) copy-start(f32[1,3,32,64,128]{4,3,2,1,0:T(8,128)} %get-tuple-element.25) | copy-start | bytes 9437188
  31.4 44.1 %copy-start = (f32[1,3,32,64,128]{4,3,2,1,0:T(8,128)S(1)}, f32[1,3,32,64,128]{4,3,2,1,0:T(8,128)}, u32[]{:S(2)}) copy-start(f32[1,3,32,64,128]{4,3,2,1,0:T(8,128)} %param.6) | copy-start | bytes 9437188
  31.5 44.1 %copy-start.2 = (f32[1,3,34,64,128]{4,3,2,1,0:T(8,128)S(1)}, f32[1,3,34,64,128]{4,3,2,1,0:T(8,128)}, u32[]{:S(2)}) copy-start(f32[1,3,34,64,128]{4,3,2,1,0:T(8,128)} %copy-done.1) | copy-start | bytes 10027012
  135.0 3.6 %copy-start.3 = (f32[1,3,32,64,128]{4,3,2,1,0:T(8,128)}, f32[1,3,32,64,128]{4,3,2,1,0:T(8,128)S(1)}, u32[]{:S(2)}) copy-start(f32[1,3,32,64,128]{4,3,2,1,0:T(8,128)S(1)} %get-tuple-element.13) | copy-start | bytes 9437188
where the time goes:
time: 140 us; the launch traced here: 139 us
  other arithmetic  45.8 us (33%)
  waiting for transfers between devices  44.9 us (32%)
  blocking collectives  27.6 us (20%)
  starting transfers between devices  11.4 us (8%)
  between operations  5.46 us (4%)
  local copies, waits for them, and re-layouts  3.47 us (2%)
    ppermute x2, waiting for transfers between devices, from_behind(): return lax.ppermute(value, axis, pairs)  42 us
    psum x1, blocking collectives, per_device(): lax.psum((tangent_part, forward_part, backward_part), ('gx', 'gy'))  14.1 us
    psum x1, blocking collectives, per_device(): along = lax.psum(jnp.sum(perp_field * tau, axis=axes_all), ('gx', 'gy'))  13.6 us
    reduce_sum x1, other arithmetic, per_device(): backward_part = jnp.sum(backward * backward, axis=axes_all)  10.3 us
    sub x1, other arithmetic, lattice_field(): diff_z = plus_z - minus_z  9.64 us
    ppermute x2, starting transfers between devices, from_behind(): return lax.ppermute(value, axis, pairs)  7.55 us
    reduce_sum x2, other arithmetic, cell_dot(): return jnp.sum(left * right, axis=1, keepdims=True)  7.03 us
    reduce_sum x1, other arithmetic, per_device(): tangent_part = jnp.sum(tangent_perp * tangent_perp, axis=axes_all)  6.35 us
  transfers between devices with their start and end apart: 6, of which 5 were waited for; matrix products, arithmetic and copies ran while one was open for 12% of the time, Pallas kernels for 0%

commit v1 on v0

--- a/solution.py
+++ b/solution.py
@@ -26,6 +26,20 @@
     size = lax.axis_size(axis)
     pairs = [(i, i + by) for i in range(size) if 0 <= i + by < size]
     return lax.ppermute(value, axis, pairs)
+
+
+def group_sum(value, axes):
+    for axis in axes:
+        size = lax.axis_size(axis)
+        if size & (size - 1):
+            value = lax.psum(value, axis)
+            continue
+        step = 1
+        while step < size:
+            pairs = [(i, i ^ step) for i in range(size)]
+            value = value + lax.ppermute(value, axis, pairs)
+            step *= 2
+    return value
 
 
 def cell_dot(left, right):
@@ -61,32 +75,38 @@
     root_cells = jnp.sqrt(jnp.asarray(cells, jnp.float32))
     indices = lax.axis_index("img") * count + jnp.arange(count, dtype=jnp.int32)
     axes_all = (1, 2, 3, 4)
-    ahead = from_behind(spins, "img", -1)
-    after = jnp.concatenate([spins[1:], ahead], 0)
-    forward = after - spins
-    forward_part = jnp.sum(forward * forward, axis=axes_all)
-    behind = from_behind(spins, "img", 1)
-    before = jnp.concatenate([behind, spins[:-1]], 0)
-    backward = spins - before
-    backward_part = jnp.sum(backward * backward, axis=axes_all)
+    ahead = from_behind(spins[:1], "img", -1)
+    behind = from_behind(spins[-1:], "img", 1)
     field = lattice_field(spins, coupling)
     perp_field = field - cell_dot(field, spins) * spins
+    after = jnp.concatenate([spins[1:], ahead], 0)
+    before = jnp.concatenate([behind, spins[:-1]], 0)
+    forward = after - spins
+    backward = spins - before
     direction = upwind.reshape(count, 1, 1, 1, 1)
     raw = jnp.where(direction > 0, forward, jnp.where(direction < 0, backward, forward + backward))
     tangent_perp = raw - cell_dot(raw, spins) * spins
-    tangent_part = jnp.sum(tangent_perp * tangent_perp, axis=axes_all)
-    norm_t, next_sq, prev_sq = lax.psum((tangent_part, forward_part, backward_part), ("gx", "gy"))
+    parts = jnp.stack(
+        [
+            jnp.sum(tangent_perp * tangent_perp, axis=axes_all),
+            jnp.sum(perp_field * tangent_perp, axis=axes_all),
+            jnp.sum(forward * forward, axis=axes_all),
+            jnp.sum(backward * backward, axis=axes_all),
+        ],
+        1,
+    )
+    norm_t, along_t, next_sq, prev_sq = jnp.moveaxis(group_sum(parts, ("gy", "gx")), 1, 0)
     scale = 1.0 / jnp.sqrt(norm_t + EPSILON)
-    tau = tangent_perp * scale.reshape(count, 1, 1, 1, 1)
-    along = lax.psum(jnp.sum(perp_field * tau, axis=axes_all), ("gx", "gy"))
+    along = along_t * scale
     dist_next = jnp.sqrt(next_sq + EPSILON)
     dist_prev = jnp.sqrt(prev_sq + EPSILON)
     spacing = jnp.stack([dist_next, dist_prev], 1) / root_cells
     climbing = indices == climber[0]
     ending = (indices == 0) | (indices == total - 1)
     weight = jnp.where(climbing, 2.0 * along, along - SPRING * (dist_next - dist_prev))
-    force = perp_field - weight.reshape(count, 1, 1, 1, 1) * tau
-    force = jnp.where(ending.reshape(count, 1, 1, 1, 1), jnp.zeros_like(force), force)
+    weight = jnp.where(ending, 0.0, weight * scale)
+    keep = jnp.where(ending, 0.0, 1.0).reshape(count, 1, 1, 1, 1)
+    force = keep * perp_field - weight.reshape(count, 1, 1, 1, 1) * tangent_perp
     projected = (
         jnp.maximum(cell_dot(velocity, force), 0.0)
         / jnp.maximum(cell_dot(force, force), 1.0)

time: 140 us -> 118 us (0.84)
  blocking collectives: 27.6 us -> 0 us
  waiting for transfers between devices: 44.9 us -> 50.2 us
  starting transfers between devices: 11.4 us -> 14.3 us
  other arithmetic: 45.8 us -> 43.5 us
    psum x2 -> x0, blocking collectives: 27.6 us -> none  [the longest x1 14.1 us: per_device(): lax.psum((tangent_part, forward_part, backward_part), ('gx', 'gy'))]
    reduce_sum x3 -> x2, other arithmetic: 21.1 us -> 13 us  [the longest x1 8.87 us: per_device(): jnp.sum(forward * forward, axis=axes_all)]
    ppermute x0 -> x3, waiting for transfers between devices: none -> 5.18 us  [group_sum(): value = value + lax.ppermute(value, axis, pairs)]
    add x0 -> x3, other arithmetic: none -> 5.17 us  [group_sum(): value = value + lax.ppermute(value, axis, pairs)]
    ppermute x0 -> x3, starting transfers between devices: none -> 3.03 us  [group_sum(): value = value + lax.ppermute(value, axis, pairs)]
    another operation x0 -> x1, other arithmetic: none -> 2.58 us  [per_device(): jnp.stack([jnp.sum(tangent_perp * tangent_perp, axis=axes_all), jnp.sum(p...]
    reduce_sum x2, other arithmetic: 7.03 us -> 5.32 us  [cell_dot(): return jnp.sum(left * right, axis=1, keepdims=True)]
  transfers between devices with their start and end apart: 6 -> 9, of which waited for: 5 -> 8; matrix products, arithmetic and copies ran while one was open for 12% -> 15% of each run, Pallas kernels for 0% -> 0%
where the time goes in v1:
time: 118 us; the launch traced here: 117 us
  waiting for transfers between devices  50.2 us (43%)
  other arithmetic  43.5 us (37%)
  starting transfers between devices  14.3 us (12%)
  between operations  4.88 us (4%)
  local copies, waits for them, and re-layouts  4.02 us (3%)
    ppermute x2, waiting for transfers between devices, from_behind(): return lax.ppermute(value, axis, pairs)  42.2 us
    sub x1, other arithmetic, lattice_field(): diff_z = plus_z - minus_z  9.84 us
    reduce_sum x1, other arithmetic, per_device(): jnp.sum(forward * forward, axis=axes_all)  8.87 us
    ppermute x2, starting transfers between devices, from_behind(): return lax.ppermute(value, axis, pairs)  7.5 us
    reduce_sum x2, other arithmetic, cell_dot(): return jnp.sum(left * right, axis=1, keepdims=True)  5.32 us
    ppermute x3, waiting for transfers between devices, group_sum(): value = value + lax.ppermute(value, axis, pairs)  5.18 us
    add x3, other arithmetic, group_sum(): value = value + lax.ppermute(value, axis, pairs)  5.17 us
    reduce_sum x1, other arithmetic, per_device(): jnp.sum(tangent_perp * tangent_perp, axis=axes_all)  4.17 us
  transfers between devices with their start and end apart: 9, of which 8 were waited for; matrix products, arithmetic and copies ran while one was open for 15% of the time, Pallas kernels for 0%

profile of v1, /device:TPU:16, one launch (start us, length us, event | category | flops | bytes accessed | tf_op | source)
XLA Modules:
  0.0 117.0 jit_solution(12986385620269873746)
XLA Ops:
  0.6 2.4 %collective-permute-start.4 = (f32[1,3,32,64,128]{4,3,2,1,0:T(8,128)}, f32[1,3,32,64,128]{4,3,2,1,0:T(8,128)}, u32[]{:S(2)}, u32[]{:S(2)}) collective-permute-start(f32[1,3,32,64,128]{4,3,2,1,0:T(8,128)} %param.6), channel_id=1, source_target_pairs={{8,0},{16,8},{24,16},{9,1},{17,9},{25,17},{10,2},{18,10},{26,18},{... | collective-permute-start | bytes 9437192 | tf_op jit(solution)/shard_map/ppermute | solution.py:28
  3.0 5.1 %collective-permute-start.5 = (f32[1,3,32,64,128]{4,3,2,1,0:T(8,128)}, f32[1,3,32,64,128]{4,3,2,1,0:T(8,128)}, u32[]{:S(2)}, u32[]{:S(2)}) collective-permute-start(f32[1,3,32,64,128]{4,3,2,1,0:T(8,128)} %param.6), channel_id=1, source_target_pairs={{0,8},{8,16},{16,24},{1,9},{9,17},{17,25},{2,10},{10,18},{18,26},{... | collective-permute-start | bytes 9437192 | tf_op jit(solution)/shard_map/ppermute | solution.py:28
  8.1 1.0 fusion.8
  9.2 1.7 %collective-permute-start = (f32[1,3,1,64,128]{4,3,2,1,0:T(8,128)S(1)}, f32[1,3,1,64,128]{4,3,2,1,0:T(8,128)S(1)}, u32[]{:S(2)}, u32[]{:S(2)}) collective-permute-start(f32[1,3,1,64,128]{4,3,2,1,0:T(8,128)S(1)} %get-tuple-element.24), channel_id=1, source_target_pairs={{2,0},{4,2},{6,4},{0,6},{3,1},{5,3},{7,5},{1,7},{10,8},{12,10},{14... | collective-permute-start | bytes 294920 | tf_op jit(solution)/shard_map/ppermute | solution.py:20
  10.9 1.4 %fusion.10 = (f32[1]{0:T(128)}, f32[1]{0:T(128)}, f32[1]{0:T(128)}) fusion(f32[3]{0:T(128)} %param.10), kind=kLoop, calls=%fused_computation.42 | loop fusion | bytes 24 | tf_op jit(solution)/shard_map/slice | solution.py:66
  12.3 0.9 collective-permute-done.1
  13.3 9.8 %fusion.3 = (f32[1,3,32,64,128]{4,3,2,1,0:T(8,128)}, f32[1,3,34,64,128]{4,3,2,1,0:T(8,128)S(1)}, f32[1,3,32,64,128]{4,3,2,1,0:T(8,128)}) fusion(f32[1,3,32,64,128]{4,3,2,1,0:T(8,128)} %param.6, f32[1,3,34,64,128]{4,3,2,1,0:T(8,128)S(1)} %constant_dynamic-update-slice_fusion.2, f32[1,3,1,64,128]{4,3,2,1,0:T(8,128)S(1)} %collective-permute-done.1, ...), kind=kLoop, calls=%fused_computation.24 | loop fusion | flops 3145728 | bytes 12779520 | tf_op jit(solution)/shard_map/sub | solution.py:60
  23.1 0.7 fusion.7
  23.8 1.5 %collective-permute-start.2 = (f32[1,3,34,1,128]{4,3,2,1,0:T(1,128)}, f32[1,3,34,1,128]{4,3,2,1,0:T(1,128)}, u32[]{:S(2)}, u32[]{:S(2)}) collective-permute-start(f32[1,3,34,1,128]{4,3,2,1,0:T(1,128)} %get-tuple-element.17), channel_id=1, source_target_pairs={{1,0},{0,1},{3,2},{2,3},{5,4},{4,5},{7,6},{6,7},{9,8},{8,9},{11,10... | collective-permute-start | bytes 156680 | tf_op jit(solution)/shard_map/ppermute | solution.py:20
  25.4 0.5 collective-permute-start.3
  25.9 0.6 broadcast_multiply_fusion.1
  27.9 0.4 collective-permute-done.2
  28.3 1.5 %collective-permute-done.3 = f32[1,3,34,1,128]{4,3,2,1,0:T(1,128)} collective-permute-done((f32[1,3,34,1,128]{4,3,2,1,0:T(1,128)}, f32[1,3,34,1,128]{4,3,2,1,0:T(1,128)}, u32[]{:S(2)}, u32[]{:S(2)}) %collective-permute-start.3) | collective-permute-done | bytes 52256 | tf_op jit(solution)/shard_map/ppermute | solution.py:17
  29.8 1.6 %fusion.5 = f32[1,3,32,64,128]{4,3,2,1,0:T(8,128)S(1)} fusion(f32[1,3,34,1,128]{4,3,2,1,0:T(1,128)} %collective-permute-done.2, f32[1,3,34,64,128]{4,3,2,1,0:T(8,128)S(1)} %constant_dynamic-update-slice_fusion, f32[1,3,34,1,128]{4,3,2,1,0:T(1,128)} %collective-permute-done.3), kind=kLoop, calls=%fused_computation.26 | loop fusion | flops 2359296 | bytes 6592512 | tf_op jit(solution)/shard_map/sub | solution.py:59
  31.5 1.9 %slice_subtract_fusion.2 = (f32[1,1,32,64,128]{4,3,2,1,0:T(8,128)}, f32[1,1,32,64,128]{4,3,2,1,0:T(8,128)}, f32[1,1,32,64,128]{4,3,2,1,0:T(8,128)}) fusion(f32[1,3,32,64,128]{4,3,2,1,0:T(8,128)S(1)} %copy-done.2, f32[1,3,32,64,128]{4,3,2,1,0:T(8,128)S(1)} %fusion.5, f32[1,3,32,64,128]{4,3,2,1,0:T(8,128)S(1)} %copy-done.3), kind=kLoop, calls=%fused_computation.31 | loop fusion | flops 786432 | bytes 9437184 | tf_op jit(solution)/shard_map/sub | solution.py:62
  33.4 39.3 %collective-permute-done.4 = f32[1,3,32,64,128]{4,3,2,1,0:T(8,128)} collective-permute-done((f32[1,3,32,64,128]{4,3,2,1,0:T(8,128)}, f32[1,3,32,64,128]{4,3,2,1,0:T(8,128)}, u32[]{:S(2)}, u32[]{:S(2)}) %collective-permute-start.4) | collective-permute-done | bytes 3145760 | tf_op jit(solution)/shard_map/ppermute | solution.py:28
  72.7 2.8 %collective-permute-done.5 = f32[1,3,32,64,128]{4,3,2,1,0:T(8,128)} collective-permute-done((f32[1,3,32,64,128]{4,3,2,1,0:T(8,128)}, f32[1,3,32,64,128]{4,3,2,1,0:T(8,128)}, u32[]{:S(2)}, u32[]{:S(2)}) %collective-permute-start.5) | collective-permute-done | bytes 3145760 | tf_op jit(solution)/shard_map/ppermute | solution.py:28
  75.5 8.9 %multiply_reduce_fusion.4 = (f32[]{:T(128)}, f32[32,64,128]{2,1,0:T(8,128)S(1)}, f32[]{:T(128)}, f32[32,64,128]{2,1,0:T(8,128)S(1)}, f32[1,3,32,64,128]{4,3,2,1,0:T(8,128)S(1)}) fusion(f32[1,3,32,64,128]{4,3,2,1,0:T(8,128)} %collective-permute-done.4, f32[1,3,32,64,128]{4,3,2,1,0:T(8,128)S(1)} %copy-done, f32[1,3,32,64,128]{4,3,2,1,0:T(8,128)} %collective-permute-done.5, ...), kind=kLoop, calls=%fused_computation.17 | loop fusion | flops 21495806 | bytes 21469214 | tf_op jit(solution)/shard_map/reduce_sum | solution.py:93
  84.4 4.2 %multiply_reduce_fusion.6 = (f32[]{:T(128)}, f32[]{:T(128)}, f32[1,3,32,64,128]{4,3,2,1,0:T(8,128)S(1)}) fusion(f32[1,3,32,64,128]{4,3,2,1,0:T(8,128)S(1)} %get-tuple-element.15, f32[1,3,32,64,128]{4,3,2,1,0:T(8,128)S(1)} %copy-done, f32[32,64,128]{2,1,0:T(8,128)S(1)} %get-tuple-element.10, f32[32,64,128]{2,1,0:T(8,128)S(1)} %get-tuple-element.4, ...), kind=kLoop, calls=%fused_computation.19 | loop fusion | flops 10223614 | bytes 17825802 | tf_op jit(solution)/shard_map/reduce_sum | solution.py:91
  88.6 2.6 %pad_maximum_fusion.4 = f32[1,4]{1,0:T(1,128)S(1)} fusion(f32[1,1]{1,0:T(1,128)} %bitcast.10, f32[1,1]{1,0:T(1,128)} %bitcast.9, f32[1,1]{1,0:T(1,128)} %bitcast.8, f32[1,1]{1,0:T(1,128)} %bitcast.7), kind=kLoop, calls=%fused_computation.36 | loop fusion | flops 12 | bytes 32 | tf_op jit(solution)/shard_map/stack | solution.py:89
  91.1 1.5 %collective-permute-start.6 = (f32[1,4]{1,0:T(1,128)S(1)}, f32[1,4]{1,0:T(1,128)S(1)}, u32[]{:S(2)}, u32[]{:S(2)}) collective-permute-start(f32[1,4]{1,0:T(1,128)S(1)} %pad_maximum_fusion.4), channel_id=1, source_target_pairs={{0,1},{1,0},{2,3},{3,2},{4,5},{5,4},{6,7},{7,6},{8,9},{9,8},{10,11... | collective-permute-start | bytes 56 | tf_op jit(solution)/shard_map/ppermute | solution.py:40
  92.7 2.0 %collective-permute-done.6 = f32[1,4]{1,0:T(1,128)S(1)} collective-permute-done((f32[1,4]{1,0:T(1,128)S(1)}, f32[1,4]{1,0:T(1,128)S(1)}, u32[]{:S(2)}, u32[]{:S(2)}) %collective-permute-start.6) | collective-permute-done | bytes 48 | tf_op jit(solution)/shard_map/ppermute | solution.py:40
  94.7 2.6 %fusion.11 = f32[1,4]{1,0:T(1,128)S(1)} fusion(f32[1,4]{1,0:T(1,128)S(1)} %collective-permute-done.6, f32[1,1]{1,0:T(1,128)} %bitcast.10, f32[1,1]{1,0:T(1,128)} %bitcast.9, f32[1,1]{1,0:T(1,128)} %bitcast.8, f32[1,1]{1,0:T(1,128)} %bitcast.7), kind=kLoop, calls=%fused_computation.43 | loop fusion | flops 16 | bytes 48 | tf_op jit(solution)/shard_map/add | solution.py:40
  97.3 1.1 collective-permute-done.7
  98.4 2.6 %fusion.12 = f32[1,4]{1,0:T(1,128)S(1)} fusion(f32[1,4]{1,0:T(1,128)S(1)} %collective-permute-done.7, f32[1,4]{1,0:T(1,128)S(1)} %collective-permute-done.6, f32[1,1]{1,0:T(1,128)} %bitcast.10, f32[1,1]{1,0:T(1,128)} %bitcast.9, f32[1,1]{1,0:T(1,128)} %bitcast.8, f32[1,1]{1,0:T(1,128)} %bitcast.7), kind=kLoop, calls=%fused_computation.44 | loop fusion | flops 20 | bytes 64 | tf_op jit(solution)/shard_map/add | solution.py:40
  101.0 1.5 %collective-permute-start.8 = (f32[1,4]{1,0:T(1,128)S(1)}, f32[1,4]{1,0:T(1,128)S(1)}, u32[]{:S(2)}, u32[]{:S(2)}) collective-permute-start(f32[1,4]{1,0:T(1,128)S(1)} %fusion.12), channel_id=1, source_target_pairs={{0,4},{2,6},{4,0},{6,2},{1,5},{3,7},{5,1},{7,3},{8,12},{10,14},{12... | collective-permute-start | bytes 56 | tf_op jit(solution)/shard_map/ppermute | solution.py:40
  102.5 2.0 %collective-permute-done.8 = f32[1,4]{1,0:T(1,128)S(1)} collective-permute-done((f32[1,4]{1,0:T(1,128)S(1)}, f32[1,4]{1,0:T(1,128)S(1)}, u32[]{:S(2)}, u32[]{:S(2)}) %collective-permute-start.8) | collective-permute-done | bytes 48 | tf_op jit(solution)/shard_map/ppermute | solution.py:40
  104.5 0.7 fusion.9
  106.6 0.6 maximum_multiply_fusion.1
  108.6 4.0 %multiply_reduce_fusion.2 = (f32[32,64,128]{2,1,0:T(8,128)S(1)}, f32[32,64,128]{2,1,0:T(8,128)S(1)}, f32[1,3,32,64,128]{4,3,2,1,0:T(8,128)S(1)}) fusion(f32[1,3,32,64,128]{4,3,2,1,0:T(8,128)} %param.7, f32[1,3,32,64,128]{4,3,2,1,0:T(8,128)S(1)} %get-tuple-element.14, f32[]{:T(128)} %bitcast.14, f32[1,3,32,64,128]{4,3,2,1,0:T(8,128)S(1)} %get-tuple-element.15, ...), kind=kLoop, calls=%fused_computation.14 | loop fusion | flops 6553600 | bytes 18874376 | tf_op jit(solution)/shard_map/reduce_sum | solution.py:46
  112.8 1.3 %multiply_reduce_fusion = (f32[32,64,128]{2,1,0:T(8,128)S(1)}, f32[1,3,32,64,128]{4,3,2,1,0:T(8,128)S(1)}) fusion(f32[1,3,32,64,128]{4,3,2,1,0:T(8,128)S(1)} %copy-done, f32[1,3,32,64,128]{4,3,2,1,0:T(8,128)S(1)} %get-tuple-element.13, f32[32,64,128]{2,1,0:T(8,128)S(1)} %divide_add_fusion), kind=kLoop, calls=%fused_computation.11 | loop fusion | flops 3670016 | bytes 11534336 | tf_op jit(solution)/shard_map/reduce_sum | solution.py:46
  114.4 2.5 %broadcast_divide_fusion = f32[1,3,32,64,128]{4,3,2,1,0:T(8,128)} fusion(f32[32,64,128]{2,1,0:T(8,128)S(1)} %sqrt.25, f32[1,3,32,64,128]{4,3,2,1,0:T(8,128)S(1)} %copy-done, f32[1,3,32,64,128]{4,3,2,1,0:T(8,128)S(1)} %get-tuple-element.12), kind=kLoop, calls=%fused_computation.28 | loop fusion | flops 2359296 | bytes 10485760 | tf_op jit(solution)/shard_map/div | solution.py:117
  (18 shorter events, 0.7 us)
Async XLA Ops:
  0.6 72.1 %collective-permute-start.4 = (f32[1,3,32,64,128]{4,3,2,1,0:T(8,128)}, f32[1,3,32,64,128]{4,3,2,1,0:T(8,128)}, u32[]{:S(2)}, u32[]{:S(2)}) collective-permute-start(f32[1,3,32,64,128]{4,3,2,1,0:T(8,128)} %param.6), channel_id=1, source_target_pairs={{8,0},{16,8},{24,16},{9,1},{17,9},{25,17},{10,2},{18,10},{26,18},{... | collective-permute-start | bytes 9437192 | tf_op jit(solution)/shard_map/ppermute | solution.py:28
  3.0 72.5 %collective-permute-start.5 = (f32[1,3,32,64,128]{4,3,2,1,0:T(8,128)}, f32[1,3,32,64,128]{4,3,2,1,0:T(8,128)}, u32[]{:S(2)}, u32[]{:S(2)}) collective-permute-start(f32[1,3,32,64,128]{4,3,2,1,0:T(8,128)} %param.6), channel_id=1, source_target_pairs={{0,8},{8,16},{16,24},{1,9},{9,17},{17,25},{2,10},{10,18},{18,26},{... | collective-permute-start | bytes 9437192 | tf_op jit(solution)/shard_map/ppermute | solution.py:28
  9.1 4.1 %collective-permute-start.1 = (f32[1,3,1,64,128]{4,3,2,1,0:T(8,128)S(1)}, f32[1,3,1,64,128]{4,3,2,1,0:T(8,128)S(1)}, u32[]{:S(2)}, u32[]{:S(2)}) collective-permute-start(f32[1,3,1,64,128]{4,3,2,1,0:T(8,128)S(1)} %get-tuple-element.25), channel_id=1, source_target_pairs={{0,2},{2,4},{4,6},{6,0},{1,3},{3,5},{5,7},{7,1},{8,10},{10,12},{12... | collective-permute-start | bytes 294920 | tf_op jit(solution)/shard_map/ppermute | solution.py:17
  9.2 4.1 %collective-permute-start = (f32[1,3,1,64,128]{4,3,2,1,0:T(8,128)S(1)}, f32[1,3,1,64,128]{4,3,2,1,0:T(8,128)S(1)}, u32[]{:S(2)}, u32[]{:S(2)}) collective-permute-start(f32[1,3,1,64,128]{4,3,2,1,0:T(8,128)S(1)} %get-tuple-element.24), channel_id=1, source_target_pairs={{2,0},{4,2},{6,4},{0,6},{3,1},{5,3},{7,5},{1,7},{10,8},{12,10},{14... | collective-permute-start | bytes 294920 | tf_op jit(solution)/shard_map/ppermute | solution.py:20
  13.2 12.6 %copy-start.4 = (f32[3]{0:T(128)S(1)}, f32[3]{0:T(128)}, u32[]{:S(2)}) copy-start(f32[3]{0:T(128)} %constant.41.clone) | copy-start | bytes 40
  23.8 4.4 %collective-permute-start.2 = (f32[1,3,34,1,128]{4,3,2,1,0:T(1,128)}, f32[1,3,34,1,128]{4,3,2,1,0:T(1,128)}, u32[]{:S(2)}, u32[]{:S(2)}) collective-permute-start(f32[1,3,34,1,128]{4,3,2,1,0:T(1,128)} %get-tuple-element.17), channel_id=1, source_target_pairs={{1,0},{0,1},{3,2},{2,3},{5,4},{4,5},{7,6},{6,7},{9,8},{8,9},{11,10... | collective-permute-start | bytes 156680 | tf_op jit(solution)/shard_map/ppermute | solution.py:20
  25.4 4.5 %collective-permute-start.3 = (f32[1,3,34,1,128]{4,3,2,1,0:T(1,128)}, f32[1,3,34,1,128]{4,3,2,1,0:T(1,128)}, u32[]{:S(2)}, u32[]{:S(2)}) collective-permute-start(f32[1,3,34,1,128]{4,3,2,1,0:T(1,128)} %get-tuple-element.16), channel_id=1, source_target_pairs={{0,1},{1,0},{2,3},{3,2},{4,5},{5,4},{6,7},{7,6},{8,9},{9,8},{10,11... | collective-permute-start | bytes 156680 | tf_op jit(solution)/shard_map/ppermute | solution.py:17
  27.8 3.6 %copy-start.2 = (f32[1,3,32,64,128]{4,3,2,1,0:T(8,128)S(1)}, f32[1,3,32,64,128]{4,3,2,1,0:T(8,128)}, u32[]{:S(2)}) copy-start(f32[1,3,32,64,128]{4,3,2,1,0:T(8,128)} %get-tuple-element.21) | copy-start | bytes 9437188
  27.8 3.6 %copy-start.3 = (f32[1,3,32,64,128]{4,3,2,1,0:T(8,128)S(1)}, f32[1,3,32,64,128]{4,3,2,1,0:T(8,128)}, u32[]{:S(2)}) copy-start(f32[1,3,32,64,128]{4,3,2,1,0:T(8,128)} %get-tuple-element.23) | copy-start | bytes 9437188
  31.5 44.0 %copy-start = (f32[1,3,32,64,128]{4,3,2,1,0:T(8,128)S(1)}, f32[1,3,32,64,128]{4,3,2,1,0:T(8,128)}, u32[]{:S(2)}) copy-start(f32[1,3,32,64,128]{4,3,2,1,0:T(8,128)} %param.6) | copy-start | bytes 9437188
  91.1 3.5 %collective-permute-start.6 = (f32[1,4]{1,0:T(1,128)S(1)}, f32[1,4]{1,0:T(1,128)S(1)}, u32[]{:S(2)}, u32[]{:S(2)}) collective-permute-start(f32[1,4]{1,0:T(1,128)S(1)} %pad_maximum_fusion.4), channel_id=1, source_target_pairs={{0,1},{1,0},{2,3},{3,2},{4,5},{5,4},{6,7},{7,6},{8,9},{9,8},{10,11... | collective-permute-start | bytes 56 | tf_op jit(solution)/shard_map/ppermute | solution.py:40
  97.3 1.1 collective-permute-start.7
  101.0 3.5 %collective-permute-start.8 = (f32[1,4]{1,0:T(1,128)S(1)}, f32[1,4]{1,0:T(1,128)S(1)}, u32[]{:S(2)}, u32[]{:S(2)}) collective-permute-start(f32[1,4]{1,0:T(1,128)S(1)} %fusion.12), channel_id=1, source_target_pairs={{0,4},{2,6},{4,0},{6,2},{1,5},{3,7},{5,1},{7,3},{8,12},{10,14},{12... | collective-permute-start | bytes 56 | tf_op jit(solution)/shard_map/ppermute | solution.py:40
  114.2 2.8 %copy-start.1 = (f32[1,3,32,64,128]{4,3,2,1,0:T(8,128)}, f32[1,3,32,64,128]{4,3,2,1,0:T(8,128)S(1)}, u32[]{:S(2)}) copy-start(f32[1,3,32,64,128]{4,3,2,1,0:T(8,128)S(1)} %get-tuple-element.12) | copy-start | bytes 9437188

commit v2 on v1

--- a/solution.py
+++ b/solution.py
@@ -1,11 +1,16 @@
+import functools
+
 import jax
 import jax.numpy as jnp
 from jax import lax
+from jax.experimental import pallas as pl
+from jax.experimental.pallas import tpu as pltpu
 from jax.sharding import PartitionSpec as P
 
 TIME_STEP = 0.1
 SPRING = 2.0
 EPSILON = 1e-06
+ROWS = 4
 
 
 def extended(block, sides, width):
@@ -66,55 +71,128 @@
     return coupling[0] * neighbours + coupling[1] * twist + coupling[2] * lift
 
 
+def fold(x):
+    return jnp.sum(x.reshape(-1, 8, x.shape[-1]), axis=0)
+
+
+def tangent_kernel(up_ref, s_ref, nx_ref, pv_ref, pf_ref, tp_ref, sums_ref, acc_ref):
+    step = pl.program_id(1)
+
+    @pl.when(step == 0)
+    def _():
+        acc_ref[...] = jnp.zeros_like(acc_ref)
+
+    up = up_ref[pl.program_id(0)]
+    ahead = jnp.where(up >= 0, 1.0, 0.0).astype(jnp.float32)
+    behind = jnp.where(up <= 0, 1.0, 0.0).astype(jnp.float32)
+    s = [s_ref[0, c] for c in range(3)]
+    fwd = [nx_ref[0, c] - s[c] for c in range(3)]
+    bwd = [s[c] - pv_ref[0, c] for c in range(3)]
+    raw = [ahead * fwd[c] + behind * bwd[c] for c in range(3)]
+    d = raw[0] * s[0] + raw[1] * s[1] + raw[2] * s[2]
+    tp = [raw[c] - d * s[c] for c in range(3)]
+    for c in range(3):
+        tp_ref[0, c] = tp[c]
+    pf = [pf_ref[0, c] for c in range(3)]
+    acc_ref[0] += fold(tp[0] * tp[0] + tp[1] * tp[1] + tp[2] * tp[2])
+    acc_ref[1] += fold(pf[0] * tp[0] + pf[1] * tp[1] + pf[2] * tp[2])
+    acc_ref[2] += fold(fwd[0] * fwd[0] + fwd[1] * fwd[1] + fwd[2] * fwd[2])
+    acc_ref[3] += fold(bwd[0] * bwd[0] + bwd[1] * bwd[1] + bwd[2] * bwd[2])
+
+    @pl.when(step == pl.num_programs(1) - 1)
+    def _():
+        lane = lax.broadcasted_iota(jnp.int32, (8, 128), 1)
+        row = lax.broadcasted_iota(jnp.int32, (8, 128), 0)
+        out = jnp.zeros((8, 128), jnp.float32)
+        for k in range(4):
+            total = jnp.sum(acc_ref[k], keepdims=True)
+            out = jnp.where((row == 0) & (lane == k), total, out)
+        sums_ref[0] = out
+
+
+def update_kernel(root_cells, flag_ref, sums_ref, s_ref, v_ref, pf_ref, tp_ref, ns_ref, nv_ref, sp_ref):
+    image = pl.program_id(0)
+    tot = sums_ref[0]
+    lane = lax.broadcasted_iota(jnp.int32, (8, 128), 1)
+    row = lax.broadcasted_iota(jnp.int32, (8, 128), 0)
+
+    def pick(k):
+        return jnp.sum(jnp.where((row == 0) & (lane == k), tot, 0.0), keepdims=True)
+
+    norm_t, along_t, next_sq, prev_sq = (pick(k) for k in range(4))
+    scale = 1.0 / jnp.sqrt(norm_t + EPSILON)
+    along = along_t * scale
+    dist_next = jnp.sqrt(next_sq + EPSILON)
+    dist_prev = jnp.sqrt(prev_sq + EPSILON)
+    climbing = jnp.full((1, 1), flag_ref[0, image]) > 0
+    ending = jnp.full((1, 1), flag_ref[1, image]) > 0
+    weight = jnp.where(climbing, 2.0 * along, along - SPRING * (dist_next - dist_prev))
+    coef = jnp.where(ending, 0.0, weight * scale)
+    keep = jnp.where(ending, 0.0, 1.0)
+
+    @pl.when(pl.program_id(1) == 0)
+    def _():
+        pair = lax.broadcasted_iota(jnp.int32, (1, 2), 1)
+        sp_ref[0] = jnp.where(pair == 0, dist_next, dist_prev) / root_cells
+
+    f = [keep * pf_ref[0, c] - coef * tp_ref[0, c] for c in range(3)]
+    v = [v_ref[0, c] for c in range(3)]
+    vf = v[0] * f[0] + v[1] * f[1] + v[2] * f[2]
+    ff = f[0] * f[0] + f[1] * f[1] + f[2] * f[2]
+    gain = jnp.maximum(vf, 0.0) / jnp.maximum(ff, 1.0)
+    nv = [gain * f[c] + TIME_STEP * f[c] for c in range(3)]
+    moved = [s_ref[0, c] + TIME_STEP * nv[c] for c in range(3)]
+    length = jnp.sqrt(moved[0] * moved[0] + moved[1] * moved[1] + moved[2] * moved[2])
+    for c in range(3):
+        nv_ref[0, c] = nv[c]
+        ns_ref[0, c] = moved[c] / length
+
+
 def per_device(spins, velocity, upwind, climber, coupling):
-    count = spins.shape[0]
+    count, _, nx, ny, nz = spins.shape
     total = count * lax.axis_size("img")
-    cells = (
-        spins.shape[2] * spins.shape[3] * spins.shape[4] * lax.axis_size("gx") * lax.axis_size("gy")
-    )
-    root_cells = jnp.sqrt(jnp.asarray(cells, jnp.float32))
+    cells = nx * ny * nz * lax.axis_size("gx") * lax.axis_size("gy")
+    root_cells = float(cells) ** 0.5
     indices = lax.axis_index("img") * count + jnp.arange(count, dtype=jnp.int32)
-    axes_all = (1, 2, 3, 4)
     ahead = from_behind(spins[:1], "img", -1)
     behind = from_behind(spins[-1:], "img", 1)
     field = lattice_field(spins, coupling)
     perp_field = field - cell_dot(field, spins) * spins
     after = jnp.concatenate([spins[1:], ahead], 0)
     before = jnp.concatenate([behind, spins[:-1]], 0)
-    forward = after - spins
-    backward = spins - before
-    direction = upwind.reshape(count, 1, 1, 1, 1)
-    raw = jnp.where(direction > 0, forward, jnp.where(direction < 0, backward, forward + backward))
-    tangent_perp = raw - cell_dot(raw, spins) * spins
-    parts = jnp.stack(
-        [
-            jnp.sum(tangent_perp * tangent_perp, axis=axes_all),
-            jnp.sum(perp_field * tangent_perp, axis=axes_all),
-            jnp.sum(forward * forward, axis=axes_all),
-            jnp.sum(backward * backward, axis=axes_all),
-        ],
-        1,
-    )
-    norm_t, along_t, next_sq, prev_sq = jnp.moveaxis(group_sum(parts, ("gy", "gx")), 1, 0)
-    scale = 1.0 / jnp.sqrt(norm_t + EPSILON)
-    along = along_t * scale
-    dist_next = jnp.sqrt(next_sq + EPSILON)
-    dist_prev = jnp.sqrt(prev_sq + EPSILON)
-    spacing = jnp.stack([dist_next, dist_prev], 1) / root_cells
+
+    rows = ROWS if nx % ROWS == 0 else nx
+    grid = (count, nx // rows)
+    block = pl.BlockSpec((1, 3, rows, ny, nz), lambda i, j: (i, 0, j, 0, 0))
+    small = pl.BlockSpec((1, 8, 128), lambda i, j: (i, 0, 0))
+    smem = pl.BlockSpec(memory_space=pltpu.SMEM)
+    big = jax.ShapeDtypeStruct(spins.shape, jnp.float32)
+    nbytes = spins.size * 4
+    tangent_perp, sums = pl.pallas_call(
+        tangent_kernel,
+        grid=grid,
+        in_specs=[smem, block, block, block, block],
+        out_specs=[block, small],
+        out_shape=[big, jax.ShapeDtypeStruct((count, 8, 128), jnp.float32)],
+        scratch_shapes=[pltpu.VMEM((4, 8, nz), jnp.float32)],
+        compiler_params=pltpu.CompilerParams(dimension_semantics=("arbitrary", "arbitrary")),
+        cost_estimate=pl.CostEstimate(flops=40 * spins.size, bytes_accessed=5 * nbytes, transcendentals=0),
+    )(upwind, spins, after, before, perp_field)
+
+    sums = group_sum(sums, ("gy", "gx"))
     climbing = indices == climber[0]
     ending = (indices == 0) | (indices == total - 1)
-    weight = jnp.where(climbing, 2.0 * along, along - SPRING * (dist_next - dist_prev))
-    weight = jnp.where(ending, 0.0, weight * scale)
-    keep = jnp.where(ending, 0.0, 1.0).reshape(count, 1, 1, 1, 1)
-    force = keep * perp_field - weight.reshape(count, 1, 1, 1, 1) * tangent_perp
-    projected = (
-        jnp.maximum(cell_dot(velocity, force), 0.0)
-        / jnp.maximum(cell_dot(force, force), 1.0)
-        * force
-    )
-    speed_new = projected + TIME_STEP * force
-    moved = spins + TIME_STEP * speed_new
-    return (moved / jnp.sqrt(cell_dot(moved, moved)), speed_new, spacing)
+    flags = jnp.stack([climbing, ending], 0).astype(jnp.int32)
+    new_spins, new_velocity, spacing = pl.pallas_call(
+        functools.partial(update_kernel, root_cells),
+        grid=grid,
+        in_specs=[smem, small, block, block, block, block],
+        out_specs=[block, block, pl.BlockSpec((1, 1, 2), lambda i, j: (i, 0, 0))],
+        out_shape=[big, big, jax.ShapeDtypeStruct((count, 1, 2), jnp.float32)],
+        compiler_params=pltpu.CompilerParams(dimension_semantics=("arbitrary", "arbitrary")),
+        cost_estimate=pl.CostEstimate(flops=45 * spins.size, bytes_accessed=6 * nbytes, transcendentals=spins.size // 3),
+    )(flags, sums, spins, velocity, perp_field, tangent_perp)
+    return new_spins, new_velocity, spacing.reshape(count, 2)
 
 
 def solution(mesh):

time: 118 us -> 106 us (0.90)
  other arithmetic: 43.5 us -> 18.5 us
  Pallas kernels: 0 us -> 19 us
  waiting for transfers between devices: 50.2 us -> 46.9 us
  between operations: 4.88 us -> 2.04 us
    pallas_call x0 -> x2, Pallas kernels: none -> 19 us  [the longest x1 10.2 us: per_device(): pl.pallas_call(functools.partial(update_kernel, root_cells), grid=grid, i...]
    reduce_sum x2 -> x0, other arithmetic: 13 us -> none  [the longest x1 8.87 us: per_device(): jnp.sum(forward * forward, axis=axes_all)]
    add x3, other arithmetic: 5.17 us -> 1.29 us  [group_sum(): value = value + lax.ppermute(value, axis, pairs)]
    div x2 -> x0, other arithmetic: 3.1 us -> none  [the longest x1 2.52 us: per_device(): return (moved / jnp.sqrt(cell_dot(moved, moved)), speed_new, spacing)]
    ppermute x2, waiting for transfers between devices: 42.2 us -> 39.2 us  [from_behind(): return lax.ppermute(value, axis, pairs)]
    another operation x1 -> x0, other arithmetic: 2.58 us -> none  [per_device(): jnp.stack([jnp.sum(tangent_perp * tangent_perp, axis=axes_all), jnp.sum(p...]
    sub x0 -> x1, other arithmetic: none -> 2.48 us  [per_device(): perp_field = field - cell_dot(field, spins) * spins]
    sub x1, other arithmetic: 9.84 us -> 7.96 us  [lattice_field(): diff_z = plus_z - minus_z]
  transfers between devices with their start and end apart: 9 -> 9, of which waited for: 8 -> 8; matrix products, arithmetic and copies ran while one was open for 15% -> 19% of each run, Pallas kernels for 0% -> 0%
where the time goes in v2:
time: 106 us; the launch traced here: 104 us
  waiting for transfers between devices  46.9 us (44%)
  Pallas kernels  19 us (18%)
  other arithmetic  18.5 us (17%)
  starting transfers between devices  14.4 us (14%)
  local copies, waits for them, and re-layouts  3.58 us (3%)
  between operations  2.04 us (2%)
    ppermute x2, waiting for transfers between devices, from_behind(): return lax.ppermute(value, axis, pairs)  39.2 us
    pallas_call x1, Pallas kernels, per_device(): pl.pallas_call(functools.partial(update_kernel, root_cells), grid=grid, i...  10.2 us
    pallas_call x1, Pallas kernels, per_device(): pl.pallas_call(tangent_kernel, grid=grid, in_specs=[smem, block, block, b...  8.84 us
    sub x1, other arithmetic, lattice_field(): diff_z = plus_z - minus_z  7.96 us
    ppermute x2, starting transfers between devices, from_behind(): return lax.ppermute(value, axis, pairs)  7.54 us
    ppermute x3, waiting for transfers between devices, group_sum(): value = value + lax.ppermute(value, axis, pairs)  4.35 us
    reduce_sum x1, other arithmetic, cell_dot(): return jnp.sum(left * right, axis=1, keepdims=True)  4.08 us
    ppermute x2, starting transfers between devices, extended(): lax.ppermute(lax.slice_in_dim(block, 0, width, axis=dim), axis, backward)  3.32 us
  transfers between devices with their start and end apart: 9, of which 8 were waited for; matrix products, arithmetic and copies ran while one was open for 19% of the time, Pallas kernels for 0%

profile of v2, /device:TPU:16, one launch (start us, length us, event | category | flops | bytes accessed | tf_op | source)
XLA Modules:
  0.0 104.4 jit_solution(14735133724785088363)
XLA Ops:
  0.6 2.4 %collective-permute-start = (f32[1,3,32,64,128]{4,3,2,1,0:T(8,128)}, f32[1,3,32,64,128]{4,3,2,1,0:T(8,128)}, u32[]{:S(2)}, u32[]{:S(2)}) collective-permute-start(f32[1,3,32,64,128]{4,3,2,1,0:T(8,128)} %s_ref.3), channel_id=1, source_target_pairs={{8,0},{16,8},{24,16},{9,1},{17,9},{25,17},{10,2},{18,10},{26,18},{... | collective-permute-start | bytes 9437192 | tf_op jit(solution)/shard_map/ppermute | solution.py:33
  3.0 5.2 %collective-permute-start.1 = (f32[1,3,32,64,128]{4,3,2,1,0:T(8,128)}, f32[1,3,32,64,128]{4,3,2,1,0:T(8,128)}, u32[]{:S(2)}, u32[]{:S(2)}) collective-permute-start(f32[1,3,32,64,128]{4,3,2,1,0:T(8,128)} %s_ref.3), channel_id=1, source_target_pairs={{0,8},{8,16},{16,24},{1,9},{9,17},{17,25},{2,10},{10,18},{18,26},{... | collective-permute-start | bytes 9437192 | tf_op jit(solution)/shard_map/ppermute | solution.py:33
  8.2 1.0 fusion.7
  9.1 0.1 collective-permute-start.3
  9.2 1.7 %collective-permute-start.2 = (f32[1,3,1,64,128]{4,3,2,1,0:T(8,128)S(1)}, f32[1,3,1,64,128]{4,3,2,1,0:T(8,128)S(1)}, u32[]{:S(2)}, u32[]{:S(2)}) collective-permute-start(f32[1,3,1,64,128]{4,3,2,1,0:T(8,128)S(1)} %get-tuple-element.23), channel_id=1, source_target_pairs={{2,0},{4,2},{6,4},{0,6},{3,1},{5,3},{7,5},{1,7},{10,8},{12,10},{14... | collective-permute-start | bytes 294920 | tf_op jit(solution)/shard_map/ppermute | solution.py:25
  10.9 1.4 %fusion.8 = (f32[1]{0:T(128)}, f32[1]{0:T(128)}, f32[1]{0:T(128)}) fusion(f32[3]{0:T(128)} %param.10), kind=kLoop, calls=%fused_computation.24 | loop fusion | bytes 24 | tf_op jit(solution)/shard_map/slice | solution.py:71
  12.3 0.9 collective-permute-done.3
  13.3 0.0 collective-permute-done.2
  13.3 8.0 %fusion.2 = (f32[1,3,32,64,128]{4,3,2,1,0:T(8,128)S(1)}, f32[1,3,34,64,128]{4,3,2,1,0:T(8,128)S(1)}, f32[1,3,32,64,128]{4,3,2,1,0:T(8,128)S(1)}) fusion(f32[1,3,32,64,128]{4,3,2,1,0:T(8,128)} %s_ref.3, f32[1,3,34,64,128]{4,3,2,1,0:T(8,128)S(1)} %constant_dynamic-update-slice_fusion.2, f32[1,3,1,64,128]{4,3,2,1,0:T(8,128)S(1)} %collective-permute-done.3, ...), kind=kLoop, calls=%fused_computation.11 | loop fusion | flops 3145728 | bytes 12779520 | tf_op jit(solution)/shard_map/sub | solution.py:65
  21.3 0.1 fusion.6
  21.4 1.6 %collective-permute-start.4 = (f32[1,3,34,1,128]{4,3,2,1,0:T(1,128)S(1)}, f32[1,3,34,1,128]{4,3,2,1,0:T(1,128)S(1)}, u32[]{:S(2)}, u32[]{:S(2)}) collective-permute-start(f32[1,3,34,1,128]{4,3,2,1,0:T(1,128)S(1)} %get-tuple-element.16), channel_id=1, source_target_pairs={{1,0},{0,1},{3,2},{2,3},{5,4},{4,5},{7,6},{6,7},{9,8},{8,9},{11,10... | collective-permute-start | bytes 156680 | tf_op jit(solution)/shard_map/ppermute | solution.py:25
  23.0 0.5 collective-permute-start.5
  23.5 0.6 broadcast_multiply_fusion
  24.8 0.8 collective-permute-done.4
  25.6 1.5 %collective-permute-done.5 = f32[1,3,34,1,128]{4,3,2,1,0:T(1,128)S(1)} collective-permute-done((f32[1,3,34,1,128]{4,3,2,1,0:T(1,128)S(1)}, f32[1,3,34,1,128]{4,3,2,1,0:T(1,128)S(1)}, u32[]{:S(2)}, u32[]{:S(2)}) %collective-permute-start.5) | collective-permute-done | bytes 52256 | tf_op jit(solution)/shard_map/ppermute | solution.py:22
  27.1 0.8 fusion.4
  27.9 0.7 slice_subtract_fusion.2
  28.6 1.2 %copy-done = f32[1,3,32,64,128]{4,3,2,1,0:T(8,128)S(1)} copy-done((f32[1,3,32,64,128]{4,3,2,1,0:T(8,128)S(1)}, f32[1,3,32,64,128]{4,3,2,1,0:T(8,128)}, u32[]{:S(2)}) %copy-start) | copy-done | bytes 3145752
  29.8 4.1 %multiply_reduce_fusion = (f32[32,64,128]{2,1,0:T(8,128)S(1)}, f32[1,3,32,64,128]{4,3,2,1,0:T(8,128)S(1)}) fusion(f32[1,3,32,64,128]{4,3,2,1,0:T(8,128)S(1)} %copy-done, f32[3]{0:T(128)S(1)} %broadcast_multiply_fusion, f32[1,1,32,64,128]{4,3,2,1,0:T(8,128)S(1)} %get-tuple-element.18, f32[1,1,32,64,128]{4,3,2,1,0:T(8,128)S(1)} %get-tuple-element.19, ...), kind=kLoop, calls=%fused_computation.10 | loop fusion | flops 13107200 | bytes 14129172 | tf_op jit(solution)/shard_map/reduce_sum | solution.py:51
  33.9 2.5 %multiply_subtract_fusion.pf_ref = f32[1,3,32,64,128]{4,3,2,1,0:T(8,128)} fusion(f32[1,3,32,64,128]{4,3,2,1,0:T(8,128)S(1)} %get-tuple-element.14, f32[1,3,32,64,128]{4,3,2,1,0:T(8,128)S(1)} %copy-done, f32[32,64,128]{2,1,0:T(8,128)S(1)} %get-tuple-element.13), kind=kLoop, calls=%fused_computation.9 | loop fusion | flops 1572864 | bytes 10485760 | tf_op jit(solution)/shard_map/sub | solution.py:160
  36.4 36.3 %collective-permute-done.nx_ref = f32[1,3,32,64,128]{4,3,2,1,0:T(8,128)} collective-permute-done((f32[1,3,32,64,128]{4,3,2,1,0:T(8,128)}, f32[1,3,32,64,128]{4,3,2,1,0:T(8,128)}, u32[]{:S(2)}, u32[]{:S(2)}) %collective-permute-start) | collective-permute-done | bytes 3145760 | tf_op jit(solution)/shard_map/ppermute | solution.py:33
  72.7 2.9 %collective-permute-done.1.pv_ref = f32[1,3,32,64,128]{4,3,2,1,0:T(8,128)} collective-permute-done((f32[1,3,32,64,128]{4,3,2,1,0:T(8,128)}, f32[1,3,32,64,128]{4,3,2,1,0:T(8,128)}, u32[]{:S(2)}, u32[]{:S(2)}) %collective-permute-start.1) | collective-permute-done | bytes 3145760 | tf_op jit(solution)/shard_map/ppermute | solution.py:33
  75.6 8.8 %shard_map.85 = (f32[1,3,32,64,128]{4,3,2,1,0:T(8,128)}, f32[1,8,128]{2,1,0:T(8,128)}) custom-call(s32[1]{0:T(128)S(6)} %copy.11.up_ref, f32[1,3,32,64,128]{4,3,2,1,0:T(8,128)} %s_ref.3, f32[1,3,32,64,128]{4,3,2,1,0:T(8,128)} %collective-permute-done.nx_ref, f32[1,3,32,64,128]{4,3,2,1,0:T(8,128)} %collective-permute-done.1.pv_ref, ...), custom_call_target="tpu_custom_call" | custom-call | flops 31457280 | bytes 15728640 | tf_op jit(solution)/shard_map/pallas_call | solution.py:171
  84.4 1.5 %collective-permute-start.6 = (f32[1,8,128]{2,1,0:T(8,128)}, f32[1,8,128]{2,1,0:T(8,128)S(1)}, u32[]{:S(2)}, u32[]{:S(2)}) collective-permute-start(f32[1,8,128]{2,1,0:T(8,128)} %get-tuple-element.8), channel_id=1, source_target_pairs={{0,1},{1,0},{2,3},{3,2},{4,5},{5,4},{6,7},{7,6},{8,9},{9,8},{10,11... | collective-permute-start | bytes 12296 | tf_op jit(solution)/shard_map/ppermute | solution.py:45
  85.9 2.3 %collective-permute-done.6 = f32[1,8,128]{2,1,0:T(8,128)S(1)} collective-permute-done((f32[1,8,128]{2,1,0:T(8,128)}, f32[1,8,128]{2,1,0:T(8,128)S(1)}, u32[]{:S(2)}, u32[]{:S(2)}) %collective-permute-start.6) | collective-permute-done | bytes 4128 | tf_op jit(solution)/shard_map/ppermute | solution.py:45
  88.2 0.7 add.49
  89.6 0.5 collective-permute-done.7
  90.1 1.5 %collective-permute-start.8 = (f32[1,8,128]{2,1,0:T(8,128)S(1)}, f32[1,8,128]{2,1,0:T(8,128)S(1)}, u32[]{:S(2)}, u32[]{:S(2)}) collective-permute-start(f32[1,8,128]{2,1,0:T(8,128)S(1)} %add.50), channel_id=1, source_target_pairs={{0,4},{2,6},{4,0},{6,2},{1,5},{3,7},{5,1},{7,3},{8,12},{10,14},{12... | collective-permute-start | bytes 12296 | tf_op jit(solution)/shard_map/ppermute | solution.py:45
  91.6 0.6 add_convert_fusion.flag_ref
  92.1 1.5 %collective-permute-done.8 = f32[1,8,128]{2,1,0:T(8,128)S(1)} collective-permute-done((f32[1,8,128]{2,1,0:T(8,128)S(1)}, f32[1,8,128]{2,1,0:T(8,128)S(1)}, u32[]{:S(2)}, u32[]{:S(2)}) %collective-permute-start.8) | collective-permute-done | bytes 4128 | tf_op jit(solution)/shard_map/ppermute | solution.py:45
  93.7 0.6 add.51.sums_ref
  94.3 10.2 %shard_map.86 = (f32[1,3,32,64,128]{4,3,2,1,0:T(8,128)}, f32[1,3,32,64,128]{4,3,2,1,0:T(8,128)}, f32[1,1,2]{2,1,0:T(1,128)}) custom-call(s32[2,1]{1,0:T(2,128)} %add_convert_fusion.flag_ref, f32[1,8,128]{2,1,0:T(8,128)} %add.51.sums_ref, f32[1,3,32,64,128]{4,3,2,1,0:T(8,128)} %s_ref.3, f32[1,3,32,64,128]{4,3,2,1,0:T(8,128)} %v_ref.1, ...), custom_call_target="tpu_custom_call" | custom-call | flops 35389440 | bytes 18874368 | tf_op jit(solution)/shard_map/pallas_call | solution.py:186
  (7 shorter events, 0.0 us)
Async XLA Ops:
  0.6 72.1 %collective-permute-start = (f32[1,3,32,64,128]{4,3,2,1,0:T(8,128)}, f32[1,3,32,64,128]{4,3,2,1,0:T(8,128)}, u32[]{:S(2)}, u32[]{:S(2)}) collective-permute-start(f32[1,3,32,64,128]{4,3,2,1,0:T(8,128)} %s_ref.3), channel_id=1, source_target_pairs={{8,0},{16,8},{24,16},{9,1},{17,9},{25,17},{10,2},{18,10},{26,18},{... | collective-permute-start | bytes 9437192 | tf_op jit(solution)/shard_map/ppermute | solution.py:33
  3.0 72.6 %collective-permute-start.1 = (f32[1,3,32,64,128]{4,3,2,1,0:T(8,128)}, f32[1,3,32,64,128]{4,3,2,1,0:T(8,128)}, u32[]{:S(2)}, u32[]{:S(2)}) collective-permute-start(f32[1,3,32,64,128]{4,3,2,1,0:T(8,128)} %s_ref.3), channel_id=1, source_target_pairs={{0,8},{8,16},{16,24},{1,9},{9,17},{17,25},{2,10},{10,18},{18,26},{... | collective-permute-start | bytes 9437192 | tf_op jit(solution)/shard_map/ppermute | solution.py:33
  9.1 4.1 %collective-permute-start.3 = (f32[1,3,1,64,128]{4,3,2,1,0:T(8,128)S(1)}, f32[1,3,1,64,128]{4,3,2,1,0:T(8,128)S(1)}, u32[]{:S(2)}, u32[]{:S(2)}) collective-permute-start(f32[1,3,1,64,128]{4,3,2,1,0:T(8,128)S(1)} %get-tuple-element.24), channel_id=1, source_target_pairs={{0,2},{2,4},{4,6},{6,0},{1,3},{3,5},{5,7},{7,1},{8,10},{10,12},{12... | collective-permute-start | bytes 294920 | tf_op jit(solution)/shard_map/ppermute | solution.py:22
  9.2 4.1 %collective-permute-start.2 = (f32[1,3,1,64,128]{4,3,2,1,0:T(8,128)S(1)}, f32[1,3,1,64,128]{4,3,2,1,0:T(8,128)S(1)}, u32[]{:S(2)}, u32[]{:S(2)}) collective-permute-start(f32[1,3,1,64,128]{4,3,2,1,0:T(8,128)S(1)} %get-tuple-element.23), channel_id=1, source_target_pairs={{2,0},{4,2},{6,4},{0,6},{3,1},{5,3},{7,5},{1,7},{10,8},{12,10},{14... | collective-permute-start | bytes 294920 | tf_op jit(solution)/shard_map/ppermute | solution.py:25
  13.3 10.2 %copy-start.1 = (f32[3]{0:T(128)S(1)}, f32[3]{0:T(128)}, u32[]{:S(2)}) copy-start(f32[3]{0:T(128)} %constant.15.clone) | copy-start | bytes 40
  21.4 4.2 %collective-permute-start.4 = (f32[1,3,34,1,128]{4,3,2,1,0:T(1,128)S(1)}, f32[1,3,34,1,128]{4,3,2,1,0:T(1,128)S(1)}, u32[]{:S(2)}, u32[]{:S(2)}) collective-permute-start(f32[1,3,34,1,128]{4,3,2,1,0:T(1,128)S(1)} %get-tuple-element.16), channel_id=1, source_target_pairs={{1,0},{0,1},{3,2},{2,3},{5,4},{4,5},{7,6},{6,7},{9,8},{8,9},{11,10... | collective-permute-start | bytes 156680 | tf_op jit(solution)/shard_map/ppermute | solution.py:25
  23.0 4.2 %collective-permute-start.5 = (f32[1,3,34,1,128]{4,3,2,1,0:T(1,128)S(1)}, f32[1,3,34,1,128]{4,3,2,1,0:T(1,128)S(1)}, u32[]{:S(2)}, u32[]{:S(2)}) collective-permute-start(f32[1,3,34,1,128]{4,3,2,1,0:T(1,128)S(1)} %get-tuple-element.15), channel_id=1, source_target_pairs={{0,1},{1,0},{2,3},{3,2},{4,5},{5,4},{6,7},{7,6},{8,9},{9,8},{10,11... | collective-permute-start | bytes 156680 | tf_op jit(solution)/shard_map/ppermute | solution.py:22
  27.9 1.9 %copy-start = (f32[1,3,32,64,128]{4,3,2,1,0:T(8,128)S(1)}, f32[1,3,32,64,128]{4,3,2,1,0:T(8,128)}, u32[]{:S(2)}) copy-start(f32[1,3,32,64,128]{4,3,2,1,0:T(8,128)} %s_ref.3) | copy-start | bytes 9437188
  84.4 3.8 %collective-permute-start.6 = (f32[1,8,128]{2,1,0:T(8,128)}, f32[1,8,128]{2,1,0:T(8,128)S(1)}, u32[]{:S(2)}, u32[]{:S(2)}) collective-permute-start(f32[1,8,128]{2,1,0:T(8,128)} %get-tuple-element.8), channel_id=1, source_target_pairs={{0,1},{1,0},{2,3},{3,2},{4,5},{5,4},{6,7},{7,6},{8,9},{9,8},{10,11... | collective-permute-start | bytes 12296 | tf_op jit(solution)/shard_map/ppermute | solution.py:45
  88.9 1.2 %collective-permute-start.7 = (f32[1,8,128]{2,1,0:T(8,128)S(1)}, f32[1,8,128]{2,1,0:T(8,128)S(1)}, u32[]{:S(2)}, u32[]{:S(2)}) collective-permute-start(f32[1,8,128]{2,1,0:T(8,128)S(1)} %add.49), channel_id=1, source_target_pairs={{0,2},{2,0},{4,6},{6,4},{1,3},{3,1},{5,7},{7,5},{8,10},{10,8},{12,... | collective-permute-start | bytes 12296 | tf_op jit(solution)/shard_map/ppermute | solution.py:45
  90.1 3.6 %collective-permute-start.8 = (f32[1,8,128]{2,1,0:T(8,128)S(1)}, f32[1,8,128]{2,1,0:T(8,128)S(1)}, u32[]{:S(2)}, u32[]{:S(2)}) collective-permute-start(f32[1,8,128]{2,1,0:T(8,128)S(1)} %add.50), channel_id=1, source_target_pairs={{0,4},{2,6},{4,0},{6,2},{1,5},{3,7},{5,1},{7,3},{8,12},{10,14},{12... | collective-permute-start | bytes 12296 | tf_op jit(solution)/shard_map/ppermute | solution.py:45

commit v3 on v2

--- a/solution.py
+++ b/solution.py
@@ -34,17 +34,19 @@
 
 
 def group_sum(value, axes):
+    size = 1
     for axis in axes:
-        size = lax.axis_size(axis)
-        if size & (size - 1):
-            value = lax.psum(value, axis)
-            continue
-        step = 1
-        while step < size:
-            pairs = [(i, i ^ step) for i in range(size)]
-            value = value + lax.ppermute(value, axis, pairs)
-            step *= 2
-    return value
+        size *= lax.axis_size(axis)
+    me = lax.axis_index(axes)
+    held = [value]
+    for shift in range(size - 1, 0, -1):
+        pairs = [(i, (i + shift) % size) for i in range(size)]
+        held.append(lax.ppermute(value, axes, pairs))
+    ordered = jnp.roll(jnp.stack(held, 0), me, axis=0)
+    total = ordered[0]
+    for m in range(1, size):
+        total = total + ordered[m]
+    return total
 
 
 def cell_dot(left, right):
@@ -179,7 +181,7 @@
         cost_estimate=pl.CostEstimate(flops=40 * spins.size, bytes_accessed=5 * nbytes, transcendentals=0),
     )(upwind, spins, after, before, perp_field)
 
-    sums = group_sum(sums, ("gy", "gx"))
+    sums = group_sum(sums, ("gx", "gy"))
     climbing = indices == climber[0]
     ending = (indices == 0) | (indices == total - 1)
     flags = jnp.stack([climbing, ending], 0).astype(jnp.int32)

time: 106 us -> 108 us (1.019)
  waiting for transfers between devices: 46.9 us -> 38.3 us
  local copies, waits for them, and re-layouts: 3.58 us -> 7.46 us
  starting transfers between devices: 14.4 us -> 17.8 us
  other arithmetic: 18.5 us -> 21.9 us
    ppermute x2, waiting for transfers between devices: 39.2 us -> 31.8 us  [from_behind(): return lax.ppermute(value, axis, pairs)]
    ppermute x3 -> x7, starting transfers between devices: 3.01 us -> 6.52 us  [group_sum(): held.append(lax.ppermute(value, axes, pairs))]
    unnamed x5 -> x26, local copies, waits for them, and re-layouts: 1.18 us -> 3.6 us
    sub x1, other arithmetic: 7.96 us -> 9.65 us  [lattice_field(): diff_z = plus_z - minus_z]
    ppermute x3 -> x7, waiting for transfers between devices: 4.35 us -> 3.39 us  [group_sum(): held.append(lax.ppermute(value, axes, pairs))]
  transfers between devices with their start and end apart: 9 -> 13, of which waited for: 8 -> 7; matrix products, arithmetic and copies ran while one was open for 19% -> 24% of each run, Pallas kernels for 0% -> 0%
where the time goes in v3:
time: 108 us; the launch traced here: 106 us
  waiting for transfers between devices  38.3 us (35%)
  other arithmetic  21.9 us (20%)
  Pallas kernels  19 us (18%)
  starting transfers between devices  17.8 us (16%)
  local copies, waits for them, and re-layouts  7.46 us (7%)
  between operations  2.12 us (2%)
    ppermute x2, waiting for transfers between devices, from_behind(): return lax.ppermute(value, axis, pairs)  31.8 us
    pallas_call x1, Pallas kernels, per_device(): pl.pallas_call(functools.partial(update_kernel, root_cells), grid=grid, i...  10.2 us
    sub x1, other arithmetic, lattice_field(): diff_z = plus_z - minus_z  9.65 us
    pallas_call x1, Pallas kernels, per_device(): pl.pallas_call(tangent_kernel, grid=grid, in_specs=[smem, block, block, b...  8.84 us
    ppermute x2, starting transfers between devices, from_behind(): return lax.ppermute(value, axis, pairs)  7.47 us
    ppermute x7, starting transfers between devices, group_sum(): held.append(lax.ppermute(value, axes, pairs))  6.52 us
    reduce_sum x1, other arithmetic, cell_dot(): return jnp.sum(left * right, axis=1, keepdims=True)  4.84 us
    unnamed x26, local copies, waits for them, and re-layouts  3.6 us
  transfers between devices with their start and end apart: 13, of which 7 were waited for; matrix products, arithmetic and copies ran while one was open for 24% of the time, Pallas kernels for 0%

profile of v3, /device:TPU:16, one launch (start us, length us, event | category | flops | bytes accessed | tf_op | source)
XLA Modules:
  0.0 106.5 jit_solution(6953272521415133347)
XLA Ops:
  0.6 2.4 %collective-permute-start = (f32[1,3,32,64,128]{4,3,2,1,0:T(8,128)}, f32[1,3,32,64,128]{4,3,2,1,0:T(8,128)}, u32[]{:S(2)}, u32[]{:S(2)}) collective-permute-start(f32[1,3,32,64,128]{4,3,2,1,0:T(8,128)} %s_ref.3), channel_id=1, source_target_pairs={{8,0},{16,8},{24,16},{9,1},{17,9},{25,17},{10,2},{18,10},{26,18},{... | collective-permute-start | bytes 9437192 | tf_op jit(solution)/shard_map/ppermute | solution.py:33
  3.0 5.1 %collective-permute-start.1 = (f32[1,3,32,64,128]{4,3,2,1,0:T(8,128)}, f32[1,3,32,64,128]{4,3,2,1,0:T(8,128)}, u32[]{:S(2)}, u32[]{:S(2)}) collective-permute-start(f32[1,3,32,64,128]{4,3,2,1,0:T(8,128)} %s_ref.3), channel_id=1, source_target_pairs={{0,8},{8,16},{16,24},{1,9},{9,17},{17,25},{2,10},{10,18},{18,26},{... | collective-permute-start | bytes 9437192 | tf_op jit(solution)/shard_map/ppermute | solution.py:33
  8.1 1.6 %fusion.8 = (f32[1,3,1,64,128]{4,3,2,1,0:T(8,128)}, f32[1,3,1,64,128]{4,3,2,1,0:T(8,128)S(1)}) fusion(f32[1,3,32,64,128]{4,3,2,1,0:T(8,128)} %s_ref.3), kind=kLoop, calls=%fused_computation.47 | loop fusion | bytes 393216 | tf_op jit(solution)/shard_map/slice | solution.py:25
  9.7 1.7 %collective-permute-start.2 = (f32[1,3,1,64,128]{4,3,2,1,0:T(8,128)}, f32[1,3,1,64,128]{4,3,2,1,0:T(8,128)S(1)}, u32[]{:S(2)}, u32[]{:S(2)}) collective-permute-start(f32[1,3,1,64,128]{4,3,2,1,0:T(8,128)} %get-tuple-element.23), channel_id=1, source_target_pairs={{2,0},{4,2},{6,4},{0,6},{3,1},{5,3},{7,5},{1,7},{10,8},{12,10},{14... | collective-permute-start | bytes 294920 | tf_op jit(solution)/shard_map/ppermute | solution.py:25
  11.5 1.4 %fusion.9 = (f32[1]{0:T(128)}, f32[1]{0:T(128)}, f32[1]{0:T(128)}) fusion(f32[3]{0:T(128)} %param.10), kind=kLoop, calls=%fused_computation.48 | loop fusion | bytes 24 | tf_op jit(solution)/shard_map/slice | solution.py:73
  12.9 1.3 %broadcast_multiply_fusion = f32[3]{0:T(128)S(1)} fusion(f32[3]{0:T(128)} %constant.45.clone, f32[]{:T(128)} %bitcast.5), kind=kLoop, calls=%fused_computation.45 | loop fusion | flops 3 | bytes 28 | tf_op jit(solution)/shard_map/mul | solution.py:73
  14.9 9.7 %fusion.2 = (f32[1,3,32,64,128]{4,3,2,1,0:T(8,128)}, f32[1,3,34,64,128]{4,3,2,1,0:T(8,128)S(1)}, f32[1,3,32,64,128]{4,3,2,1,0:T(8,128)}) fusion(f32[1,3,32,64,128]{4,3,2,1,0:T(8,128)} %s_ref.3, f32[1,3,34,64,128]{4,3,2,1,0:T(8,128)S(1)} %constant_dynamic-update-slice_fusion.2, f32[1,3,1,64,128]{4,3,2,1,0:T(8,128)S(1)} %collective-permute-done.3, ...), kind=kLoop, calls=%fused_computation.11 | loop fusion | flops 3145728 | bytes 12779520 | tf_op jit(solution)/shard_map/sub | solution.py:67
  24.5 0.8 fusion.7
  25.4 1.5 %collective-permute-start.4 = (f32[1,3,34,1,128]{4,3,2,1,0:T(1,128)}, f32[1,3,34,1,128]{4,3,2,1,0:T(1,128)}, u32[]{:S(2)}, u32[]{:S(2)}) collective-permute-start(f32[1,3,34,1,128]{4,3,2,1,0:T(1,128)} %get-tuple-element.16), channel_id=1, source_target_pairs={{1,0},{0,1},{3,2},{2,3},{5,4},{4,5},{7,6},{6,7},{9,8},{8,9},{11,10... | collective-permute-start | bytes 156680 | tf_op jit(solution)/shard_map/ppermute | solution.py:25
  27.4 0.6 add_convert_fusion.flag_ref
  28.7 1.6 %collective-permute-done.4 = f32[1,3,34,1,128]{4,3,2,1,0:T(1,128)} collective-permute-done((f32[1,3,34,1,128]{4,3,2,1,0:T(1,128)}, f32[1,3,34,1,128]{4,3,2,1,0:T(1,128)}, u32[]{:S(2)}, u32[]{:S(2)}) %collective-permute-start.4) | collective-permute-done | bytes 52256 | tf_op jit(solution)/shard_map/ppermute | solution.py:25
  30.2 1.5 %collective-permute-done.5 = f32[1,3,34,1,128]{4,3,2,1,0:T(1,128)} collective-permute-done((f32[1,3,34,1,128]{4,3,2,1,0:T(1,128)}, f32[1,3,34,1,128]{4,3,2,1,0:T(1,128)}, u32[]{:S(2)}, u32[]{:S(2)}) %collective-permute-start.5) | collective-permute-done | bytes 52256 | tf_op jit(solution)/shard_map/ppermute | solution.py:22
  31.8 1.6 %fusion.4 = f32[1,3,32,64,128]{4,3,2,1,0:T(8,128)S(1)} fusion(f32[1,3,34,1,128]{4,3,2,1,0:T(1,128)} %collective-permute-done.4, f32[1,3,34,64,128]{4,3,2,1,0:T(8,128)S(1)} %constant_dynamic-update-slice_fusion, f32[1,3,34,1,128]{4,3,2,1,0:T(1,128)} %collective-permute-done.5), kind=kLoop, calls=%fused_computation.13 | loop fusion | flops 2359296 | bytes 6592512 | tf_op jit(solution)/shard_map/sub | solution.py:66
  33.4 0.7 slice_subtract_fusion.2
  34.2 1.1 %copy-done = f32[1,3,32,64,128]{4,3,2,1,0:T(8,128)S(1)} copy-done((f32[1,3,32,64,128]{4,3,2,1,0:T(8,128)S(1)}, f32[1,3,32,64,128]{4,3,2,1,0:T(8,128)}, u32[]{:S(2)}) %copy-start) | copy-done | bytes 3145752
  35.3 1.0 copy-done.2
  36.3 4.8 %multiply_reduce_fusion = (f32[32,64,128]{2,1,0:T(8,128)S(1)}, f32[1,3,32,64,128]{4,3,2,1,0:T(8,128)S(1)}) fusion(f32[1,3,32,64,128]{4,3,2,1,0:T(8,128)S(1)} %copy-done, f32[3]{0:T(128)S(1)} %broadcast_multiply_fusion, f32[1,1,32,64,128]{4,3,2,1,0:T(8,128)S(1)} %get-tuple-element.18, f32[1,1,32,64,128]{4,3,2,1,0:T(8,128)S(1)} %get-tuple-element.19, ...), kind=kLoop, calls=%fused_computation.10 | loop fusion | flops 13107200 | bytes 14129172 | tf_op jit(solution)/shard_map/reduce_sum | solution.py:53
  41.2 2.5 %multiply_subtract_fusion.pf_ref = f32[1,3,32,64,128]{4,3,2,1,0:T(8,128)} fusion(f32[1,3,32,64,128]{4,3,2,1,0:T(8,128)S(1)} %get-tuple-element.14, f32[1,3,32,64,128]{4,3,2,1,0:T(8,128)S(1)} %copy-done, f32[32,64,128]{2,1,0:T(8,128)S(1)} %get-tuple-element.13), kind=kLoop, calls=%fused_computation.9 | loop fusion | flops 1572864 | bytes 10485760 | tf_op jit(solution)/shard_map/sub | solution.py:162
  43.7 29.0 %collective-permute-done.nx_ref = f32[1,3,32,64,128]{4,3,2,1,0:T(8,128)} collective-permute-done((f32[1,3,32,64,128]{4,3,2,1,0:T(8,128)}, f32[1,3,32,64,128]{4,3,2,1,0:T(8,128)}, u32[]{:S(2)}, u32[]{:S(2)}) %collective-permute-start) | collective-permute-done | bytes 3145760 | tf_op jit(solution)/shard_map/ppermute | solution.py:33
  72.7 2.8 %collective-permute-done.1.pv_ref = f32[1,3,32,64,128]{4,3,2,1,0:T(8,128)} collective-permute-done((f32[1,3,32,64,128]{4,3,2,1,0:T(8,128)}, f32[1,3,32,64,128]{4,3,2,1,0:T(8,128)}, u32[]{:S(2)}, u32[]{:S(2)}) %collective-permute-start.1) | collective-permute-done | bytes 3145760 | tf_op jit(solution)/shard_map/ppermute | solution.py:33
  75.5 8.8 %shard_map.85 = (f32[1,3,32,64,128]{4,3,2,1,0:T(8,128)}, f32[1,8,128]{2,1,0:T(8,128)}) custom-call(s32[1]{0:T(128)S(6)} %copy.26.up_ref, f32[1,3,32,64,128]{4,3,2,1,0:T(8,128)} %s_ref.3, f32[1,3,32,64,128]{4,3,2,1,0:T(8,128)} %collective-permute-done.nx_ref, f32[1,3,32,64,128]{4,3,2,1,0:T(8,128)} %collective-permute-done.1.pv_ref, ...), custom_call_target="tpu_custom_call" | custom-call | flops 31457280 | bytes 15728640 | tf_op jit(solution)/shard_map/pallas_call | solution.py:173
  84.3 0.7 collective-permute-start.6
  85.0 0.7 constant_dynamic-update-slice_fusion.18
  85.7 2.0 %collective-permute-start.7 = (f32[1,8,128]{2,1,0:T(8,128)}, f32[1,8,128]{2,1,0:T(8,128)S(1)}, u32[]{:S(2)}, u32[]{:S(2)}) collective-permute-start(f32[1,8,128]{2,1,0:T(8,128)} %get-tuple-element.8), channel_id=1, source_target_pairs={{0,6},{1,7},{2,0},{3,1},{4,2},{5,3},{6,4},{7,5},{8,14},{9,15},{10,... | collective-permute-start | bytes 12296 | tf_op jit(solution)/shard_map/ppermute | solution.py:44
  88.5 1.2 %collective-permute-start.10 = (f32[1,8,128]{2,1,0:T(8,128)}, f32[1,8,128]{2,1,0:T(8,128)S(1)}, u32[]{:S(2)}, u32[]{:S(2)}) collective-permute-start(f32[1,8,128]{2,1,0:T(8,128)} %get-tuple-element.8), channel_id=1, source_target_pairs={{0,3},{1,4},{2,5},{3,6},{4,7},{5,0},{6,1},{7,2},{8,11},{9,12},{10,... | collective-permute-start | bytes 12296 | tf_op jit(solution)/shard_map/ppermute | solution.py:44
  89.8 1.0 collective-permute-start.11
  90.8 0.7 collective-permute-start.12
  91.8 1.4 %collective-permute-done.10 = f32[1,8,128]{2,1,0:T(8,128)S(1)} collective-permute-done((f32[1,8,128]{2,1,0:T(8,128)}, f32[1,8,128]{2,1,0:T(8,128)S(1)}, u32[]{:S(2)}, u32[]{:S(2)}) %collective-permute-start.10) | collective-permute-done | bytes 4128 | tf_op jit(solution)/shard_map/ppermute | solution.py:44
  93.3 1.7 %collective-permute-done.12 = f32[1,8,128]{2,1,0:T(8,128)S(1)} collective-permute-done((f32[1,8,128]{2,1,0:T(8,128)}, f32[1,8,128]{2,1,0:T(8,128)S(1)}, u32[]{:S(2)}, u32[]{:S(2)}) %collective-permute-start.12) | collective-permute-done | bytes 4128 | tf_op jit(solution)/shard_map/ppermute | solution.py:44
  95.0 0.7 constant_dynamic-update-slice_fusion.10
  95.7 0.6 fusion.5.sums_ref
  96.3 10.2 %shard_map.86 = (f32[1,3,32,64,128]{4,3,2,1,0:T(8,128)}, f32[1,3,32,64,128]{4,3,2,1,0:T(8,128)}, f32[1,1,2]{2,1,0:T(1,128)}) custom-call(s32[2,1]{1,0:T(2,128)} %add_convert_fusion.flag_ref, f32[1,8,128]{2,1,0:T(8,128)} %fusion.5.sums_ref, f32[1,3,32,64,128]{4,3,2,1,0:T(8,128)} %s_ref.3, f32[1,3,32,64,128]{4,3,2,1,0:T(8,128)} %v_ref.1, ...), custom_call_target="tpu_custom_call" | custom-call | flops 35389440 | bytes 18874368 | tf_op jit(solution)/shard_map/pallas_call | solution.py:188
  (35 shorter events, 1.6 us)
Async XLA Ops:
  0.6 72.1 %collective-permute-start = (f32[1,3,32,64,128]{4,3,2,1,0:T(8,128)}, f32[1,3,32,64,128]{4,3,2,1,0:T(8,128)}, u32[]{:S(2)}, u32[]{:S(2)}) collective-permute-start(f32[1,3,32,64,128]{4,3,2,1,0:T(8,128)} %s_ref.3), channel_id=1, source_target_pairs={{8,0},{16,8},{24,16},{9,1},{17,9},{25,17},{10,2},{18,10},{26,18},{... | collective-permute-start | bytes 9437192 | tf_op jit(solution)/shard_map/ppermute | solution.py:33
  3.0 72.5 %collective-permute-start.1 = (f32[1,3,32,64,128]{4,3,2,1,0:T(8,128)}, f32[1,3,32,64,128]{4,3,2,1,0:T(8,128)}, u32[]{:S(2)}, u32[]{:S(2)}) collective-permute-start(f32[1,3,32,64,128]{4,3,2,1,0:T(8,128)} %s_ref.3), channel_id=1, source_target_pairs={{0,8},{8,16},{16,24},{1,9},{9,17},{17,25},{2,10},{10,18},{18,26},{... | collective-permute-start | bytes 9437192 | tf_op jit(solution)/shard_map/ppermute | solution.py:33
  9.7 5.1 %collective-permute-start.3 = (f32[1,3,1,64,128]{4,3,2,1,0:T(8,128)S(1)}, f32[1,3,1,64,128]{4,3,2,1,0:T(8,128)S(1)}, u32[]{:S(2)}, u32[]{:S(2)}) collective-permute-start(f32[1,3,1,64,128]{4,3,2,1,0:T(8,128)S(1)} %get-tuple-element.24), channel_id=1, source_target_pairs={{0,2},{2,4},{4,6},{6,0},{1,3},{3,5},{5,7},{7,1},{8,10},{10,12},{12... | collective-permute-start | bytes 294920 | tf_op jit(solution)/shard_map/ppermute | solution.py:22
  9.7 5.1 %collective-permute-start.2 = (f32[1,3,1,64,128]{4,3,2,1,0:T(8,128)}, f32[1,3,1,64,128]{4,3,2,1,0:T(8,128)S(1)}, u32[]{:S(2)}, u32[]{:S(2)}) collective-permute-start(f32[1,3,1,64,128]{4,3,2,1,0:T(8,128)} %get-tuple-element.23), channel_id=1, source_target_pairs={{2,0},{4,2},{6,4},{0,6},{3,1},{5,3},{7,5},{1,7},{10,8},{12,10},{14... | collective-permute-start | bytes 294920 | tf_op jit(solution)/shard_map/ppermute | solution.py:25
  24.5 8.8 %copy-start.1 = (f32[1,3,34,64,128]{4,3,2,1,0:T(8,128)}, f32[1,3,34,64,128]{4,3,2,1,0:T(8,128)S(1)}, u32[]{:S(2)}) copy-start(f32[1,3,34,64,128]{4,3,2,1,0:T(8,128)S(1)} %constant_dynamic-update-slice_fusion) | copy-start | bytes 10027012
  25.4 4.9 %collective-permute-start.4 = (f32[1,3,34,1,128]{4,3,2,1,0:T(1,128)}, f32[1,3,34,1,128]{4,3,2,1,0:T(1,128)}, u32[]{:S(2)}, u32[]{:S(2)}) collective-permute-start(f32[1,3,34,1,128]{4,3,2,1,0:T(1,128)} %get-tuple-element.16), channel_id=1, source_target_pairs={{1,0},{0,1},{3,2},{2,3},{5,4},{4,5},{7,6},{6,7},{9,8},{8,9},{11,10... | collective-permute-start | bytes 156680 | tf_op jit(solution)/shard_map/ppermute | solution.py:25
  26.9 4.9 %collective-permute-start.5 = (f32[1,3,34,1,128]{4,3,2,1,0:T(1,128)}, f32[1,3,34,1,128]{4,3,2,1,0:T(1,128)}, u32[]{:S(2)}, u32[]{:S(2)}) collective-permute-start(f32[1,3,34,1,128]{4,3,2,1,0:T(1,128)} %get-tuple-element.15), channel_id=1, source_target_pairs={{0,1},{1,0},{2,3},{3,2},{4,5},{5,4},{6,7},{7,6},{8,9},{9,8},{10,11... | collective-permute-start | bytes 156680 | tf_op jit(solution)/shard_map/ppermute | solution.py:22
  28.7 4.7 %copy-start.3 = (f32[1,3,32,64,128]{4,3,2,1,0:T(8,128)S(1)}, f32[1,3,32,64,128]{4,3,2,1,0:T(8,128)}, u32[]{:S(2)}) copy-start(f32[1,3,32,64,128]{4,3,2,1,0:T(8,128)} %get-tuple-element.20) | copy-start | bytes 9437188
  28.7 4.7 %copy-start.4 = (f32[1,3,32,64,128]{4,3,2,1,0:T(8,128)S(1)}, f32[1,3,32,64,128]{4,3,2,1,0:T(8,128)}, u32[]{:S(2)}) copy-start(f32[1,3,32,64,128]{4,3,2,1,0:T(8,128)} %get-tuple-element.22) | copy-start | bytes 9437188
  33.4 1.9 %copy-start = (f32[1,3,32,64,128]{4,3,2,1,0:T(8,128)S(1)}, f32[1,3,32,64,128]{4,3,2,1,0:T(8,128)}, u32[]{:S(2)}) copy-start(f32[1,3,32,64,128]{4,3,2,1,0:T(8,128)} %s_ref.3) | copy-start | bytes 9437188
  33.4 2.9 %copy-start.2 = (f32[1,3,34,64,128]{4,3,2,1,0:T(8,128)S(1)}, f32[1,3,34,64,128]{4,3,2,1,0:T(8,128)}, u32[]{:S(2)}) copy-start(f32[1,3,34,64,128]{4,3,2,1,0:T(8,128)} %copy-done.1) | copy-start | bytes 10027012
  84.3 5.5 %collective-permute-start.6 = (f32[1,8,128]{2,1,0:T(8,128)}, f32[1,8,128]{2,1,0:T(8,128)S(1)}, u32[]{:S(2)}, u32[]{:S(2)}) collective-permute-start(f32[1,8,128]{2,1,0:T(8,128)} %get-tuple-element.8), channel_id=1, source_target_pairs={{0,7},{1,0},{2,1},{3,2},{4,3},{5,4},{6,5},{7,6},{8,15},{9,8},{10,9... | collective-permute-start | bytes 12296 | tf_op jit(solution)/shard_map/ppermute | solution.py:44
  85.7 5.1 %collective-permute-start.7 = (f32[1,8,128]{2,1,0:T(8,128)}, f32[1,8,128]{2,1,0:T(8,128)S(1)}, u32[]{:S(2)}, u32[]{:S(2)}) collective-permute-start(f32[1,8,128]{2,1,0:T(8,128)} %get-tuple-element.8), channel_id=1, source_target_pairs={{0,6},{1,7},{2,0},{3,1},{4,2},{5,3},{6,4},{7,5},{8,14},{9,15},{10,... | collective-permute-start | bytes 12296 | tf_op jit(solution)/shard_map/ppermute | solution.py:44
  87.8 3.8 %collective-permute-start.8 = (f32[1,8,128]{2,1,0:T(8,128)}, f32[1,8,128]{2,1,0:T(8,128)S(1)}, u32[]{:S(2)}, u32[]{:S(2)}) collective-permute-start(f32[1,8,128]{2,1,0:T(8,128)} %get-tuple-element.8), channel_id=1, source_target_pairs={{0,5},{1,6},{2,7},{3,0},{4,1},{5,2},{6,3},{7,4},{8,13},{9,14},{10,... | collective-permute-start | bytes 12296 | tf_op jit(solution)/shard_map/ppermute | solution.py:44
  88.0 3.8 %collective-permute-start.9 = (f32[1,8,128]{2,1,0:T(8,128)}, f32[1,8,128]{2,1,0:T(8,128)S(1)}, u32[]{:S(2)}, u32[]{:S(2)}) collective-permute-start(f32[1,8,128]{2,1,0:T(8,128)} %get-tuple-element.8), channel_id=1, source_target_pairs={{0,4},{1,5},{2,6},{3,7},{4,0},{5,1},{6,2},{7,3},{8,12},{9,13},{10,... | collective-permute-start | bytes 12296 | tf_op jit(solution)/shard_map/ppermute | solution.py:44
  88.5 4.7 %collective-permute-start.10 = (f32[1,8,128]{2,1,0:T(8,128)}, f32[1,8,128]{2,1,0:T(8,128)S(1)}, u32[]{:S(2)}, u32[]{:S(2)}) collective-permute-start(f32[1,8,128]{2,1,0:T(8,128)} %get-tuple-element.8), channel_id=1, source_target_pairs={{0,3},{1,4},{2,5},{3,6},{4,7},{5,0},{6,1},{7,2},{8,11},{9,12},{10,... | collective-permute-start | bytes 12296 | tf_op jit(solution)/shard_map/ppermute | solution.py:44
  89.8 3.5 %collective-permute-start.11 = (f32[1,8,128]{2,1,0:T(8,128)}, f32[1,8,128]{2,1,0:T(8,128)S(1)}, u32[]{:S(2)}, u32[]{:S(2)}) collective-permute-start(f32[1,8,128]{2,1,0:T(8,128)} %get-tuple-element.8), channel_id=1, source_target_pairs={{0,2},{1,3},{2,4},{3,5},{4,6},{5,7},{6,0},{7,1},{8,10},{9,11},{10,... | collective-permute-start | bytes 12296 | tf_op jit(solution)/shard_map/ppermute | solution.py:44
  90.8 4.1 %collective-permute-start.12 = (f32[1,8,128]{2,1,0:T(8,128)}, f32[1,8,128]{2,1,0:T(8,128)S(1)}, u32[]{:S(2)}, u32[]{:S(2)}) collective-permute-start(f32[1,8,128]{2,1,0:T(8,128)} %get-tuple-element.8), channel_id=1, source_target_pairs={{0,1},{1,2},{2,3},{3,4},{4,5},{5,6},{6,7},{7,0},{8,9},{9,10},{10,1... | collective-permute-start | bytes 12296 | tf_op jit(solution)/shard_map/ppermute | solution.py:44

commit v4 on v2

--- a/solution.py
+++ b/solution.py
@@ -11,6 +11,7 @@
 SPRING = 2.0
 EPSILON = 1e-06
 ROWS = 4
+VMEM_LIMIT = 8 * 1024 * 1024
 
 
 def extended(block, sides, width):
@@ -75,8 +76,10 @@
     return jnp.sum(x.reshape(-1, 8, x.shape[-1]), axis=0)
 
 
-def tangent_kernel(up_ref, s_ref, nx_ref, pv_ref, pf_ref, tp_ref, sums_ref, acc_ref):
+def tangent_kernel(rows, up_ref, s_ref, nx_ref, pv_ref, pf_ref, tp_ref, sums_ref, acc_ref):
+    image = pl.program_id(0)
     step = pl.program_id(1)
+    here = pl.ds(pl.multiple_of(step * rows, rows), rows)
 
     @pl.when(step == 0)
     def _():
@@ -85,15 +88,15 @@
     up = up_ref[pl.program_id(0)]
     ahead = jnp.where(up >= 0, 1.0, 0.0).astype(jnp.float32)
     behind = jnp.where(up <= 0, 1.0, 0.0).astype(jnp.float32)
-    s = [s_ref[0, c] for c in range(3)]
+    s = [s_ref[image, c, here] for c in range(3)]
     fwd = [nx_ref[0, c] - s[c] for c in range(3)]
     bwd = [s[c] - pv_ref[0, c] for c in range(3)]
     raw = [ahead * fwd[c] + behind * bwd[c] for c in range(3)]
     d = raw[0] * s[0] + raw[1] * s[1] + raw[2] * s[2]
     tp = [raw[c] - d * s[c] for c in range(3)]
     for c in range(3):
-        tp_ref[0, c] = tp[c]
-    pf = [pf_ref[0, c] for c in range(3)]
+        tp_ref[image, c, here] = tp[c]
+    pf = [pf_ref[image, c, here] for c in range(3)]
     acc_ref[0] += fold(tp[0] * tp[0] + tp[1] * tp[1] + tp[2] * tp[2])
     acc_ref[1] += fold(pf[0] * tp[0] + pf[1] * tp[1] + pf[2] * tp[2])
     acc_ref[2] += fold(fwd[0] * fwd[0] + fwd[1] * fwd[1] + fwd[2] * fwd[2])
@@ -110,8 +113,9 @@
         sums_ref[0] = out
 
 
-def update_kernel(root_cells, flag_ref, sums_ref, s_ref, v_ref, pf_ref, tp_ref, ns_ref, nv_ref, sp_ref):
+def update_kernel(root_cells, rows, flag_ref, sums_ref, s_ref, v_ref, pf_ref, tp_ref, ns_ref, nv_ref, sp_ref):
     image = pl.program_id(0)
+    here = pl.ds(pl.multiple_of(pl.program_id(1) * rows, rows), rows)
     tot = sums_ref[0]
     lane = lax.broadcasted_iota(jnp.int32, (8, 128), 1)
     row = lax.broadcasted_iota(jnp.int32, (8, 128), 0)
@@ -135,13 +139,13 @@
         pair = lax.broadcasted_iota(jnp.int32, (1, 2), 1)
         sp_ref[0] = jnp.where(pair == 0, dist_next, dist_prev) / root_cells
 
-    f = [keep * pf_ref[0, c] - coef * tp_ref[0, c] for c in range(3)]
-    v = [v_ref[0, c] for c in range(3)]
+    f = [keep * pf_ref[image, c, here] - coef * tp_ref[image, c, here] for c in range(3)]
+    v = [v_ref[image, c, here] for c in range(3)]
     vf = v[0] * f[0] + v[1] * f[1] + v[2] * f[2]
     ff = f[0] * f[0] + f[1] * f[1] + f[2] * f[2]
     gain = jnp.maximum(vf, 0.0) / jnp.maximum(ff, 1.0)
     nv = [gain * f[c] + TIME_STEP * f[c] for c in range(3)]
-    moved = [s_ref[0, c] + TIME_STEP * nv[c] for c in range(3)]
+    moved = [s_ref[image, c, here] + TIME_STEP * nv[c] for c in range(3)]
     length = jnp.sqrt(moved[0] * moved[0] + moved[1] * moved[1] + moved[2] * moved[2])
     for c in range(3):
         nv_ref[0, c] = nv[c]
@@ -166,16 +170,20 @@
     block = pl.BlockSpec((1, 3, rows, ny, nz), lambda i, j: (i, 0, j, 0, 0))
     small = pl.BlockSpec((1, 8, 128), lambda i, j: (i, 0, 0))
     smem = pl.BlockSpec(memory_space=pltpu.SMEM)
+    whole = pl.BlockSpec(memory_space=pltpu.VMEM)
+    params = pltpu.CompilerParams(
+        dimension_semantics=("arbitrary", "arbitrary"), vmem_limit_bytes=VMEM_LIMIT
+    )
     big = jax.ShapeDtypeStruct(spins.shape, jnp.float32)
     nbytes = spins.size * 4
     tangent_perp, sums = pl.pallas_call(
-        tangent_kernel,
+        functools.partial(tangent_kernel, rows),
         grid=grid,
-        in_specs=[smem, block, block, block, block],
-        out_specs=[block, small],
+        in_specs=[smem, whole, block, block, whole],
+        out_specs=[whole, small],
         out_shape=[big, jax.ShapeDtypeStruct((count, 8, 128), jnp.float32)],
         scratch_shapes=[pltpu.VMEM((4, 8, nz), jnp.float32)],
-        compiler_params=pltpu.CompilerParams(dimension_semantics=("arbitrary", "arbitrary")),
+        compiler_params=params,
         cost_estimate=pl.CostEstimate(flops=40 * spins.size, bytes_accessed=5 * nbytes, transcendentals=0),
     )(upwind, spins, after, before, perp_field)
 
@@ -184,12 +192,12 @@
     ending = (indices == 0) | (indices == total - 1)
     flags = jnp.stack([climbing, ending], 0).astype(jnp.int32)
     new_spins, new_velocity, spacing = pl.pallas_call(
-        functools.partial(update_kernel, root_cells),
+        functools.partial(update_kernel, root_cells, rows),
         grid=grid,
-        in_specs=[smem, small, block, block, block, block],
+        in_specs=[smem, small, whole, whole, whole, whole],
         out_specs=[block, block, pl.BlockSpec((1, 1, 2), lambda i, j: (i, 0, 0))],
         out_shape=[big, big, jax.ShapeDtypeStruct((count, 1, 2), jnp.float32)],
-        compiler_params=pltpu.CompilerParams(dimension_semantics=("arbitrary", "arbitrary")),
+        compiler_params=params,
         cost_estimate=pl.CostEstimate(flops=45 * spins.size, bytes_accessed=6 * nbytes, transcendentals=spins.size // 3),
     )(flags, sums, spins, velocity, perp_field, tangent_perp)
     return new_spins, new_velocity, spacing.reshape(count, 2)

time: 106 us -> 100 us (0.943)
  Pallas kernels: 19 us -> 8.67 us
  local copies, waits for them, and re-layouts: 3.58 us -> 10.9 us
  other arithmetic: 18.5 us -> 15.4 us
  waiting for transfers between devices: 46.9 us -> 49.1 us
  starting transfers between devices: 14.4 us -> 12.9 us
    pallas_call x2, Pallas kernels: 19 us -> 8.67 us  [the longest x1 5.98 us: per_device(): pl.pallas_call(functools.partial(update_kernel, root_cells, rows), grid=g...]
    unnamed x5 -> x15, local copies, waits for them, and re-layouts: 1.18 us -> 8.52 us
    ppermute x2, waiting for transfers between devices: 39.2 us -> 41.1 us  [from_behind(): return lax.ppermute(value, axis, pairs)]
    sub x1, other arithmetic: 2.48 us -> 0.83 us  [per_device(): perp_field = field - cell_dot(field, spins) * spins]
    ppermute x2, starting transfers between devices: 7.54 us -> 6.04 us  [from_behind(): return lax.ppermute(value, axis, pairs)]
    add x3, other arithmetic: 1.29 us -> 0.01 us  [group_sum(): value = value + lax.ppermute(value, axis, pairs)]
  transfers between devices with their start and end apart: 9 -> 9, of which waited for: 8 -> 8; matrix products, arithmetic and copies ran while one was open for 19% -> 18% of each run, Pallas kernels for 0% -> 0%
where the time goes in v4:
time: 100 us; the launch traced here: 99.1 us
  waiting for transfers between devices  49.1 us (49%)
  other arithmetic  15.4 us (15%)
  starting transfers between devices  12.9 us (13%)
  local copies, waits for them, and re-layouts  10.9 us (11%)
  Pallas kernels  8.67 us (9%)
  between operations  2.08 us (2%)
    ppermute x2, waiting for transfers between devices, from_behind(): return lax.ppermute(value, axis, pairs)  41.1 us
    unnamed x15, local copies, waits for them, and re-layouts  8.52 us
    sub x1, other arithmetic, lattice_field(): diff_z = plus_z - minus_z  8.29 us
    ppermute x2, starting transfers between devices, from_behind(): return lax.ppermute(value, axis, pairs)  6.04 us
    pallas_call x1, Pallas kernels, per_device(): pl.pallas_call(functools.partial(update_kernel, root_cells, rows), grid=g...  5.98 us
    ppermute x3, waiting for transfers between devices, group_sum(): value = value + lax.ppermute(value, axis, pairs)  4.7 us
    reduce_sum x1, other arithmetic, cell_dot(): return jnp.sum(left * right, axis=1, keepdims=True)  4.08 us
    ppermute x2, starting transfers between devices, extended(): lax.ppermute(lax.slice_in_dim(block, 0, width, axis=dim), axis, backward)  3.32 us
  transfers between devices with their start and end apart: 9, of which 8 were waited for; matrix products, arithmetic and copies ran while one was open for 18% of the time, Pallas kernels for 0%

profile of v4, /device:TPU:16, one launch (start us, length us, event | category | flops | bytes accessed | tf_op | source)
XLA Modules:
  0.0 99.1 jit_solution(10227991469592198925)
XLA Ops:
  0.6 2.4 %collective-permute-start = (f32[1,3,32,64,128]{4,3,2,1,0:T(8,128)}, f32[1,3,32,64,128]{4,3,2,1,0:T(8,128)S(1)}, u32[]{:S(2)}, u32[]{:S(2)}) collective-permute-start(f32[1,3,32,64,128]{4,3,2,1,0:T(8,128)} %s_ref.3), channel_id=1, source_target_pairs={{8,0},{16,8},{24,16},{9,1},{17,9},{25,17},{10,2},{18,10},{26,18},{... | collective-permute-start | bytes 9437192 | tf_op jit(solution)/shard_map/ppermute | solution.py:34
  3.0 3.7 %collective-permute-start.1 = (f32[1,3,32,64,128]{4,3,2,1,0:T(8,128)}, f32[1,3,32,64,128]{4,3,2,1,0:T(8,128)S(1)}, u32[]{:S(2)}, u32[]{:S(2)}) collective-permute-start(f32[1,3,32,64,128]{4,3,2,1,0:T(8,128)} %s_ref.3), channel_id=1, source_target_pairs={{0,8},{8,16},{16,24},{1,9},{9,17},{17,25},{2,10},{10,18},{18,26},{... | collective-permute-start | bytes 9437192 | tf_op jit(solution)/shard_map/ppermute | solution.py:34
  6.7 1.0 fusion.7
  7.7 0.1 collective-permute-start.3
  7.7 1.7 %collective-permute-start.2 = (f32[1,3,1,64,128]{4,3,2,1,0:T(8,128)S(1)}, f32[1,3,1,64,128]{4,3,2,1,0:T(8,128)S(1)}, u32[]{:S(2)}, u32[]{:S(2)}) collective-permute-start(f32[1,3,1,64,128]{4,3,2,1,0:T(8,128)S(1)} %get-tuple-element.23), channel_id=1, source_target_pairs={{2,0},{4,2},{6,4},{0,6},{3,1},{5,3},{7,5},{1,7},{10,8},{12,10},{14... | collective-permute-start | bytes 294920 | tf_op jit(solution)/shard_map/ppermute | solution.py:26
  9.5 1.4 %fusion.8 = (f32[1]{0:T(128)}, f32[1]{0:T(128)}, f32[1]{0:T(128)}) fusion(f32[3]{0:T(128)} %param.10), kind=kLoop, calls=%fused_computation.24 | loop fusion | bytes 24 | tf_op jit(solution)/shard_map/slice | solution.py:72
  10.8 0.9 collective-permute-done.3
  11.8 8.3 %fusion.2 = (f32[1,3,32,64,128]{4,3,2,1,0:T(8,128)S(1)}, f32[1,3,34,64,128]{4,3,2,1,0:T(8,128)S(1)}, f32[1,3,32,64,128]{4,3,2,1,0:T(8,128)S(1)}) fusion(f32[1,3,32,64,128]{4,3,2,1,0:T(8,128)} %s_ref.3, f32[1,3,34,64,128]{4,3,2,1,0:T(8,128)S(1)} %constant_dynamic-update-slice_fusion.2, f32[1,3,1,64,128]{4,3,2,1,0:T(8,128)S(1)} %collective-permute-done.3, ...), kind=kLoop, calls=%fused_computation.11 | loop fusion | flops 3145728 | bytes 12779520 | tf_op jit(solution)/shard_map/sub | solution.py:66
  20.1 0.1 fusion.6
  20.2 1.6 %collective-permute-start.4 = (f32[1,3,34,1,128]{4,3,2,1,0:T(1,128)S(1)}, f32[1,3,34,1,128]{4,3,2,1,0:T(1,128)S(1)}, u32[]{:S(2)}, u32[]{:S(2)}) collective-permute-start(f32[1,3,34,1,128]{4,3,2,1,0:T(1,128)S(1)} %get-tuple-element.16), channel_id=1, source_target_pairs={{1,0},{0,1},{3,2},{2,3},{5,4},{4,5},{7,6},{6,7},{9,8},{8,9},{11,10... | collective-permute-start | bytes 156680 | tf_op jit(solution)/shard_map/ppermute | solution.py:26
  21.8 0.5 collective-permute-start.5
  22.3 0.6 broadcast_multiply_fusion
  23.6 0.8 collective-permute-done.4
  24.4 1.5 %collective-permute-done.5 = f32[1,3,34,1,128]{4,3,2,1,0:T(1,128)S(1)} collective-permute-done((f32[1,3,34,1,128]{4,3,2,1,0:T(1,128)S(1)}, f32[1,3,34,1,128]{4,3,2,1,0:T(1,128)S(1)}, u32[]{:S(2)}, u32[]{:S(2)}) %collective-permute-start.5) | collective-permute-done | bytes 52256 | tf_op jit(solution)/shard_map/ppermute | solution.py:23
  25.9 0.8 fusion.4
  26.7 0.7 slice_subtract_fusion.2
  27.4 1.2 %copy-done = f32[1,3,32,64,128]{4,3,2,1,0:T(8,128)S(1)} copy-done((f32[1,3,32,64,128]{4,3,2,1,0:T(8,128)S(1)}, f32[1,3,32,64,128]{4,3,2,1,0:T(8,128)}, u32[]{:S(2)}) %copy-start) | copy-done | bytes 3145752
  28.6 4.1 %multiply_reduce_fusion = (f32[32,64,128]{2,1,0:T(8,128)S(1)}, f32[1,3,32,64,128]{4,3,2,1,0:T(8,128)S(1)}) fusion(f32[1,3,32,64,128]{4,3,2,1,0:T(8,128)S(1)} %copy-done, f32[3]{0:T(128)S(1)} %broadcast_multiply_fusion, f32[1,1,32,64,128]{4,3,2,1,0:T(8,128)S(1)} %get-tuple-element.18, f32[1,1,32,64,128]{4,3,2,1,0:T(8,128)S(1)} %get-tuple-element.19, ...), kind=kLoop, calls=%fused_computation.10 | loop fusion | flops 13107200 | bytes 14129172 | tf_op jit(solution)/shard_map/reduce_sum | solution.py:52
  32.7 0.8 multiply_subtract_fusion.pf_ref
  33.5 39.0 %collective-permute-done.nx_ref = f32[1,3,32,64,128]{4,3,2,1,0:T(8,128)S(1)} collective-permute-done((f32[1,3,32,64,128]{4,3,2,1,0:T(8,128)}, f32[1,3,32,64,128]{4,3,2,1,0:T(8,128)S(1)}, u32[]{:S(2)}, u32[]{:S(2)}) %collective-permute-start) | collective-permute-done | bytes 3145760 | tf_op jit(solution)/shard_map/ppermute | solution.py:34
  72.6 2.1 %collective-permute-done.1.pv_ref = f32[1,3,32,64,128]{4,3,2,1,0:T(8,128)S(1)} collective-permute-done((f32[1,3,32,64,128]{4,3,2,1,0:T(8,128)}, f32[1,3,32,64,128]{4,3,2,1,0:T(8,128)S(1)}, u32[]{:S(2)}, u32[]{:S(2)}) %collective-permute-start.1) | collective-permute-done | bytes 3145760 | tf_op jit(solution)/shard_map/ppermute | solution.py:34
  74.7 2.7 %shard_map.85 = (f32[1,3,32,64,128]{4,3,2,1,0:T(8,128)S(1)}, f32[1,8,128]{2,1,0:T(8,128)S(1)}) custom-call(s32[1]{0:T(128)S(6)} %copy.11.up_ref, f32[1,3,32,64,128]{4,3,2,1,0:T(8,128)S(1)} %copy-done, f32[1,3,32,64,128]{4,3,2,1,0:T(8,128)S(1)} %collective-permute-done.nx_ref, f32[1,3,32,64,128]{4,3,2,1,0:T(8,128)S(1)} %collective-permute-done.1.pv_ref, ...), custom_call_target="tpu_custom_call" | custom-call | flops 31457280 | bytes 15728640 | tf_op jit(solution)/shard_map/pallas_call | solution.py:179
  77.4 1.7 %copy-done.4 = f32[1,3,32,64,128]{4,3,2,1,0:T(8,128)} copy-done((f32[1,3,32,64,128]{4,3,2,1,0:T(8,128)}, f32[1,3,32,64,128]{4,3,2,1,0:T(8,128)S(1)}, u32[]{:S(2)}) %copy-start.4) | copy-done | bytes 3145752
  79.0 1.5 %collective-permute-start.6 = (f32[1,8,128]{2,1,0:T(8,128)S(1)}, f32[1,8,128]{2,1,0:T(8,128)S(1)}, u32[]{:S(2)}, u32[]{:S(2)}) collective-permute-start(f32[1,8,128]{2,1,0:T(8,128)S(1)} %get-tuple-element.8), channel_id=1, source_target_pairs={{0,1},{1,0},{2,3},{3,2},{4,5},{5,4},{6,7},{7,6},{8,9},{9,8},{10,11... | collective-permute-start | bytes 12296 | tf_op jit(solution)/shard_map/ppermute | solution.py:46
  80.6 2.1 %collective-permute-done.6 = f32[1,8,128]{2,1,0:T(8,128)S(1)} collective-permute-done((f32[1,8,128]{2,1,0:T(8,128)S(1)}, f32[1,8,128]{2,1,0:T(8,128)S(1)}, u32[]{:S(2)}, u32[]{:S(2)}) %collective-permute-start.6) | collective-permute-done | bytes 4128 | tf_op jit(solution)/shard_map/ppermute | solution.py:46
  83.3 0.5 collective-permute-done.7
  83.8 1.5 %collective-permute-start.8 = (f32[1,8,128]{2,1,0:T(8,128)S(1)}, f32[1,8,128]{2,1,0:T(8,128)S(1)}, u32[]{:S(2)}, u32[]{:S(2)}) collective-permute-start(f32[1,8,128]{2,1,0:T(8,128)S(1)} %add.50), channel_id=1, source_target_pairs={{0,4},{2,6},{4,0},{6,2},{1,5},{3,7},{5,1},{7,3},{8,12},{10,14},{12... | collective-permute-start | bytes 12296 | tf_op jit(solution)/shard_map/ppermute | solution.py:46
  85.3 2.1 %collective-permute-done.8 = f32[1,8,128]{2,1,0:T(8,128)S(1)} collective-permute-done((f32[1,8,128]{2,1,0:T(8,128)S(1)}, f32[1,8,128]{2,1,0:T(8,128)S(1)}, u32[]{:S(2)}, u32[]{:S(2)}) %collective-permute-start.8) | collective-permute-done | bytes 4128 | tf_op jit(solution)/shard_map/ppermute | solution.py:46
  87.4 1.9 %copy-done.2 = f32[1,3,32,64,128]{4,3,2,1,0:T(8,128)S(1)} copy-done((f32[1,3,32,64,128]{4,3,2,1,0:T(8,128)S(1)}, f32[1,3,32,64,128]{4,3,2,1,0:T(8,128)}, u32[]{:S(2)}) %copy-start.2) | copy-done | bytes 3145752
  89.3 1.9 %copy-done.3 = f32[1,3,32,64,128]{4,3,2,1,0:T(8,128)S(1)} copy-done((f32[1,3,32,64,128]{4,3,2,1,0:T(8,128)S(1)}, f32[1,3,32,64,128]{4,3,2,1,0:T(8,128)}, u32[]{:S(2)}) %copy-start.3) | copy-done | bytes 3145752
  91.2 1.9 %copy-done.5 = f32[1,3,32,64,128]{4,3,2,1,0:T(8,128)S(1)} copy-done((f32[1,3,32,64,128]{4,3,2,1,0:T(8,128)S(1)}, f32[1,3,32,64,128]{4,3,2,1,0:T(8,128)}, u32[]{:S(2)}) %copy-start.5) | copy-done | bytes 3145752
  93.1 6.0 %shard_map.86 = (f32[1,3,32,64,128]{4,3,2,1,0:T(8,128)}, f32[1,3,32,64,128]{4,3,2,1,0:T(8,128)}, f32[1,1,2]{2,1,0:T(1,128)}) custom-call(s32[2,1]{1,0:T(2,128)S(1)} %add_convert_fusion.flag_ref, f32[1,8,128]{2,1,0:T(8,128)S(1)} %add.51.sums_ref, f32[1,3,32,64,128]{4,3,2,1,0:T(8,128)S(1)} %copy-done, f32[1,3,32,64,128]{4,3,2,1,0:T(8,128)S(1)} %copy-done.3, ...), custom_call_target="tpu_custom_call" | custom-call | flops 35389440 | bytes 18874368 | tf_op jit(solution)/shard_map/pallas_call | solution.py:194
  (17 shorter events, 0.1 us)
Async XLA Ops:
  0.6 71.9 %collective-permute-start = (f32[1,3,32,64,128]{4,3,2,1,0:T(8,128)}, f32[1,3,32,64,128]{4,3,2,1,0:T(8,128)S(1)}, u32[]{:S(2)}, u32[]{:S(2)}) collective-permute-start(f32[1,3,32,64,128]{4,3,2,1,0:T(8,128)} %s_ref.3), channel_id=1, source_target_pairs={{8,0},{16,8},{24,16},{9,1},{17,9},{25,17},{10,2},{18,10},{26,18},{... | collective-permute-start | bytes 9437192 | tf_op jit(solution)/shard_map/ppermute | solution.py:34
  3.0 71.7 %collective-permute-start.1 = (f32[1,3,32,64,128]{4,3,2,1,0:T(8,128)}, f32[1,3,32,64,128]{4,3,2,1,0:T(8,128)S(1)}, u32[]{:S(2)}, u32[]{:S(2)}) collective-permute-start(f32[1,3,32,64,128]{4,3,2,1,0:T(8,128)} %s_ref.3), channel_id=1, source_target_pairs={{0,8},{8,16},{16,24},{1,9},{9,17},{17,25},{2,10},{10,18},{18,26},{... | collective-permute-start | bytes 9437192 | tf_op jit(solution)/shard_map/ppermute | solution.py:34
  7.7 4.1 %collective-permute-start.3 = (f32[1,3,1,64,128]{4,3,2,1,0:T(8,128)S(1)}, f32[1,3,1,64,128]{4,3,2,1,0:T(8,128)S(1)}, u32[]{:S(2)}, u32[]{:S(2)}) collective-permute-start(f32[1,3,1,64,128]{4,3,2,1,0:T(8,128)S(1)} %get-tuple-element.24), channel_id=1, source_target_pairs={{0,2},{2,4},{4,6},{6,0},{1,3},{3,5},{5,7},{7,1},{8,10},{10,12},{12... | collective-permute-start | bytes 294920 | tf_op jit(solution)/shard_map/ppermute | solution.py:23
  7.7 4.1 %collective-permute-start.2 = (f32[1,3,1,64,128]{4,3,2,1,0:T(8,128)S(1)}, f32[1,3,1,64,128]{4,3,2,1,0:T(8,128)S(1)}, u32[]{:S(2)}, u32[]{:S(2)}) collective-permute-start(f32[1,3,1,64,128]{4,3,2,1,0:T(8,128)S(1)} %get-tuple-element.23), channel_id=1, source_target_pairs={{2,0},{4,2},{6,4},{0,6},{3,1},{5,3},{7,5},{1,7},{10,8},{12,10},{14... | collective-permute-start | bytes 294920 | tf_op jit(solution)/shard_map/ppermute | solution.py:26
  11.8 10.5 %copy-start.6 = (f32[3]{0:T(128)S(1)}, f32[3]{0:T(128)}, u32[]{:S(2)}) copy-start(f32[3]{0:T(128)} %constant.15.clone) | copy-start | bytes 40
  20.2 4.2 %collective-permute-start.4 = (f32[1,3,34,1,128]{4,3,2,1,0:T(1,128)S(1)}, f32[1,3,34,1,128]{4,3,2,1,0:T(1,128)S(1)}, u32[]{:S(2)}, u32[]{:S(2)}) collective-permute-start(f32[1,3,34,1,128]{4,3,2,1,0:T(1,128)S(1)} %get-tuple-element.16), channel_id=1, source_target_pairs={{1,0},{0,1},{3,2},{2,3},{5,4},{4,5},{7,6},{6,7},{9,8},{8,9},{11,10... | collective-permute-start | bytes 156680 | tf_op jit(solution)/shard_map/ppermute | solution.py:26
  21.8 4.1 %collective-permute-start.5 = (f32[1,3,34,1,128]{4,3,2,1,0:T(1,128)S(1)}, f32[1,3,34,1,128]{4,3,2,1,0:T(1,128)S(1)}, u32[]{:S(2)}, u32[]{:S(2)}) collective-permute-start(f32[1,3,34,1,128]{4,3,2,1,0:T(1,128)S(1)} %get-tuple-element.15), channel_id=1, source_target_pairs={{0,1},{1,0},{2,3},{3,2},{4,5},{5,4},{6,7},{7,6},{8,9},{9,8},{10,11... | collective-permute-start | bytes 156680 | tf_op jit(solution)/shard_map/ppermute | solution.py:23
  26.7 1.9 %copy-start = (f32[1,3,32,64,128]{4,3,2,1,0:T(8,128)S(1)}, f32[1,3,32,64,128]{4,3,2,1,0:T(8,128)}, u32[]{:S(2)}) copy-start(f32[1,3,32,64,128]{4,3,2,1,0:T(8,128)} %s_ref.3) | copy-start | bytes 9437188
  33.5 43.8 %copy-start.1 = (f32[1,3,32,64,128]{4,3,2,1,0:T(8,128)}, f32[1,3,32,64,128]{4,3,2,1,0:T(8,128)S(1)}, u32[]{:S(2)}) copy-start(f32[1,3,32,64,128]{4,3,2,1,0:T(8,128)S(1)} %multiply_subtract_fusion.pf_ref) | copy-start | bytes 9437188
  77.4 1.7 %copy-start.4 = (f32[1,3,32,64,128]{4,3,2,1,0:T(8,128)}, f32[1,3,32,64,128]{4,3,2,1,0:T(8,128)S(1)}, u32[]{:S(2)}) copy-start(f32[1,3,32,64,128]{4,3,2,1,0:T(8,128)S(1)} %get-tuple-element.9.tp_ref) | copy-start | bytes 9437188
  79.0 3.6 %collective-permute-start.6 = (f32[1,8,128]{2,1,0:T(8,128)S(1)}, f32[1,8,128]{2,1,0:T(8,128)S(1)}, u32[]{:S(2)}, u32[]{:S(2)}) collective-permute-start(f32[1,8,128]{2,1,0:T(8,128)S(1)} %get-tuple-element.8), channel_id=1, source_target_pairs={{0,1},{1,0},{2,3},{3,2},{4,5},{5,4},{6,7},{7,6},{8,9},{9,8},{10,11... | collective-permute-start | bytes 12296 | tf_op jit(solution)/shard_map/ppermute | solution.py:46
  82.6 1.2 %collective-permute-start.7 = (f32[1,8,128]{2,1,0:T(8,128)S(1)}, f32[1,8,128]{2,1,0:T(8,128)S(1)}, u32[]{:S(2)}, u32[]{:S(2)}) collective-permute-start(f32[1,8,128]{2,1,0:T(8,128)S(1)} %add.49), channel_id=1, source_target_pairs={{0,2},{2,0},{4,6},{6,4},{1,3},{3,1},{5,7},{7,5},{8,10},{10,8},{12,... | collective-permute-start | bytes 12296 | tf_op jit(solution)/shard_map/ppermute | solution.py:46
  83.8 3.6 %collective-permute-start.8 = (f32[1,8,128]{2,1,0:T(8,128)S(1)}, f32[1,8,128]{2,1,0:T(8,128)S(1)}, u32[]{:S(2)}, u32[]{:S(2)}) collective-permute-start(f32[1,8,128]{2,1,0:T(8,128)S(1)} %add.50), channel_id=1, source_target_pairs={{0,4},{2,6},{4,0},{6,2},{1,5},{3,7},{5,1},{7,3},{8,12},{10,14},{12... | collective-permute-start | bytes 12296 | tf_op jit(solution)/shard_map/ppermute | solution.py:46
  87.4 1.9 %copy-start.2 = (f32[1,3,32,64,128]{4,3,2,1,0:T(8,128)S(1)}, f32[1,3,32,64,128]{4,3,2,1,0:T(8,128)}, u32[]{:S(2)}) copy-start(f32[1,3,32,64,128]{4,3,2,1,0:T(8,128)} %copy-done.1) | copy-start | bytes 9437188
  89.3 1.9 %copy-start.3 = (f32[1,3,32,64,128]{4,3,2,1,0:T(8,128)S(1)}, f32[1,3,32,64,128]{4,3,2,1,0:T(8,128)}, u32[]{:S(2)}) copy-start(f32[1,3,32,64,128]{4,3,2,1,0:T(8,128)} %v_ref.1) | copy-start | bytes 9437188
  91.2 1.9 %copy-start.5 = (f32[1,3,32,64,128]{4,3,2,1,0:T(8,128)S(1)}, f32[1,3,32,64,128]{4,3,2,1,0:T(8,128)}, u32[]{:S(2)}) copy-start(f32[1,3,32,64,128]{4,3,2,1,0:T(8,128)} %copy-done.4) | copy-start | bytes 9437188

commit v5 on v4

--- a/solution.py
+++ b/solution.py
@@ -34,6 +34,21 @@
     return lax.ppermute(value, axis, pairs)
 
 
+def add_kernel(a_ref, b_ref, o_ref):
+    o_ref[...] = a_ref[...] + b_ref[...]
+
+
+def small_add(a, b):
+    whole = pl.BlockSpec(memory_space=pltpu.VMEM)
+    return pl.pallas_call(
+        add_kernel,
+        in_specs=[whole, whole],
+        out_specs=whole,
+        out_shape=jax.ShapeDtypeStruct(a.shape, a.dtype),
+        compiler_params=pltpu.CompilerParams(vmem_limit_bytes=1024 * 1024),
+    )(a, b)
+
+
 def group_sum(value, axes):
     for axis in axes:
         size = lax.axis_size(axis)
@@ -43,7 +58,7 @@
         step = 1
         while step < size:
             pairs = [(i, i ^ step) for i in range(size)]
-            value = value + lax.ppermute(value, axis, pairs)
+            value = small_add(value, lax.ppermute(value, axis, pairs))
             step *= 2
     return value
 
@@ -76,7 +91,7 @@
     return jnp.sum(x.reshape(-1, 8, x.shape[-1]), axis=0)
 
 
-def tangent_kernel(rows, up_ref, s_ref, nx_ref, pv_ref, pf_ref, tp_ref, sums_ref, acc_ref):
+def tangent_kernel(rows, up_ref, s_ref, nx_ref, pv_ref, pf_ref, v_ref, tp_ref, sums_ref, acc_ref):
     image = pl.program_id(0)
     step = pl.program_id(1)
     here = pl.ds(pl.multiple_of(step * rows, rows), rows)
@@ -113,7 +128,7 @@
         sums_ref[0] = out
 
 
-def update_kernel(root_cells, rows, flag_ref, sums_ref, s_ref, v_ref, pf_ref, tp_ref, ns_ref, nv_ref, sp_ref):
+def update_kernel(root_cells, rows, last, climber_ref, sums_ref, s_ref, v_ref, pf_ref, tp_ref, ns_ref, nv_ref, sp_ref):
     image = pl.program_id(0)
     here = pl.ds(pl.multiple_of(pl.program_id(1) * rows, rows), rows)
     tot = sums_ref[0]
@@ -128,8 +143,9 @@
     along = along_t * scale
     dist_next = jnp.sqrt(next_sq + EPSILON)
     dist_prev = jnp.sqrt(prev_sq + EPSILON)
-    climbing = jnp.full((1, 1), flag_ref[0, image]) > 0
-    ending = jnp.full((1, 1), flag_ref[1, image]) > 0
+    index = lax.axis_index("img") * pl.num_programs(0) + image
+    climbing = jnp.full((1, 1), index) == climber_ref[0]
+    ending = (jnp.full((1, 1), index) == 0) | (jnp.full((1, 1), index) == last)
     weight = jnp.where(climbing, 2.0 * along, along - SPRING * (dist_next - dist_prev))
     coef = jnp.where(ending, 0.0, weight * scale)
     keep = jnp.where(ending, 0.0, 1.0)
@@ -179,27 +195,24 @@
     tangent_perp, sums = pl.pallas_call(
         functools.partial(tangent_kernel, rows),
         grid=grid,
-        in_specs=[smem, whole, block, block, whole],
+        in_specs=[smem, whole, block, block, whole, whole],
         out_specs=[whole, small],
         out_shape=[big, jax.ShapeDtypeStruct((count, 8, 128), jnp.float32)],
         scratch_shapes=[pltpu.VMEM((4, 8, nz), jnp.float32)],
         compiler_params=params,
         cost_estimate=pl.CostEstimate(flops=40 * spins.size, bytes_accessed=5 * nbytes, transcendentals=0),
-    )(upwind, spins, after, before, perp_field)
+    )(upwind, spins, after, before, perp_field, velocity)
 
     sums = group_sum(sums, ("gy", "gx"))
-    climbing = indices == climber[0]
-    ending = (indices == 0) | (indices == total - 1)
-    flags = jnp.stack([climbing, ending], 0).astype(jnp.int32)
     new_spins, new_velocity, spacing = pl.pallas_call(
-        functools.partial(update_kernel, root_cells, rows),
+        functools.partial(update_kernel, root_cells, rows, total - 1),
         grid=grid,
         in_specs=[smem, small, whole, whole, whole, whole],
         out_specs=[block, block, pl.BlockSpec((1, 1, 2), lambda i, j: (i, 0, 0))],
         out_shape=[big, big, jax.ShapeDtypeStruct((count, 1, 2), jnp.float32)],
         compiler_params=params,
         cost_estimate=pl.CostEstimate(flops=45 * spins.size, bytes_accessed=6 * nbytes, transcendentals=spins.size // 3),
-    )(flags, sums, spins, velocity, perp_field, tangent_perp)
+    )(climber, sums, spins, velocity, perp_field, tangent_perp)
     return new_spins, new_velocity, spacing.reshape(count, 2)
 
 

time: 100 us -> 92 us (0.920)
  local copies, waits for them, and re-layouts: 10.9 us -> 3.58 us
    unnamed x15 -> x7, local copies, waits for them, and re-layouts: 8.52 us -> 1.19 us
    pallas_call x1 -> x4, Pallas kernels: 5.98 us -> 5.42 us  [the longest x1 5.41 us: per_device(): pl.pallas_call(functools.partial(update_kernel, root_cells, rows, total -...]
  transfers between devices with their start and end apart: 9 -> 9, of which waited for: 8 -> 8; matrix products, arithmetic and copies ran while one was open for 18% -> 19% of each run, Pallas kernels for 0% -> 0%
where the time goes in v5:
time: 92 us; the launch traced here: 91.2 us
  waiting for transfers between devices  49.1 us (53%)
  other arithmetic  15.4 us (17%)
  starting transfers between devices  13 us (14%)
  Pallas kernels  8.1 us (9%)
  local copies, waits for them, and re-layouts  3.58 us (4%)
  between operations  2.06 us (2%)
    ppermute x2, waiting for transfers between devices, from_behind(): return lax.ppermute(value, axis, pairs)  41.1 us
    sub x1, other arithmetic, lattice_field(): diff_z = plus_z - minus_z  8.29 us
    ppermute x2, starting transfers between devices, from_behind(): return lax.ppermute(value, axis, pairs)  6.04 us
    pallas_call x1, Pallas kernels, per_device(): pl.pallas_call(functools.partial(update_kernel, root_cells, rows, total -...  5.41 us
    ppermute x3, waiting for transfers between devices, group_sum(): value = small_add(value, lax.ppermute(value, axis, pairs))  4.71 us
    reduce_sum x1, other arithmetic, cell_dot(): return jnp.sum(left * right, axis=1, keepdims=True)  4.08 us
    ppermute x2, starting transfers between devices, extended(): lax.ppermute(lax.slice_in_dim(block, 0, width, axis=dim), axis, backward)  3.32 us
    ppermute x3, starting transfers between devices, group_sum(): value = small_add(value, lax.ppermute(value, axis, pairs))  3.08 us
  transfers between devices with their start and end apart: 9, of which 8 were waited for; matrix products, arithmetic and copies ran while one was open for 19% of the time, Pallas kernels for 0%

profile of v5, /device:TPU:16, one launch (start us, length us, event | category | flops | bytes accessed | tf_op | source)
XLA Modules:
  0.0 91.2 jit_solution(13860137357467989420)
XLA Ops:
  0.6 2.4 %collective-permute-start = (f32[1,3,32,64,128]{4,3,2,1,0:T(8,128)}, f32[1,3,32,64,128]{4,3,2,1,0:T(8,128)S(1)}, u32[]{:S(2)}, u32[]{:S(2)}) collective-permute-start(f32[1,3,32,64,128]{4,3,2,1,0:T(8,128)} %s_ref.3), channel_id=1, source_target_pairs={{8,0},{16,8},{24,16},{9,1},{17,9},{25,17},{10,2},{18,10},{26,18},{... | collective-permute-start | bytes 9437192 | tf_op jit(solution)/shard_map/ppermute | solution.py:34
  3.0 3.7 %collective-permute-start.1 = (f32[1,3,32,64,128]{4,3,2,1,0:T(8,128)}, f32[1,3,32,64,128]{4,3,2,1,0:T(8,128)S(1)}, u32[]{:S(2)}, u32[]{:S(2)}) collective-permute-start(f32[1,3,32,64,128]{4,3,2,1,0:T(8,128)} %s_ref.3), channel_id=1, source_target_pairs={{0,8},{8,16},{16,24},{1,9},{9,17},{17,25},{2,10},{10,18},{18,26},{... | collective-permute-start | bytes 9437192 | tf_op jit(solution)/shard_map/ppermute | solution.py:34
  6.7 1.0 %fusion.7 = (f32[1,3,1,64,128]{4,3,2,1,0:T(8,128)S(1)}, f32[1,3,1,64,128]{4,3,2,1,0:T(8,128)S(1)}) fusion(f32[1,3,32,64,128]{4,3,2,1,0:T(8,128)} %s_ref.3), kind=kLoop, calls=%fused_computation.22 | loop fusion | bytes 393216 | tf_op jit(solution)/shard_map/slice | solution.py:26
  7.7 0.1 collective-permute-start.3
  7.7 1.7 %collective-permute-start.2 = (f32[1,3,1,64,128]{4,3,2,1,0:T(8,128)S(1)}, f32[1,3,1,64,128]{4,3,2,1,0:T(8,128)S(1)}, u32[]{:S(2)}, u32[]{:S(2)}) collective-permute-start(f32[1,3,1,64,128]{4,3,2,1,0:T(8,128)S(1)} %get-tuple-element.23), channel_id=1, source_target_pairs={{2,0},{4,2},{6,4},{0,6},{3,1},{5,3},{7,5},{1,7},{10,8},{12,10},{14... | collective-permute-start | bytes 294920 | tf_op jit(solution)/shard_map/ppermute | solution.py:26
  9.5 1.4 %fusion.8 = (f32[1]{0:T(128)}, f32[1]{0:T(128)}, f32[1]{0:T(128)}) fusion(f32[3]{0:T(128)} %param.10), kind=kLoop, calls=%fused_computation.23 | loop fusion | bytes 24 | tf_op jit(solution)/shard_map/slice | solution.py:87
  10.8 0.9 %collective-permute-done.3 = f32[1,3,1,64,128]{4,3,2,1,0:T(8,128)S(1)} collective-permute-done((f32[1,3,1,64,128]{4,3,2,1,0:T(8,128)S(1)}, f32[1,3,1,64,128]{4,3,2,1,0:T(8,128)S(1)}, u32[]{:S(2)}, u32[]{:S(2)}) %collective-permute-start.3) | collective-permute-done | bytes 98336 | tf_op jit(solution)/shard_map/ppermute | solution.py:23
  11.8 0.0 copy-start.2
  11.8 0.0 collective-permute-done.2
  11.8 8.3 %fusion.2 = (f32[1,3,32,64,128]{4,3,2,1,0:T(8,128)S(1)}, f32[1,3,34,64,128]{4,3,2,1,0:T(8,128)S(1)}, f32[1,3,32,64,128]{4,3,2,1,0:T(8,128)S(1)}) fusion(f32[1,3,32,64,128]{4,3,2,1,0:T(8,128)} %s_ref.3, f32[1,3,34,64,128]{4,3,2,1,0:T(8,128)S(1)} %constant_dynamic-update-slice_fusion.2, f32[1,3,1,64,128]{4,3,2,1,0:T(8,128)S(1)} %collective-permute-done.3, ...), kind=kLoop, calls=%fused_computation.11 | loop fusion | flops 3145728 | bytes 12779520 | tf_op jit(solution)/shard_map/sub | solution.py:81
  20.1 0.1 fusion.6
  20.2 1.6 %collective-permute-start.4 = (f32[1,3,34,1,128]{4,3,2,1,0:T(1,128)S(1)}, f32[1,3,34,1,128]{4,3,2,1,0:T(1,128)S(1)}, u32[]{:S(2)}, u32[]{:S(2)}) collective-permute-start(f32[1,3,34,1,128]{4,3,2,1,0:T(1,128)S(1)} %get-tuple-element.16), channel_id=1, source_target_pairs={{1,0},{0,1},{3,2},{2,3},{5,4},{4,5},{7,6},{6,7},{9,8},{8,9},{11,10... | collective-permute-start | bytes 156680 | tf_op jit(solution)/shard_map/ppermute | solution.py:26
  21.8 0.5 collective-permute-start.5
  22.3 0.6 broadcast_multiply_fusion
  23.6 0.8 collective-permute-done.4
  24.4 1.5 %collective-permute-done.5 = f32[1,3,34,1,128]{4,3,2,1,0:T(1,128)S(1)} collective-permute-done((f32[1,3,34,1,128]{4,3,2,1,0:T(1,128)S(1)}, f32[1,3,34,1,128]{4,3,2,1,0:T(1,128)S(1)}, u32[]{:S(2)}, u32[]{:S(2)}) %collective-permute-start.5) | collective-permute-done | bytes 52256 | tf_op jit(solution)/shard_map/ppermute | solution.py:23
  25.9 0.8 fusion.4
  26.7 0.0 copy-start
  26.7 0.7 slice_subtract_fusion.2
  27.4 1.2 %copy-done = f32[1,3,32,64,128]{4,3,2,1,0:T(8,128)S(1)} copy-done((f32[1,3,32,64,128]{4,3,2,1,0:T(8,128)S(1)}, f32[1,3,32,64,128]{4,3,2,1,0:T(8,128)}, u32[]{:S(2)}) %copy-start) | copy-done | bytes 3145752
  28.6 4.1 %multiply_reduce_fusion = (f32[32,64,128]{2,1,0:T(8,128)S(1)}, f32[1,3,32,64,128]{4,3,2,1,0:T(8,128)S(1)}) fusion(f32[1,3,32,64,128]{4,3,2,1,0:T(8,128)S(1)} %copy-done, f32[3]{0:T(128)S(1)} %broadcast_multiply_fusion, f32[1,1,32,64,128]{4,3,2,1,0:T(8,128)S(1)} %get-tuple-element.18, f32[1,1,32,64,128]{4,3,2,1,0:T(8,128)S(1)} %get-tuple-element.19, ...), kind=kLoop, calls=%fused_computation.10 | loop fusion | flops 13107200 | bytes 14129172 | tf_op jit(solution)/shard_map/reduce_sum | solution.py:67
  32.7 0.0 copy-start.1
  32.7 0.8 multiply_subtract_fusion.pf_ref
  33.6 39.0 %collective-permute-done.nx_ref = f32[1,3,32,64,128]{4,3,2,1,0:T(8,128)S(1)} collective-permute-done((f32[1,3,32,64,128]{4,3,2,1,0:T(8,128)}, f32[1,3,32,64,128]{4,3,2,1,0:T(8,128)S(1)}, u32[]{:S(2)}, u32[]{:S(2)}) %collective-permute-start) | collective-permute-done | bytes 3145760 | tf_op jit(solution)/shard_map/ppermute | solution.py:34
  72.6 2.1 %collective-permute-done.1.pv_ref = f32[1,3,32,64,128]{4,3,2,1,0:T(8,128)S(1)} collective-permute-done((f32[1,3,32,64,128]{4,3,2,1,0:T(8,128)}, f32[1,3,32,64,128]{4,3,2,1,0:T(8,128)S(1)}, u32[]{:S(2)}, u32[]{:S(2)}) %collective-permute-start.1) | collective-permute-done | bytes 3145760 | tf_op jit(solution)/shard_map/ppermute | solution.py:34
  74.7 2.7 %shard_map.85 = (f32[1,3,32,64,128]{4,3,2,1,0:T(8,128)S(1)}, f32[1,8,128]{2,1,0:T(8,128)S(1)}) custom-call(s32[1]{0:T(128)S(6)} %copy.11.up_ref, f32[1,3,32,64,128]{4,3,2,1,0:T(8,128)S(1)} %copy-done, f32[1,3,32,64,128]{4,3,2,1,0:T(8,128)S(1)} %collective-permute-done.nx_ref, f32[1,3,32,64,128]{4,3,2,1,0:T(8,128)S(1)} %collective-permute-done.1.pv_ref, ...), custom_call_target="tpu_custom_call" | custom-call | flops 31457280 | bytes 15728640 | tf_op jit(solution)/shard_map/pallas_call | solution.py:195
  77.4 1.6 %collective-permute-start.6 = (f32[1,8,128]{2,1,0:T(8,128)S(1)}, f32[1,8,128]{2,1,0:T(8,128)S(1)}, u32[]{:S(2)}, u32[]{:S(2)}) collective-permute-start(f32[1,8,128]{2,1,0:T(8,128)S(1)} %get-tuple-element.8.a_ref), channel_id=1, source_target_pairs={{0,1},{1,0},{2,3},{3,2},{4,5},{5,4},{6,7},{7,6},{8,9},{9,8},{10,11... | collective-permute-start | bytes 12296 | tf_op jit(solution)/shard_map/ppermute | solution.py:61
  78.9 2.1 %collective-permute-done.6.b_ref = f32[1,8,128]{2,1,0:T(8,128)S(1)} collective-permute-done((f32[1,8,128]{2,1,0:T(8,128)S(1)}, f32[1,8,128]{2,1,0:T(8,128)S(1)}, u32[]{:S(2)}, u32[]{:S(2)}) %collective-permute-start.6) | collective-permute-done | bytes 4128 | tf_op jit(solution)/shard_map/ppermute | solution.py:61
  81.0 1.2 %collective-permute-done.7.b_ref = f32[1,8,128]{2,1,0:T(8,128)S(1)} collective-permute-done((f32[1,8,128]{2,1,0:T(8,128)S(1)}, f32[1,8,128]{2,1,0:T(8,128)S(1)}, u32[]{:S(2)}, u32[]{:S(2)}) %collective-permute-start.7) | collective-permute-done | bytes 4128 | tf_op jit(solution)/shard_map/ppermute | solution.py:61
  82.2 1.5 %collective-permute-start.8 = (f32[1,8,128]{2,1,0:T(8,128)S(1)}, f32[1,8,128]{2,1,0:T(8,128)S(1)}, u32[]{:S(2)}, u32[]{:S(2)}) collective-permute-start(f32[1,8,128]{2,1,0:T(8,128)S(1)} %shard_map.87.a_ref), channel_id=1, source_target_pairs={{0,4},{2,6},{4,0},{6,2},{1,5},{3,7},{5,1},{7,3},{8,12},{10,14},{12... | collective-permute-start | bytes 12296 | tf_op jit(solution)/shard_map/ppermute | solution.py:61
  84.4 1.5 %collective-permute-done.8.b_ref = f32[1,8,128]{2,1,0:T(8,128)S(1)} collective-permute-done((f32[1,8,128]{2,1,0:T(8,128)S(1)}, f32[1,8,128]{2,1,0:T(8,128)S(1)}, u32[]{:S(2)}, u32[]{:S(2)}) %collective-permute-start.8) | collective-permute-done | bytes 4128 | tf_op jit(solution)/shard_map/ppermute | solution.py:61
  85.8 5.4 %shard_map.89 = (f32[1,3,32,64,128]{4,3,2,1,0:T(8,128)}, f32[1,3,32,64,128]{4,3,2,1,0:T(8,128)}, f32[1,1,2]{2,1,0:T(1,128)}) custom-call(s32[1]{0:T(128)S(6)} %copy.12.climber_ref, f32[1,8,128]{2,1,0:T(8,128)S(1)} %shard_map.88.sums_ref, f32[1,3,32,64,128]{4,3,2,1,0:T(8,128)S(1)} %copy-done, f32[1,3,32,64,128]{4,3,2,1,0:T(8,128)S(1)} %copy-done.1, ...), custom_call_target="tpu_custom_call" | custom-call | flops 35389440 | bytes 18874368 | tf_op jit(solution)/shard_map/pallas_call | solution.py:207
  (8 shorter events, 0.0 us)
Async XLA Ops:
  0.6 71.9 %collective-permute-start = (f32[1,3,32,64,128]{4,3,2,1,0:T(8,128)}, f32[1,3,32,64,128]{4,3,2,1,0:T(8,128)S(1)}, u32[]{:S(2)}, u32[]{:S(2)}) collective-permute-start(f32[1,3,32,64,128]{4,3,2,1,0:T(8,128)} %s_ref.3), channel_id=1, source_target_pairs={{8,0},{16,8},{24,16},{9,1},{17,9},{25,17},{10,2},{18,10},{26,18},{... | collective-permute-start | bytes 9437192 | tf_op jit(solution)/shard_map/ppermute | solution.py:34
  3.0 71.7 %collective-permute-start.1 = (f32[1,3,32,64,128]{4,3,2,1,0:T(8,128)}, f32[1,3,32,64,128]{4,3,2,1,0:T(8,128)S(1)}, u32[]{:S(2)}, u32[]{:S(2)}) collective-permute-start(f32[1,3,32,64,128]{4,3,2,1,0:T(8,128)} %s_ref.3), channel_id=1, source_target_pairs={{0,8},{8,16},{16,24},{1,9},{9,17},{17,25},{2,10},{10,18},{18,26},{... | collective-permute-start | bytes 9437192 | tf_op jit(solution)/shard_map/ppermute | solution.py:34
  7.7 4.1 %collective-permute-start.3 = (f32[1,3,1,64,128]{4,3,2,1,0:T(8,128)S(1)}, f32[1,3,1,64,128]{4,3,2,1,0:T(8,128)S(1)}, u32[]{:S(2)}, u32[]{:S(2)}) collective-permute-start(f32[1,3,1,64,128]{4,3,2,1,0:T(8,128)S(1)} %get-tuple-element.24), channel_id=1, source_target_pairs={{0,2},{2,4},{4,6},{6,0},{1,3},{3,5},{5,7},{7,1},{8,10},{10,12},{12... | collective-permute-start | bytes 294920 | tf_op jit(solution)/shard_map/ppermute | solution.py:23
  7.7 4.1 %collective-permute-start.2 = (f32[1,3,1,64,128]{4,3,2,1,0:T(8,128)S(1)}, f32[1,3,1,64,128]{4,3,2,1,0:T(8,128)S(1)}, u32[]{:S(2)}, u32[]{:S(2)}) collective-permute-start(f32[1,3,1,64,128]{4,3,2,1,0:T(8,128)S(1)} %get-tuple-element.23), channel_id=1, source_target_pairs={{2,0},{4,2},{6,4},{0,6},{3,1},{5,3},{7,5},{1,7},{10,8},{12,10},{14... | collective-permute-start | bytes 294920 | tf_op jit(solution)/shard_map/ppermute | solution.py:26
  11.8 10.5 %copy-start.2 = (f32[3]{0:T(128)S(1)}, f32[3]{0:T(128)}, u32[]{:S(2)}) copy-start(f32[3]{0:T(128)} %constant.6.clone) | copy-start | bytes 40
  20.2 4.2 %collective-permute-start.4 = (f32[1,3,34,1,128]{4,3,2,1,0:T(1,128)S(1)}, f32[1,3,34,1,128]{4,3,2,1,0:T(1,128)S(1)}, u32[]{:S(2)}, u32[]{:S(2)}) collective-permute-start(f32[1,3,34,1,128]{4,3,2,1,0:T(1,128)S(1)} %get-tuple-element.16), channel_id=1, source_target_pairs={{1,0},{0,1},{3,2},{2,3},{5,4},{4,5},{7,6},{6,7},{9,8},{8,9},{11,10... | collective-permute-start | bytes 156680 | tf_op jit(solution)/shard_map/ppermute | solution.py:26
  21.8 4.1 %collective-permute-start.5 = (f32[1,3,34,1,128]{4,3,2,1,0:T(1,128)S(1)}, f32[1,3,34,1,128]{4,3,2,1,0:T(1,128)S(1)}, u32[]{:S(2)}, u32[]{:S(2)}) collective-permute-start(f32[1,3,34,1,128]{4,3,2,1,0:T(1,128)S(1)} %get-tuple-element.15), channel_id=1, source_target_pairs={{0,1},{1,0},{2,3},{3,2},{4,5},{5,4},{6,7},{7,6},{8,9},{9,8},{10,11... | collective-permute-start | bytes 156680 | tf_op jit(solution)/shard_map/ppermute | solution.py:23
  26.7 1.9 %copy-start = (f32[1,3,32,64,128]{4,3,2,1,0:T(8,128)S(1)}, f32[1,3,32,64,128]{4,3,2,1,0:T(8,128)}, u32[]{:S(2)}) copy-start(f32[1,3,32,64,128]{4,3,2,1,0:T(8,128)} %s_ref.3) | copy-start | bytes 9437188
  32.7 42.0 %copy-start.1 = (f32[1,3,32,64,128]{4,3,2,1,0:T(8,128)S(1)}, f32[1,3,32,64,128]{4,3,2,1,0:T(8,128)}, u32[]{:S(2)}) copy-start(f32[1,3,32,64,128]{4,3,2,1,0:T(8,128)} %v_ref.3) | copy-start | bytes 9437188
  77.4 3.7 %collective-permute-start.6 = (f32[1,8,128]{2,1,0:T(8,128)S(1)}, f32[1,8,128]{2,1,0:T(8,128)S(1)}, u32[]{:S(2)}, u32[]{:S(2)}) collective-permute-start(f32[1,8,128]{2,1,0:T(8,128)S(1)} %get-tuple-element.8.a_ref), channel_id=1, source_target_pairs={{0,1},{1,0},{2,3},{3,2},{4,5},{5,4},{6,7},{7,6},{8,9},{9,8},{10,11... | collective-permute-start | bytes 12296 | tf_op jit(solution)/shard_map/ppermute | solution.py:61
  81.0 1.2 %collective-permute-start.7 = (f32[1,8,128]{2,1,0:T(8,128)S(1)}, f32[1,8,128]{2,1,0:T(8,128)S(1)}, u32[]{:S(2)}, u32[]{:S(2)}) collective-permute-start(f32[1,8,128]{2,1,0:T(8,128)S(1)} %shard_map.86.a_ref), channel_id=1, source_target_pairs={{0,2},{2,0},{4,6},{6,4},{1,3},{3,1},{5,7},{7,5},{8,10},{10,8},{12,... | collective-permute-start | bytes 12296 | tf_op jit(solution)/shard_map/ppermute | solution.py:61
  82.2 3.6 %collective-permute-start.8 = (f32[1,8,128]{2,1,0:T(8,128)S(1)}, f32[1,8,128]{2,1,0:T(8,128)S(1)}, u32[]{:S(2)}, u32[]{:S(2)}) collective-permute-start(f32[1,8,128]{2,1,0:T(8,128)S(1)} %shard_map.87.a_ref), channel_id=1, source_target_pairs={{0,4},{2,6},{4,0},{6,2},{1,5},{3,7},{5,1},{7,3},{8,12},{10,14},{12... | collective-permute-start | bytes 12296 | tf_op jit(solution)/shard_map/ppermute | solution.py:61

commit v6 on v5

--- a/solution.py
+++ b/solution.py
@@ -162,10 +162,10 @@
     gain = jnp.maximum(vf, 0.0) / jnp.maximum(ff, 1.0)
     nv = [gain * f[c] + TIME_STEP * f[c] for c in range(3)]
     moved = [s_ref[image, c, here] + TIME_STEP * nv[c] for c in range(3)]
-    length = jnp.sqrt(moved[0] * moved[0] + moved[1] * moved[1] + moved[2] * moved[2])
+    inverse = lax.rsqrt(moved[0] * moved[0] + moved[1] * moved[1] + moved[2] * moved[2])
     for c in range(3):
         nv_ref[0, c] = nv[c]
-        ns_ref[0, c] = moved[c] / length
+        ns_ref[0, c] = moved[c] * inverse
 
 
 def per_device(spins, velocity, upwind, climber, coupling):

time: 92 us -> 91.9 us (level)
  transfers between devices with their start and end apart: 9 -> 9, of which waited for: 8 -> 8; matrix products, arithmetic and copies ran while one was open for 19% -> 20% of each run, Pallas kernels for 0% -> 0%
where the time goes in v6:
time: 91.9 us; the launch traced here: 91.1 us
  waiting for transfers between devices  49.1 us (53%)
  other arithmetic  15.4 us (17%)
  starting transfers between devices  13 us (14%)
  Pallas kernels  7.99 us (9%)
  local copies, waits for them, and re-layouts  3.58 us (4%)
  between operations  2.06 us (2%)
    ppermute x2, waiting for transfers between devices, from_behind(): return lax.ppermute(value, axis, pairs)  41.1 us
    sub x1, other arithmetic, lattice_field(): diff_z = plus_z - minus_z  8.29 us
    ppermute x2, starting transfers between devices, from_behind(): return lax.ppermute(value, axis, pairs)  6.04 us
    pallas_call x1, Pallas kernels, per_device(): pl.pallas_call(functools.partial(update_kernel, root_cells, rows, total -...  5.29 us
    ppermute x3, waiting for transfers between devices, group_sum(): value = small_add(value, lax.ppermute(value, axis, pairs))  4.71 us
    reduce_sum x1, other arithmetic, cell_dot(): return jnp.sum(left * right, axis=1, keepdims=True)  4.08 us
    ppermute x2, starting transfers between devices, extended(): lax.ppermute(lax.slice_in_dim(block, 0, width, axis=dim), axis, backward)  3.32 us
    ppermute x3, starting transfers between devices, group_sum(): value = small_add(value, lax.ppermute(value, axis, pairs))  3.08 us
  transfers between devices with their start and end apart: 9, of which 8 were waited for; matrix products, arithmetic and copies ran while one was open for 20% of the time, Pallas kernels for 0%

profile of v6, /device:TPU:16, one launch (start us, length us, event | category | flops | bytes accessed | tf_op | source)
XLA Modules:
  0.0 91.1 jit_solution(1484556177983579807)
XLA Ops:
  0.6 2.4 %collective-permute-start = (f32[1,3,32,64,128]{4,3,2,1,0:T(8,128)}, f32[1,3,32,64,128]{4,3,2,1,0:T(8,128)S(1)}, u32[]{:S(2)}, u32[]{:S(2)}) collective-permute-start(f32[1,3,32,64,128]{4,3,2,1,0:T(8,128)} %s_ref.3), channel_id=1, source_target_pairs={{8,0},{16,8},{24,16},{9,1},{17,9},{25,17},{10,2},{18,10},{26,18},{... | collective-permute-start | bytes 9437192 | tf_op jit(solution)/shard_map/ppermute | solution.py:34
  3.0 3.7 %collective-permute-start.1 = (f32[1,3,32,64,128]{4,3,2,1,0:T(8,128)}, f32[1,3,32,64,128]{4,3,2,1,0:T(8,128)S(1)}, u32[]{:S(2)}, u32[]{:S(2)}) collective-permute-start(f32[1,3,32,64,128]{4,3,2,1,0:T(8,128)} %s_ref.3), channel_id=1, source_target_pairs={{0,8},{8,16},{16,24},{1,9},{9,17},{17,25},{2,10},{10,18},{18,26},{... | collective-permute-start | bytes 9437192 | tf_op jit(solution)/shard_map/ppermute | solution.py:34
  6.7 1.0 %fusion.7 = (f32[1,3,1,64,128]{4,3,2,1,0:T(8,128)S(1)}, f32[1,3,1,64,128]{4,3,2,1,0:T(8,128)S(1)}) fusion(f32[1,3,32,64,128]{4,3,2,1,0:T(8,128)} %s_ref.3), kind=kLoop, calls=%fused_computation.22 | loop fusion | bytes 393216 | tf_op jit(solution)/shard_map/slice | solution.py:26
  7.7 0.1 collective-permute-start.3
  7.7 1.7 %collective-permute-start.2 = (f32[1,3,1,64,128]{4,3,2,1,0:T(8,128)S(1)}, f32[1,3,1,64,128]{4,3,2,1,0:T(8,128)S(1)}, u32[]{:S(2)}, u32[]{:S(2)}) collective-permute-start(f32[1,3,1,64,128]{4,3,2,1,0:T(8,128)S(1)} %get-tuple-element.23), channel_id=1, source_target_pairs={{2,0},{4,2},{6,4},{0,6},{3,1},{5,3},{7,5},{1,7},{10,8},{12,10},{14... | collective-permute-start | bytes 294920 | tf_op jit(solution)/shard_map/ppermute | solution.py:26
  9.5 1.4 %fusion.8 = (f32[1]{0:T(128)}, f32[1]{0:T(128)}, f32[1]{0:T(128)}) fusion(f32[3]{0:T(128)} %param.10), kind=kLoop, calls=%fused_computation.23 | loop fusion | bytes 24 | tf_op jit(solution)/shard_map/slice | solution.py:87
  10.8 0.9 %collective-permute-done.3 = f32[1,3,1,64,128]{4,3,2,1,0:T(8,128)S(1)} collective-permute-done((f32[1,3,1,64,128]{4,3,2,1,0:T(8,128)S(1)}, f32[1,3,1,64,128]{4,3,2,1,0:T(8,128)S(1)}, u32[]{:S(2)}, u32[]{:S(2)}) %collective-permute-start.3) | collective-permute-done | bytes 98336 | tf_op jit(solution)/shard_map/ppermute | solution.py:23
  11.8 0.0 copy-start.2
  11.8 0.0 collective-permute-done.2
  11.8 8.3 %fusion.2 = (f32[1,3,32,64,128]{4,3,2,1,0:T(8,128)S(1)}, f32[1,3,34,64,128]{4,3,2,1,0:T(8,128)S(1)}, f32[1,3,32,64,128]{4,3,2,1,0:T(8,128)S(1)}) fusion(f32[1,3,32,64,128]{4,3,2,1,0:T(8,128)} %s_ref.3, f32[1,3,34,64,128]{4,3,2,1,0:T(8,128)S(1)} %constant_dynamic-update-slice_fusion.2, f32[1,3,1,64,128]{4,3,2,1,0:T(8,128)S(1)} %collective-permute-done.3, ...), kind=kLoop, calls=%fused_computation.11 | loop fusion | flops 3145728 | bytes 12779520 | tf_op jit(solution)/shard_map/sub | solution.py:81
  20.1 0.1 fusion.6
  20.2 1.6 %collective-permute-start.4 = (f32[1,3,34,1,128]{4,3,2,1,0:T(1,128)S(1)}, f32[1,3,34,1,128]{4,3,2,1,0:T(1,128)S(1)}, u32[]{:S(2)}, u32[]{:S(2)}) collective-permute-start(f32[1,3,34,1,128]{4,3,2,1,0:T(1,128)S(1)} %get-tuple-element.16), channel_id=1, source_target_pairs={{1,0},{0,1},{3,2},{2,3},{5,4},{4,5},{7,6},{6,7},{9,8},{8,9},{11,10... | collective-permute-start | bytes 156680 | tf_op jit(solution)/shard_map/ppermute | solution.py:26
  21.8 0.5 collective-permute-start.5
  22.3 0.6 broadcast_multiply_fusion
  23.6 0.8 collective-permute-done.4
  24.4 1.5 %collective-permute-done.5 = f32[1,3,34,1,128]{4,3,2,1,0:T(1,128)S(1)} collective-permute-done((f32[1,3,34,1,128]{4,3,2,1,0:T(1,128)S(1)}, f32[1,3,34,1,128]{4,3,2,1,0:T(1,128)S(1)}, u32[]{:S(2)}, u32[]{:S(2)}) %collective-permute-start.5) | collective-permute-done | bytes 52256 | tf_op jit(solution)/shard_map/ppermute | solution.py:23
  25.9 0.8 fusion.4
  26.7 0.0 copy-start
  26.7 0.7 slice_subtract_fusion.2
  27.4 1.2 %copy-done = f32[1,3,32,64,128]{4,3,2,1,0:T(8,128)S(1)} copy-done((f32[1,3,32,64,128]{4,3,2,1,0:T(8,128)S(1)}, f32[1,3,32,64,128]{4,3,2,1,0:T(8,128)}, u32[]{:S(2)}) %copy-start) | copy-done | bytes 3145752
  28.6 4.1 %multiply_reduce_fusion = (f32[32,64,128]{2,1,0:T(8,128)S(1)}, f32[1,3,32,64,128]{4,3,2,1,0:T(8,128)S(1)}) fusion(f32[1,3,32,64,128]{4,3,2,1,0:T(8,128)S(1)} %copy-done, f32[3]{0:T(128)S(1)} %broadcast_multiply_fusion, f32[1,1,32,64,128]{4,3,2,1,0:T(8,128)S(1)} %get-tuple-element.18, f32[1,1,32,64,128]{4,3,2,1,0:T(8,128)S(1)} %get-tuple-element.19, ...), kind=kLoop, calls=%fused_computation.10 | loop fusion | flops 13107200 | bytes 14129172 | tf_op jit(solution)/shard_map/reduce_sum | solution.py:67
  32.7 0.0 copy-start.1
  32.7 0.8 multiply_subtract_fusion.pf_ref
  33.6 39.0 %collective-permute-done.nx_ref = f32[1,3,32,64,128]{4,3,2,1,0:T(8,128)S(1)} collective-permute-done((f32[1,3,32,64,128]{4,3,2,1,0:T(8,128)}, f32[1,3,32,64,128]{4,3,2,1,0:T(8,128)S(1)}, u32[]{:S(2)}, u32[]{:S(2)}) %collective-permute-start) | collective-permute-done | bytes 3145760 | tf_op jit(solution)/shard_map/ppermute | solution.py:34
  72.6 2.1 %collective-permute-done.1.pv_ref = f32[1,3,32,64,128]{4,3,2,1,0:T(8,128)S(1)} collective-permute-done((f32[1,3,32,64,128]{4,3,2,1,0:T(8,128)}, f32[1,3,32,64,128]{4,3,2,1,0:T(8,128)S(1)}, u32[]{:S(2)}, u32[]{:S(2)}) %collective-permute-start.1) | collective-permute-done | bytes 3145760 | tf_op jit(solution)/shard_map/ppermute | solution.py:34
  74.7 2.7 %shard_map.85 = (f32[1,3,32,64,128]{4,3,2,1,0:T(8,128)S(1)}, f32[1,8,128]{2,1,0:T(8,128)S(1)}) custom-call(s32[1]{0:T(128)S(6)} %copy.11.up_ref, f32[1,3,32,64,128]{4,3,2,1,0:T(8,128)S(1)} %copy-done, f32[1,3,32,64,128]{4,3,2,1,0:T(8,128)S(1)} %collective-permute-done.nx_ref, f32[1,3,32,64,128]{4,3,2,1,0:T(8,128)S(1)} %collective-permute-done.1.pv_ref, ...), custom_call_target="tpu_custom_call" | custom-call | flops 31457280 | bytes 15728640 | tf_op jit(solution)/shard_map/pallas_call | solution.py:195
  77.4 1.6 %collective-permute-start.6 = (f32[1,8,128]{2,1,0:T(8,128)S(1)}, f32[1,8,128]{2,1,0:T(8,128)S(1)}, u32[]{:S(2)}, u32[]{:S(2)}) collective-permute-start(f32[1,8,128]{2,1,0:T(8,128)S(1)} %get-tuple-element.8.a_ref), channel_id=1, source_target_pairs={{0,1},{1,0},{2,3},{3,2},{4,5},{5,4},{6,7},{7,6},{8,9},{9,8},{10,11... | collective-permute-start | bytes 12296 | tf_op jit(solution)/shard_map/ppermute | solution.py:61
  78.9 2.1 %collective-permute-done.6.b_ref = f32[1,8,128]{2,1,0:T(8,128)S(1)} collective-permute-done((f32[1,8,128]{2,1,0:T(8,128)S(1)}, f32[1,8,128]{2,1,0:T(8,128)S(1)}, u32[]{:S(2)}, u32[]{:S(2)}) %collective-permute-start.6) | collective-permute-done | bytes 4128 | tf_op jit(solution)/shard_map/ppermute | solution.py:61
  81.0 1.2 %collective-permute-done.7.b_ref = f32[1,8,128]{2,1,0:T(8,128)S(1)} collective-permute-done((f32[1,8,128]{2,1,0:T(8,128)S(1)}, f32[1,8,128]{2,1,0:T(8,128)S(1)}, u32[]{:S(2)}, u32[]{:S(2)}) %collective-permute-start.7) | collective-permute-done | bytes 4128 | tf_op jit(solution)/shard_map/ppermute | solution.py:61
  82.2 1.5 %collective-permute-start.8 = (f32[1,8,128]{2,1,0:T(8,128)S(1)}, f32[1,8,128]{2,1,0:T(8,128)S(1)}, u32[]{:S(2)}, u32[]{:S(2)}) collective-permute-start(f32[1,8,128]{2,1,0:T(8,128)S(1)} %shard_map.87.a_ref), channel_id=1, source_target_pairs={{0,4},{2,6},{4,0},{6,2},{1,5},{3,7},{5,1},{7,3},{8,12},{10,14},{12... | collective-permute-start | bytes 12296 | tf_op jit(solution)/shard_map/ppermute | solution.py:61
  84.4 1.5 %collective-permute-done.8.b_ref = f32[1,8,128]{2,1,0:T(8,128)S(1)} collective-permute-done((f32[1,8,128]{2,1,0:T(8,128)S(1)}, f32[1,8,128]{2,1,0:T(8,128)S(1)}, u32[]{:S(2)}, u32[]{:S(2)}) %collective-permute-start.8) | collective-permute-done | bytes 4128 | tf_op jit(solution)/shard_map/ppermute | solution.py:61
  85.8 5.3 %shard_map.89 = (f32[1,3,32,64,128]{4,3,2,1,0:T(8,128)}, f32[1,3,32,64,128]{4,3,2,1,0:T(8,128)}, f32[1,1,2]{2,1,0:T(1,128)}) custom-call(s32[1]{0:T(128)S(6)} %copy.12.climber_ref, f32[1,8,128]{2,1,0:T(8,128)S(1)} %shard_map.88.sums_ref, f32[1,3,32,64,128]{4,3,2,1,0:T(8,128)S(1)} %copy-done, f32[1,3,32,64,128]{4,3,2,1,0:T(8,128)S(1)} %copy-done.1, ...), custom_call_target="tpu_custom_call" | custom-call | flops 35389440 | bytes 18874368 | tf_op jit(solution)/shard_map/pallas_call | solution.py:207
  (8 shorter events, 0.0 us)
Async XLA Ops:
  0.6 71.9 %collective-permute-start = (f32[1,3,32,64,128]{4,3,2,1,0:T(8,128)}, f32[1,3,32,64,128]{4,3,2,1,0:T(8,128)S(1)}, u32[]{:S(2)}, u32[]{:S(2)}) collective-permute-start(f32[1,3,32,64,128]{4,3,2,1,0:T(8,128)} %s_ref.3), channel_id=1, source_target_pairs={{8,0},{16,8},{24,16},{9,1},{17,9},{25,17},{10,2},{18,10},{26,18},{... | collective-permute-start | bytes 9437192 | tf_op jit(solution)/shard_map/ppermute | solution.py:34
  3.0 71.7 %collective-permute-start.1 = (f32[1,3,32,64,128]{4,3,2,1,0:T(8,128)}, f32[1,3,32,64,128]{4,3,2,1,0:T(8,128)S(1)}, u32[]{:S(2)}, u32[]{:S(2)}) collective-permute-start(f32[1,3,32,64,128]{4,3,2,1,0:T(8,128)} %s_ref.3), channel_id=1, source_target_pairs={{0,8},{8,16},{16,24},{1,9},{9,17},{17,25},{2,10},{10,18},{18,26},{... | collective-permute-start | bytes 9437192 | tf_op jit(solution)/shard_map/ppermute | solution.py:34
  7.7 4.1 %collective-permute-start.3 = (f32[1,3,1,64,128]{4,3,2,1,0:T(8,128)S(1)}, f32[1,3,1,64,128]{4,3,2,1,0:T(8,128)S(1)}, u32[]{:S(2)}, u32[]{:S(2)}) collective-permute-start(f32[1,3,1,64,128]{4,3,2,1,0:T(8,128)S(1)} %get-tuple-element.24), channel_id=1, source_target_pairs={{0,2},{2,4},{4,6},{6,0},{1,3},{3,5},{5,7},{7,1},{8,10},{10,12},{12... | collective-permute-start | bytes 294920 | tf_op jit(solution)/shard_map/ppermute | solution.py:23
  7.7 4.1 %collective-permute-start.2 = (f32[1,3,1,64,128]{4,3,2,1,0:T(8,128)S(1)}, f32[1,3,1,64,128]{4,3,2,1,0:T(8,128)S(1)}, u32[]{:S(2)}, u32[]{:S(2)}) collective-permute-start(f32[1,3,1,64,128]{4,3,2,1,0:T(8,128)S(1)} %get-tuple-element.23), channel_id=1, source_target_pairs={{2,0},{4,2},{6,4},{0,6},{3,1},{5,3},{7,5},{1,7},{10,8},{12,10},{14... | collective-permute-start | bytes 294920 | tf_op jit(solution)/shard_map/ppermute | solution.py:26
  11.8 10.5 %copy-start.2 = (f32[3]{0:T(128)S(1)}, f32[3]{0:T(128)}, u32[]{:S(2)}) copy-start(f32[3]{0:T(128)} %constant.6.clone) | copy-start | bytes 40
  20.2 4.2 %collective-permute-start.4 = (f32[1,3,34,1,128]{4,3,2,1,0:T(1,128)S(1)}, f32[1,3,34,1,128]{4,3,2,1,0:T(1,128)S(1)}, u32[]{:S(2)}, u32[]{:S(2)}) collective-permute-start(f32[1,3,34,1,128]{4,3,2,1,0:T(1,128)S(1)} %get-tuple-element.16), channel_id=1, source_target_pairs={{1,0},{0,1},{3,2},{2,3},{5,4},{4,5},{7,6},{6,7},{9,8},{8,9},{11,10... | collective-permute-start | bytes 156680 | tf_op jit(solution)/shard_map/ppermute | solution.py:26
  21.8 4.1 %collective-permute-start.5 = (f32[1,3,34,1,128]{4,3,2,1,0:T(1,128)S(1)}, f32[1,3,34,1,128]{4,3,2,1,0:T(1,128)S(1)}, u32[]{:S(2)}, u32[]{:S(2)}) collective-permute-start(f32[1,3,34,1,128]{4,3,2,1,0:T(1,128)S(1)} %get-tuple-element.15), channel_id=1, source_target_pairs={{0,1},{1,0},{2,3},{3,2},{4,5},{5,4},{6,7},{7,6},{8,9},{9,8},{10,11... | collective-permute-start | bytes 156680 | tf_op jit(solution)/shard_map/ppermute | solution.py:23
  26.7 1.9 %copy-start = (f32[1,3,32,64,128]{4,3,2,1,0:T(8,128)S(1)}, f32[1,3,32,64,128]{4,3,2,1,0:T(8,128)}, u32[]{:S(2)}) copy-start(f32[1,3,32,64,128]{4,3,2,1,0:T(8,128)} %s_ref.3) | copy-start | bytes 9437188
  32.7 42.0 %copy-start.1 = (f32[1,3,32,64,128]{4,3,2,1,0:T(8,128)S(1)}, f32[1,3,32,64,128]{4,3,2,1,0:T(8,128)}, u32[]{:S(2)}) copy-start(f32[1,3,32,64,128]{4,3,2,1,0:T(8,128)} %v_ref.3) | copy-start | bytes 9437188
  77.4 3.7 %collective-permute-start.6 = (f32[1,8,128]{2,1,0:T(8,128)S(1)}, f32[1,8,128]{2,1,0:T(8,128)S(1)}, u32[]{:S(2)}, u32[]{:S(2)}) collective-permute-start(f32[1,8,128]{2,1,0:T(8,128)S(1)} %get-tuple-element.8.a_ref), channel_id=1, source_target_pairs={{0,1},{1,0},{2,3},{3,2},{4,5},{5,4},{6,7},{7,6},{8,9},{9,8},{10,11... | collective-permute-start | bytes 12296 | tf_op jit(solution)/shard_map/ppermute | solution.py:61
  81.0 1.2 %collective-permute-start.7 = (f32[1,8,128]{2,1,0:T(8,128)S(1)}, f32[1,8,128]{2,1,0:T(8,128)S(1)}, u32[]{:S(2)}, u32[]{:S(2)}) collective-permute-start(f32[1,8,128]{2,1,0:T(8,128)S(1)} %shard_map.86.a_ref), channel_id=1, source_target_pairs={{0,2},{2,0},{4,6},{6,4},{1,3},{3,1},{5,7},{7,5},{8,10},{10,8},{12,... | collective-permute-start | bytes 12296 | tf_op jit(solution)/shard_map/ppermute | solution.py:61
  82.2 3.6 %collective-permute-start.8 = (f32[1,8,128]{2,1,0:T(8,128)S(1)}, f32[1,8,128]{2,1,0:T(8,128)S(1)}, u32[]{:S(2)}, u32[]{:S(2)}) collective-permute-start(f32[1,8,128]{2,1,0:T(8,128)S(1)} %shard_map.87.a_ref), channel_id=1, source_target_pairs={{0,4},{2,6},{4,0},{6,2},{1,5},{3,7},{5,1},{7,3},{8,12},{10,14},{12... | collective-permute-start | bytes 12296 | tf_op jit(solution)/shard_map/ppermute | solution.py:61

commit v7 on v6

--- a/solution.py
+++ b/solution.py
@@ -10,7 +10,8 @@
 TIME_STEP = 0.1
 SPRING = 2.0
 EPSILON = 1e-06
-ROWS = 4
+ROWS = 8
+ROWS_A = 8
 VMEM_LIMIT = 8 * 1024 * 1024
 
 
@@ -104,8 +105,8 @@
     ahead = jnp.where(up >= 0, 1.0, 0.0).astype(jnp.float32)
     behind = jnp.where(up <= 0, 1.0, 0.0).astype(jnp.float32)
     s = [s_ref[image, c, here] for c in range(3)]
-    fwd = [nx_ref[0, c] - s[c] for c in range(3)]
-    bwd = [s[c] - pv_ref[0, c] for c in range(3)]
+    fwd = [nx_ref[image, c, here] - s[c] for c in range(3)]
+    bwd = [s[c] - pv_ref[image, c, here] for c in range(3)]
     raw = [ahead * fwd[c] + behind * bwd[c] for c in range(3)]
     d = raw[0] * s[0] + raw[1] * s[1] + raw[2] * s[2]
     tp = [raw[c] - d * s[c] for c in range(3)]
@@ -192,10 +193,11 @@
     )
     big = jax.ShapeDtypeStruct(spins.shape, jnp.float32)
     nbytes = spins.size * 4
+    rows_a = ROWS_A if nx % ROWS_A == 0 else nx
     tangent_perp, sums = pl.pallas_call(
-        functools.partial(tangent_kernel, rows),
-        grid=grid,
-        in_specs=[smem, whole, block, block, whole, whole],
+        functools.partial(tangent_kernel, rows_a),
+        grid=(count, nx // rows_a),
+        in_specs=[smem, whole, whole, whole, whole, whole],
         out_specs=[whole, small],
         out_shape=[big, jax.ShapeDtypeStruct((count, 8, 128), jnp.float32)],
         scratch_shapes=[pltpu.VMEM((4, 8, nz), jnp.float32)],

time: 91.9 us -> 90.1 us (0.980)
  Pallas kernels: 7.99 us -> 6.19 us
    pallas_call x1, Pallas kernels: 5.29 us -> 4.01 us  [per_device(): pl.pallas_call(functools.partial(update_kernel, root_cells, rows, total -...]
where the time goes in v7:
time: 90.1 us; the launch traced here: 89.3 us
  waiting for transfers between devices  49.1 us (54%)
  other arithmetic  15.4 us (17%)
  starting transfers between devices  13 us (14%)
  Pallas kernels  6.19 us (7%)
  local copies, waits for them, and re-layouts  3.58 us (4%)
  between operations  2.06 us (2%)
    ppermute x2, waiting for transfers between devices, from_behind(): return lax.ppermute(value, axis, pairs)  41.1 us
    sub x1, other arithmetic, lattice_field(): diff_z = plus_z - minus_z  8.29 us
    ppermute x2, starting transfers between devices, from_behind(): return lax.ppermute(value, axis, pairs)  6.04 us
    ppermute x3, waiting for transfers between devices, group_sum(): value = small_add(value, lax.ppermute(value, axis, pairs))  4.71 us
    reduce_sum x1, other arithmetic, cell_dot(): return jnp.sum(left * right, axis=1, keepdims=True)  4.08 us
    pallas_call x1, Pallas kernels, per_device(): pl.pallas_call(functools.partial(update_kernel, root_cells, rows, total -...  4.01 us
    ppermute x2, starting transfers between devices, extended(): lax.ppermute(lax.slice_in_dim(block, 0, width, axis=dim), axis, backward)  3.32 us
    ppermute x3, starting transfers between devices, group_sum(): value = small_add(value, lax.ppermute(value, axis, pairs))  3.08 us
  transfers between devices with their start and end apart: 9, of which 8 were waited for; matrix products, arithmetic and copies ran while one was open for 20% of the time, Pallas kernels for 0%

profile of v7, /device:TPU:16, one launch (start us, length us, event | category | flops | bytes accessed | tf_op | source)
XLA Modules:
  0.0 89.3 jit_solution(11411319360210491030)
XLA Ops:
  0.6 2.4 %collective-permute-start = (f32[1,3,32,64,128]{4,3,2,1,0:T(8,128)}, f32[1,3,32,64,128]{4,3,2,1,0:T(8,128)S(1)}, u32[]{:S(2)}, u32[]{:S(2)}) collective-permute-start(f32[1,3,32,64,128]{4,3,2,1,0:T(8,128)} %s_ref.3), channel_id=1, source_target_pairs={{8,0},{16,8},{24,16},{9,1},{17,9},{25,17},{10,2},{18,10},{26,18},{... | collective-permute-start | bytes 9437192 | tf_op jit(solution)/shard_map/ppermute | solution.py:35
  3.0 3.7 %collective-permute-start.1 = (f32[1,3,32,64,128]{4,3,2,1,0:T(8,128)}, f32[1,3,32,64,128]{4,3,2,1,0:T(8,128)S(1)}, u32[]{:S(2)}, u32[]{:S(2)}) collective-permute-start(f32[1,3,32,64,128]{4,3,2,1,0:T(8,128)} %s_ref.3), channel_id=1, source_target_pairs={{0,8},{8,16},{16,24},{1,9},{9,17},{17,25},{2,10},{10,18},{18,26},{... | collective-permute-start | bytes 9437192 | tf_op jit(solution)/shard_map/ppermute | solution.py:35
  6.7 1.0 %fusion.7 = (f32[1,3,1,64,128]{4,3,2,1,0:T(8,128)S(1)}, f32[1,3,1,64,128]{4,3,2,1,0:T(8,128)S(1)}) fusion(f32[1,3,32,64,128]{4,3,2,1,0:T(8,128)} %s_ref.3), kind=kLoop, calls=%fused_computation.22 | loop fusion | bytes 393216 | tf_op jit(solution)/shard_map/slice | solution.py:27
  7.7 0.1 collective-permute-start.3
  7.7 1.7 %collective-permute-start.2 = (f32[1,3,1,64,128]{4,3,2,1,0:T(8,128)S(1)}, f32[1,3,1,64,128]{4,3,2,1,0:T(8,128)S(1)}, u32[]{:S(2)}, u32[]{:S(2)}) collective-permute-start(f32[1,3,1,64,128]{4,3,2,1,0:T(8,128)S(1)} %get-tuple-element.23), channel_id=1, source_target_pairs={{2,0},{4,2},{6,4},{0,6},{3,1},{5,3},{7,5},{1,7},{10,8},{12,10},{14... | collective-permute-start | bytes 294920 | tf_op jit(solution)/shard_map/ppermute | solution.py:27
  9.5 1.4 %fusion.8 = (f32[1]{0:T(128)}, f32[1]{0:T(128)}, f32[1]{0:T(128)}) fusion(f32[3]{0:T(128)} %param.10), kind=kLoop, calls=%fused_computation.23 | loop fusion | bytes 24 | tf_op jit(solution)/shard_map/slice | solution.py:88
  10.8 0.9 %collective-permute-done.3 = f32[1,3,1,64,128]{4,3,2,1,0:T(8,128)S(1)} collective-permute-done((f32[1,3,1,64,128]{4,3,2,1,0:T(8,128)S(1)}, f32[1,3,1,64,128]{4,3,2,1,0:T(8,128)S(1)}, u32[]{:S(2)}, u32[]{:S(2)}) %collective-permute-start.3) | collective-permute-done | bytes 98336 | tf_op jit(solution)/shard_map/ppermute | solution.py:24
  11.8 0.0 copy-start.2
  11.8 0.0 collective-permute-done.2
  11.8 8.3 %fusion.2 = (f32[1,3,32,64,128]{4,3,2,1,0:T(8,128)S(1)}, f32[1,3,34,64,128]{4,3,2,1,0:T(8,128)S(1)}, f32[1,3,32,64,128]{4,3,2,1,0:T(8,128)S(1)}) fusion(f32[1,3,32,64,128]{4,3,2,1,0:T(8,128)} %s_ref.3, f32[1,3,34,64,128]{4,3,2,1,0:T(8,128)S(1)} %constant_dynamic-update-slice_fusion.2, f32[1,3,1,64,128]{4,3,2,1,0:T(8,128)S(1)} %collective-permute-done.3, ...), kind=kLoop, calls=%fused_computation.11 | loop fusion | flops 3145728 | bytes 12779520 | tf_op jit(solution)/shard_map/sub | solution.py:82
  20.1 0.1 fusion.6
  20.2 1.6 %collective-permute-start.4 = (f32[1,3,34,1,128]{4,3,2,1,0:T(1,128)S(1)}, f32[1,3,34,1,128]{4,3,2,1,0:T(1,128)S(1)}, u32[]{:S(2)}, u32[]{:S(2)}) collective-permute-start(f32[1,3,34,1,128]{4,3,2,1,0:T(1,128)S(1)} %get-tuple-element.16), channel_id=1, source_target_pairs={{1,0},{0,1},{3,2},{2,3},{5,4},{4,5},{7,6},{6,7},{9,8},{8,9},{11,10... | collective-permute-start | bytes 156680 | tf_op jit(solution)/shard_map/ppermute | solution.py:27
  21.8 0.5 collective-permute-start.5
  22.3 0.6 broadcast_multiply_fusion
  23.6 0.8 collective-permute-done.4
  24.4 1.5 %collective-permute-done.5 = f32[1,3,34,1,128]{4,3,2,1,0:T(1,128)S(1)} collective-permute-done((f32[1,3,34,1,128]{4,3,2,1,0:T(1,128)S(1)}, f32[1,3,34,1,128]{4,3,2,1,0:T(1,128)S(1)}, u32[]{:S(2)}, u32[]{:S(2)}) %collective-permute-start.5) | collective-permute-done | bytes 52256 | tf_op jit(solution)/shard_map/ppermute | solution.py:24
  25.9 0.8 fusion.4
  26.7 0.0 copy-start
  26.7 0.7 slice_subtract_fusion.2
  27.4 1.2 %copy-done = f32[1,3,32,64,128]{4,3,2,1,0:T(8,128)S(1)} copy-done((f32[1,3,32,64,128]{4,3,2,1,0:T(8,128)S(1)}, f32[1,3,32,64,128]{4,3,2,1,0:T(8,128)}, u32[]{:S(2)}) %copy-start) | copy-done | bytes 3145752
  28.6 4.1 %multiply_reduce_fusion = (f32[32,64,128]{2,1,0:T(8,128)S(1)}, f32[1,3,32,64,128]{4,3,2,1,0:T(8,128)S(1)}) fusion(f32[1,3,32,64,128]{4,3,2,1,0:T(8,128)S(1)} %copy-done, f32[3]{0:T(128)S(1)} %broadcast_multiply_fusion, f32[1,1,32,64,128]{4,3,2,1,0:T(8,128)S(1)} %get-tuple-element.18, f32[1,1,32,64,128]{4,3,2,1,0:T(8,128)S(1)} %get-tuple-element.19, ...), kind=kLoop, calls=%fused_computation.10 | loop fusion | flops 13107200 | bytes 14129172 | tf_op jit(solution)/shard_map/reduce_sum | solution.py:68
  32.7 0.0 copy-start.1
  32.7 0.8 multiply_subtract_fusion.pf_ref
  33.6 39.0 %collective-permute-done.nx_ref = f32[1,3,32,64,128]{4,3,2,1,0:T(8,128)S(1)} collective-permute-done((f32[1,3,32,64,128]{4,3,2,1,0:T(8,128)}, f32[1,3,32,64,128]{4,3,2,1,0:T(8,128)S(1)}, u32[]{:S(2)}, u32[]{:S(2)}) %collective-permute-start) | collective-permute-done | bytes 3145760 | tf_op jit(solution)/shard_map/ppermute | solution.py:35
  72.6 2.1 %collective-permute-done.1.pv_ref = f32[1,3,32,64,128]{4,3,2,1,0:T(8,128)S(1)} collective-permute-done((f32[1,3,32,64,128]{4,3,2,1,0:T(8,128)}, f32[1,3,32,64,128]{4,3,2,1,0:T(8,128)S(1)}, u32[]{:S(2)}, u32[]{:S(2)}) %collective-permute-start.1) | collective-permute-done | bytes 3145760 | tf_op jit(solution)/shard_map/ppermute | solution.py:35
  74.7 2.2 %shard_map.85 = (f32[1,3,32,64,128]{4,3,2,1,0:T(8,128)S(1)}, f32[1,8,128]{2,1,0:T(8,128)S(1)}) custom-call(s32[1]{0:T(128)S(6)} %copy.11.up_ref, f32[1,3,32,64,128]{4,3,2,1,0:T(8,128)S(1)} %copy-done, f32[1,3,32,64,128]{4,3,2,1,0:T(8,128)S(1)} %collective-permute-done.nx_ref, f32[1,3,32,64,128]{4,3,2,1,0:T(8,128)S(1)} %collective-permute-done.1.pv_ref, ...), custom_call_target="tpu_custom_call" | custom-call | flops 31457280 | bytes 15728640 | tf_op jit(solution)/shard_map/pallas_call | solution.py:197
  76.8 1.6 %collective-permute-start.6 = (f32[1,8,128]{2,1,0:T(8,128)S(1)}, f32[1,8,128]{2,1,0:T(8,128)S(1)}, u32[]{:S(2)}, u32[]{:S(2)}) collective-permute-start(f32[1,8,128]{2,1,0:T(8,128)S(1)} %get-tuple-element.8.a_ref), channel_id=1, source_target_pairs={{0,1},{1,0},{2,3},{3,2},{4,5},{5,4},{6,7},{7,6},{8,9},{9,8},{10,11... | collective-permute-start | bytes 12296 | tf_op jit(solution)/shard_map/ppermute | solution.py:62
  78.4 2.1 %collective-permute-done.6.b_ref = f32[1,8,128]{2,1,0:T(8,128)S(1)} collective-permute-done((f32[1,8,128]{2,1,0:T(8,128)S(1)}, f32[1,8,128]{2,1,0:T(8,128)S(1)}, u32[]{:S(2)}, u32[]{:S(2)}) %collective-permute-start.6) | collective-permute-done | bytes 4128 | tf_op jit(solution)/shard_map/ppermute | solution.py:62
  80.5 1.2 %collective-permute-done.7.b_ref = f32[1,8,128]{2,1,0:T(8,128)S(1)} collective-permute-done((f32[1,8,128]{2,1,0:T(8,128)S(1)}, f32[1,8,128]{2,1,0:T(8,128)S(1)}, u32[]{:S(2)}, u32[]{:S(2)}) %collective-permute-start.7) | collective-permute-done | bytes 4128 | tf_op jit(solution)/shard_map/ppermute | solution.py:62
  81.7 1.5 %collective-permute-start.8 = (f32[1,8,128]{2,1,0:T(8,128)S(1)}, f32[1,8,128]{2,1,0:T(8,128)S(1)}, u32[]{:S(2)}, u32[]{:S(2)}) collective-permute-start(f32[1,8,128]{2,1,0:T(8,128)S(1)} %shard_map.87.a_ref), channel_id=1, source_target_pairs={{0,4},{2,6},{4,0},{6,2},{1,5},{3,7},{5,1},{7,3},{8,12},{10,14},{12... | collective-permute-start | bytes 12296 | tf_op jit(solution)/shard_map/ppermute | solution.py:62
  83.8 1.5 %collective-permute-done.8.b_ref = f32[1,8,128]{2,1,0:T(8,128)S(1)} collective-permute-done((f32[1,8,128]{2,1,0:T(8,128)S(1)}, f32[1,8,128]{2,1,0:T(8,128)S(1)}, u32[]{:S(2)}, u32[]{:S(2)}) %collective-permute-start.8) | collective-permute-done | bytes 4128 | tf_op jit(solution)/shard_map/ppermute | solution.py:62
  85.3 4.0 %shard_map.89 = (f32[1,3,32,64,128]{4,3,2,1,0:T(8,128)}, f32[1,3,32,64,128]{4,3,2,1,0:T(8,128)}, f32[1,1,2]{2,1,0:T(1,128)}) custom-call(s32[1]{0:T(128)S(6)} %copy.12.climber_ref, f32[1,8,128]{2,1,0:T(8,128)S(1)} %shard_map.88.sums_ref, f32[1,3,32,64,128]{4,3,2,1,0:T(8,128)S(1)} %copy-done, f32[1,3,32,64,128]{4,3,2,1,0:T(8,128)S(1)} %copy-done.1, ...), custom_call_target="tpu_custom_call" | custom-call | flops 35389440 | bytes 18874368 | tf_op jit(solution)/shard_map/pallas_call | solution.py:209
  (8 shorter events, 0.0 us)
Async XLA Ops:
  0.6 71.9 %collective-permute-start = (f32[1,3,32,64,128]{4,3,2,1,0:T(8,128)}, f32[1,3,32,64,128]{4,3,2,1,0:T(8,128)S(1)}, u32[]{:S(2)}, u32[]{:S(2)}) collective-permute-start(f32[1,3,32,64,128]{4,3,2,1,0:T(8,128)} %s_ref.3), channel_id=1, source_target_pairs={{8,0},{16,8},{24,16},{9,1},{17,9},{25,17},{10,2},{18,10},{26,18},{... | collective-permute-start | bytes 9437192 | tf_op jit(solution)/shard_map/ppermute | solution.py:35
  3.0 71.7 %collective-permute-start.1 = (f32[1,3,32,64,128]{4,3,2,1,0:T(8,128)}, f32[1,3,32,64,128]{4,3,2,1,0:T(8,128)S(1)}, u32[]{:S(2)}, u32[]{:S(2)}) collective-permute-start(f32[1,3,32,64,128]{4,3,2,1,0:T(8,128)} %s_ref.3), channel_id=1, source_target_pairs={{0,8},{8,16},{16,24},{1,9},{9,17},{17,25},{2,10},{10,18},{18,26},{... | collective-permute-start | bytes 9437192 | tf_op jit(solution)/shard_map/ppermute | solution.py:35
  7.7 4.1 %collective-permute-start.3 = (f32[1,3,1,64,128]{4,3,2,1,0:T(8,128)S(1)}, f32[1,3,1,64,128]{4,3,2,1,0:T(8,128)S(1)}, u32[]{:S(2)}, u32[]{:S(2)}) collective-permute-start(f32[1,3,1,64,128]{4,3,2,1,0:T(8,128)S(1)} %get-tuple-element.24), channel_id=1, source_target_pairs={{0,2},{2,4},{4,6},{6,0},{1,3},{3,5},{5,7},{7,1},{8,10},{10,12},{12... | collective-permute-start | bytes 294920 | tf_op jit(solution)/shard_map/ppermute | solution.py:24
  7.7 4.1 %collective-permute-start.2 = (f32[1,3,1,64,128]{4,3,2,1,0:T(8,128)S(1)}, f32[1,3,1,64,128]{4,3,2,1,0:T(8,128)S(1)}, u32[]{:S(2)}, u32[]{:S(2)}) collective-permute-start(f32[1,3,1,64,128]{4,3,2,1,0:T(8,128)S(1)} %get-tuple-element.23), channel_id=1, source_target_pairs={{2,0},{4,2},{6,4},{0,6},{3,1},{5,3},{7,5},{1,7},{10,8},{12,10},{14... | collective-permute-start | bytes 294920 | tf_op jit(solution)/shard_map/ppermute | solution.py:27
  11.8 10.5 %copy-start.2 = (f32[3]{0:T(128)S(1)}, f32[3]{0:T(128)}, u32[]{:S(2)}) copy-start(f32[3]{0:T(128)} %constant.6.clone) | copy-start | bytes 40
  20.2 4.2 %collective-permute-start.4 = (f32[1,3,34,1,128]{4,3,2,1,0:T(1,128)S(1)}, f32[1,3,34,1,128]{4,3,2,1,0:T(1,128)S(1)}, u32[]{:S(2)}, u32[]{:S(2)}) collective-permute-start(f32[1,3,34,1,128]{4,3,2,1,0:T(1,128)S(1)} %get-tuple-element.16), channel_id=1, source_target_pairs={{1,0},{0,1},{3,2},{2,3},{5,4},{4,5},{7,6},{6,7},{9,8},{8,9},{11,10... | collective-permute-start | bytes 156680 | tf_op jit(solution)/shard_map/ppermute | solution.py:27
  21.8 4.1 %collective-permute-start.5 = (f32[1,3,34,1,128]{4,3,2,1,0:T(1,128)S(1)}, f32[1,3,34,1,128]{4,3,2,1,0:T(1,128)S(1)}, u32[]{:S(2)}, u32[]{:S(2)}) collective-permute-start(f32[1,3,34,1,128]{4,3,2,1,0:T(1,128)S(1)} %get-tuple-element.15), channel_id=1, source_target_pairs={{0,1},{1,0},{2,3},{3,2},{4,5},{5,4},{6,7},{7,6},{8,9},{9,8},{10,11... | collective-permute-start | bytes 156680 | tf_op jit(solution)/shard_map/ppermute | solution.py:24
  26.7 1.9 %copy-start = (f32[1,3,32,64,128]{4,3,2,1,0:T(8,128)S(1)}, f32[1,3,32,64,128]{4,3,2,1,0:T(8,128)}, u32[]{:S(2)}) copy-start(f32[1,3,32,64,128]{4,3,2,1,0:T(8,128)} %s_ref.3) | copy-start | bytes 9437188
  32.7 42.0 %copy-start.1 = (f32[1,3,32,64,128]{4,3,2,1,0:T(8,128)S(1)}, f32[1,3,32,64,128]{4,3,2,1,0:T(8,128)}, u32[]{:S(2)}) copy-start(f32[1,3,32,64,128]{4,3,2,1,0:T(8,128)} %v_ref.3) | copy-start | bytes 9437188
  76.8 3.7 %collective-permute-start.6 = (f32[1,8,128]{2,1,0:T(8,128)S(1)}, f32[1,8,128]{2,1,0:T(8,128)S(1)}, u32[]{:S(2)}, u32[]{:S(2)}) collective-permute-start(f32[1,8,128]{2,1,0:T(8,128)S(1)} %get-tuple-element.8.a_ref), channel_id=1, source_target_pairs={{0,1},{1,0},{2,3},{3,2},{4,5},{5,4},{6,7},{7,6},{8,9},{9,8},{10,11... | collective-permute-start | bytes 12296 | tf_op jit(solution)/shard_map/ppermute | solution.py:62
  80.5 1.2 %collective-permute-start.7 = (f32[1,8,128]{2,1,0:T(8,128)S(1)}, f32[1,8,128]{2,1,0:T(8,128)S(1)}, u32[]{:S(2)}, u32[]{:S(2)}) collective-permute-start(f32[1,8,128]{2,1,0:T(8,128)S(1)} %shard_map.86.a_ref), channel_id=1, source_target_pairs={{0,2},{2,0},{4,6},{6,4},{1,3},{3,1},{5,7},{7,5},{8,10},{10,8},{12,... | collective-permute-start | bytes 12296 | tf_op jit(solution)/shard_map/ppermute | solution.py:62
  81.7 3.6 %collective-permute-start.8 = (f32[1,8,128]{2,1,0:T(8,128)S(1)}, f32[1,8,128]{2,1,0:T(8,128)S(1)}, u32[]{:S(2)}, u32[]{:S(2)}) collective-permute-start(f32[1,8,128]{2,1,0:T(8,128)S(1)} %shard_map.87.a_ref), channel_id=1, source_target_pairs={{0,4},{2,6},{4,0},{6,2},{1,5},{3,7},{5,1},{7,3},{8,12},{10,14},{12... | collective-permute-start | bytes 12296 | tf_op jit(solution)/shard_map/ppermute | solution.py:62

commit v8 on v7

--- a/solution.py
+++ b/solution.py
@@ -92,10 +92,11 @@
     return jnp.sum(x.reshape(-1, 8, x.shape[-1]), axis=0)
 
 
-def tangent_kernel(rows, up_ref, s_ref, nx_ref, pv_ref, pf_ref, v_ref, tp_ref, sums_ref, acc_ref):
+def tangent_kernel(rows, up_ref, s_ref, first_ref, second_ref, pf_ref, v_ref, tp_ref, sums_ref, acc_ref):
     image = pl.program_id(0)
     step = pl.program_id(1)
     here = pl.ds(pl.multiple_of(step * rows, rows), rows)
+    even = jnp.full((1, 1, 1), lax.axis_index("img") % 2) == 0
 
     @pl.when(step == 0)
     def _():
@@ -105,8 +106,10 @@
     ahead = jnp.where(up >= 0, 1.0, 0.0).astype(jnp.float32)
     behind = jnp.where(up <= 0, 1.0, 0.0).astype(jnp.float32)
     s = [s_ref[image, c, here] for c in range(3)]
-    fwd = [nx_ref[image, c, here] - s[c] for c in range(3)]
-    bwd = [s[c] - pv_ref[image, c, here] for c in range(3)]
+    first = [first_ref[image, c, here] for c in range(3)]
+    second = [second_ref[image, c, here] for c in range(3)]
+    fwd = [jnp.where(even, first[c], second[c]) - s[c] for c in range(3)]
+    bwd = [s[c] - jnp.where(even, second[c], first[c]) for c in range(3)]
     raw = [ahead * fwd[c] + behind * bwd[c] for c in range(3)]
     d = raw[0] * s[0] + raw[1] * s[1] + raw[2] * s[2]
     tp = [raw[c] - d * s[c] for c in range(3)]
@@ -175,12 +178,14 @@
     cells = nx * ny * nz * lax.axis_size("gx") * lax.axis_size("gy")
     root_cells = float(cells) ** 0.5
     indices = lax.axis_index("img") * count + jnp.arange(count, dtype=jnp.int32)
-    ahead = from_behind(spins[:1], "img", -1)
-    behind = from_behind(spins[-1:], "img", 1)
+    assert count == 1
+    places = lax.axis_size("img")
+    first = lax.ppermute(spins, "img", [(i, i ^ 1) for i in range(places) if i ^ 1 < places])
+    second = lax.ppermute(
+        spins, "img", [(i, i - 1 + 2 * (i % 2)) for i in range(1, places - 1)]
+    )
     field = lattice_field(spins, coupling)
     perp_field = field - cell_dot(field, spins) * spins
-    after = jnp.concatenate([spins[1:], ahead], 0)
-    before = jnp.concatenate([behind, spins[:-1]], 0)
 
     rows = ROWS if nx % ROWS == 0 else nx
     grid = (count, nx // rows)
@@ -203,7 +208,7 @@
         scratch_shapes=[pltpu.VMEM((4, 8, nz), jnp.float32)],
         compiler_params=params,
         cost_estimate=pl.CostEstimate(flops=40 * spins.size, bytes_accessed=5 * nbytes, transcendentals=0),
-    )(upwind, spins, after, before, perp_field, velocity)
+    )(upwind, spins, first, second, perp_field, velocity)
 
     sums = group_sum(sums, ("gy", "gx"))
     new_spins, new_velocity, spacing = pl.pallas_call(

time: 90.1 us -> 89.1 us (0.989)
  starting transfers between devices: 13 us -> 10.5 us
  waiting for transfers between devices: 49.1 us -> 50.9 us
    ppermute x2, starting transfers between devices: 6.04 us -> 3.55 us  [the longest x1 1.91 us: per_device(): lax.ppermute(spins, 'img', [(i, i - 1 + 2 * (i % 2)) for i in range(1, pl...]
    ppermute x2, waiting for transfers between devices: 41.1 us -> 42.9 us  [the longest x1 39.7 us: per_device(): lax.ppermute(spins, 'img', [(i, i ^ 1) for i in range(places) if i ^ 1 <...]
where the time goes in v8:
time: 89.1 us; the launch traced here: 88.8 us
  waiting for transfers between devices  50.9 us (57%)
  other arithmetic  15.4 us (17%)
  starting transfers between devices  10.5 us (12%)
  Pallas kernels  6.45 us (7%)
  local copies, waits for them, and re-layouts  3.58 us (4%)
  between operations  2.05 us (2%)
    ppermute x1, waiting for transfers between devices, per_device(): lax.ppermute(spins, 'img', [(i, i ^ 1) for i in range(places) if i ^ 1 <...  39.7 us
    sub x1, other arithmetic, lattice_field(): diff_z = plus_z - minus_z  8.29 us
    ppermute x3, waiting for transfers between devices, group_sum(): value = small_add(value, lax.ppermute(value, axis, pairs))  4.71 us
    reduce_sum x1, other arithmetic, cell_dot(): return jnp.sum(left * right, axis=1, keepdims=True)  4.08 us
    pallas_call x1, Pallas kernels, per_device(): pl.pallas_call(functools.partial(update_kernel, root_cells, rows, total -...  4.01 us
    ppermute x2, starting transfers between devices, extended(): lax.ppermute(lax.slice_in_dim(block, 0, width, axis=dim), axis, backward)  3.32 us
    ppermute x1, waiting for transfers between devices, per_device(): lax.ppermute(spins, 'img', [(i, i - 1 + 2 * (i % 2)) for i in range(1, pl...  3.18 us
    ppermute x3, starting transfers between devices, group_sum(): value = small_add(value, lax.ppermute(value, axis, pairs))  3.08 us
  transfers between devices with their start and end apart: 9, of which 8 were waited for; matrix products, arithmetic and copies ran while one was open for 20% of the time, Pallas kernels for 0%

profile of v8, /device:TPU:16, one launch (start us, length us, event | category | flops | bytes accessed | tf_op | source)
XLA Modules:
  0.0 88.8 jit_solution(8513334702315530763)
XLA Ops:
  0.6 1.6 %collective-permute-start = (f32[1,3,32,64,128]{4,3,2,1,0:T(8,128)}, f32[1,3,32,64,128]{4,3,2,1,0:T(8,128)S(1)}, u32[]{:S(2)}, u32[]{:S(2)}) collective-permute-start(f32[1,3,32,64,128]{4,3,2,1,0:T(8,128)} %s_ref.3), channel_id=1, source_target_pairs={{0,8},{8,0},{16,24},{24,16},{1,9},{9,1},{17,25},{25,17},{2,10},{10... | collective-permute-start | bytes 9437192 | tf_op jit(solution)/shard_map/ppermute | solution.py:183
  2.3 1.9 %collective-permute-start.1 = (f32[1,3,32,64,128]{4,3,2,1,0:T(8,128)}, f32[1,3,32,64,128]{4,3,2,1,0:T(8,128)S(1)}, u32[]{:S(2)}, u32[]{:S(2)}) collective-permute-start(f32[1,3,32,64,128]{4,3,2,1,0:T(8,128)} %s_ref.3), channel_id=1, source_target_pairs={{8,16},{16,8},{9,17},{17,9},{10,18},{18,10},{11,19},{19,11},{12,20... | collective-permute-start | bytes 9437192 | tf_op jit(solution)/shard_map/ppermute | solution.py:184
  4.2 1.0 %fusion.7 = (f32[1,3,1,64,128]{4,3,2,1,0:T(8,128)S(1)}, f32[1,3,1,64,128]{4,3,2,1,0:T(8,128)S(1)}) fusion(f32[1,3,32,64,128]{4,3,2,1,0:T(8,128)} %s_ref.3), kind=kLoop, calls=%fused_computation.22 | loop fusion | bytes 393216 | tf_op jit(solution)/shard_map/slice | solution.py:27
  5.2 0.1 collective-permute-start.3
  5.2 1.7 %collective-permute-start.2 = (f32[1,3,1,64,128]{4,3,2,1,0:T(8,128)S(1)}, f32[1,3,1,64,128]{4,3,2,1,0:T(8,128)S(1)}, u32[]{:S(2)}, u32[]{:S(2)}) collective-permute-start(f32[1,3,1,64,128]{4,3,2,1,0:T(8,128)S(1)} %get-tuple-element.23), channel_id=1, source_target_pairs={{2,0},{4,2},{6,4},{0,6},{3,1},{5,3},{7,5},{1,7},{10,8},{12,10},{14... | collective-permute-start | bytes 294920 | tf_op jit(solution)/shard_map/ppermute | solution.py:27
  7.0 1.4 %fusion.8 = (f32[1]{0:T(128)}, f32[1]{0:T(128)}, f32[1]{0:T(128)}) fusion(f32[3]{0:T(128)} %param.10), kind=kLoop, calls=%fused_computation.23 | loop fusion | bytes 24 | tf_op jit(solution)/shard_map/slice | solution.py:88
  8.3 0.9 %collective-permute-done.3 = f32[1,3,1,64,128]{4,3,2,1,0:T(8,128)S(1)} collective-permute-done((f32[1,3,1,64,128]{4,3,2,1,0:T(8,128)S(1)}, f32[1,3,1,64,128]{4,3,2,1,0:T(8,128)S(1)}, u32[]{:S(2)}, u32[]{:S(2)}) %collective-permute-start.3) | collective-permute-done | bytes 98336 | tf_op jit(solution)/shard_map/ppermute | solution.py:24
  9.3 0.0 copy-start.2
  9.3 0.0 collective-permute-done.2
  9.3 8.3 %fusion.2 = (f32[1,3,32,64,128]{4,3,2,1,0:T(8,128)S(1)}, f32[1,3,34,64,128]{4,3,2,1,0:T(8,128)S(1)}, f32[1,3,32,64,128]{4,3,2,1,0:T(8,128)S(1)}) fusion(f32[1,3,32,64,128]{4,3,2,1,0:T(8,128)} %s_ref.3, f32[1,3,34,64,128]{4,3,2,1,0:T(8,128)S(1)} %constant_dynamic-update-slice_fusion.2, f32[1,3,1,64,128]{4,3,2,1,0:T(8,128)S(1)} %collective-permute-done.3, ...), kind=kLoop, calls=%fused_computation.11 | loop fusion | flops 3145728 | bytes 12779520 | tf_op jit(solution)/shard_map/sub | solution.py:82
  17.6 0.1 fusion.6
  17.7 1.6 %collective-permute-start.4 = (f32[1,3,34,1,128]{4,3,2,1,0:T(1,128)S(1)}, f32[1,3,34,1,128]{4,3,2,1,0:T(1,128)S(1)}, u32[]{:S(2)}, u32[]{:S(2)}) collective-permute-start(f32[1,3,34,1,128]{4,3,2,1,0:T(1,128)S(1)} %get-tuple-element.16), channel_id=1, source_target_pairs={{1,0},{0,1},{3,2},{2,3},{5,4},{4,5},{7,6},{6,7},{9,8},{8,9},{11,10... | collective-permute-start | bytes 156680 | tf_op jit(solution)/shard_map/ppermute | solution.py:27
  19.3 0.5 collective-permute-start.5
  19.8 0.6 broadcast_multiply_fusion
  21.1 0.8 collective-permute-done.4
  21.9 1.5 %collective-permute-done.5 = f32[1,3,34,1,128]{4,3,2,1,0:T(1,128)S(1)} collective-permute-done((f32[1,3,34,1,128]{4,3,2,1,0:T(1,128)S(1)}, f32[1,3,34,1,128]{4,3,2,1,0:T(1,128)S(1)}, u32[]{:S(2)}, u32[]{:S(2)}) %collective-permute-start.5) | collective-permute-done | bytes 52256 | tf_op jit(solution)/shard_map/ppermute | solution.py:24
  23.4 0.8 fusion.4
  24.2 0.0 copy-start
  24.2 0.7 slice_subtract_fusion.2
  24.9 1.2 %copy-done = f32[1,3,32,64,128]{4,3,2,1,0:T(8,128)S(1)} copy-done((f32[1,3,32,64,128]{4,3,2,1,0:T(8,128)S(1)}, f32[1,3,32,64,128]{4,3,2,1,0:T(8,128)}, u32[]{:S(2)}) %copy-start) | copy-done | bytes 3145752
  26.1 4.1 %multiply_reduce_fusion = (f32[32,64,128]{2,1,0:T(8,128)S(1)}, f32[1,3,32,64,128]{4,3,2,1,0:T(8,128)S(1)}) fusion(f32[1,3,32,64,128]{4,3,2,1,0:T(8,128)S(1)} %copy-done, f32[3]{0:T(128)S(1)} %broadcast_multiply_fusion, f32[1,1,32,64,128]{4,3,2,1,0:T(8,128)S(1)} %get-tuple-element.18, f32[1,1,32,64,128]{4,3,2,1,0:T(8,128)S(1)} %get-tuple-element.19, ...), kind=kLoop, calls=%fused_computation.10 | loop fusion | flops 13107200 | bytes 14129172 | tf_op jit(solution)/shard_map/reduce_sum | solution.py:68
  30.2 0.0 copy-start.1
  30.2 0.8 multiply_subtract_fusion.pf_ref
  31.1 39.7 %collective-permute-done.first_ref = f32[1,3,32,64,128]{4,3,2,1,0:T(8,128)S(1)} collective-permute-done((f32[1,3,32,64,128]{4,3,2,1,0:T(8,128)}, f32[1,3,32,64,128]{4,3,2,1,0:T(8,128)S(1)}, u32[]{:S(2)}, u32[]{:S(2)}) %collective-permute-start) | collective-permute-done | bytes 3145760 | tf_op jit(solution)/shard_map/ppermute | solution.py:183
  70.7 3.2 %collective-permute-done.1.second_ref = f32[1,3,32,64,128]{4,3,2,1,0:T(8,128)S(1)} collective-permute-done((f32[1,3,32,64,128]{4,3,2,1,0:T(8,128)}, f32[1,3,32,64,128]{4,3,2,1,0:T(8,128)S(1)}, u32[]{:S(2)}, u32[]{:S(2)}) %collective-permute-start.1) | collective-permute-done | bytes 3145760 | tf_op jit(solution)/shard_map/ppermute | solution.py:184
  73.9 2.4 %shard_map.85 = (f32[1,3,32,64,128]{4,3,2,1,0:T(8,128)S(1)}, f32[1,8,128]{2,1,0:T(8,128)S(1)}) custom-call(s32[1]{0:T(128)S(6)} %copy.11.up_ref, f32[1,3,32,64,128]{4,3,2,1,0:T(8,128)S(1)} %copy-done, f32[1,3,32,64,128]{4,3,2,1,0:T(8,128)S(1)} %collective-permute-done.first_ref, f32[1,3,32,64,128]{4,3,2,1,0:T(8,128)S(1)} %collective-permute-done.1.second_ref, ...), custom_call_target="tpu_custom_call" | custom-call | flops 31457280 | bytes 15728640 | tf_op jit(solution)/shard_map/pallas_call | solution.py:202
  76.4 1.6 %collective-permute-start.6 = (f32[1,8,128]{2,1,0:T(8,128)S(1)}, f32[1,8,128]{2,1,0:T(8,128)S(1)}, u32[]{:S(2)}, u32[]{:S(2)}) collective-permute-start(f32[1,8,128]{2,1,0:T(8,128)S(1)} %get-tuple-element.8.a_ref), channel_id=1, source_target_pairs={{0,1},{1,0},{2,3},{3,2},{4,5},{5,4},{6,7},{7,6},{8,9},{9,8},{10,11... | collective-permute-start | bytes 12296 | tf_op jit(solution)/shard_map/ppermute | solution.py:62
  78.0 2.1 %collective-permute-done.6.b_ref = f32[1,8,128]{2,1,0:T(8,128)S(1)} collective-permute-done((f32[1,8,128]{2,1,0:T(8,128)S(1)}, f32[1,8,128]{2,1,0:T(8,128)S(1)}, u32[]{:S(2)}, u32[]{:S(2)}) %collective-permute-start.6) | collective-permute-done | bytes 4128 | tf_op jit(solution)/shard_map/ppermute | solution.py:62
  80.0 1.2 %collective-permute-done.7.b_ref = f32[1,8,128]{2,1,0:T(8,128)S(1)} collective-permute-done((f32[1,8,128]{2,1,0:T(8,128)S(1)}, f32[1,8,128]{2,1,0:T(8,128)S(1)}, u32[]{:S(2)}, u32[]{:S(2)}) %collective-permute-start.7) | collective-permute-done | bytes 4128 | tf_op jit(solution)/shard_map/ppermute | solution.py:62
  81.2 1.5 %collective-permute-start.8 = (f32[1,8,128]{2,1,0:T(8,128)S(1)}, f32[1,8,128]{2,1,0:T(8,128)S(1)}, u32[]{:S(2)}, u32[]{:S(2)}) collective-permute-start(f32[1,8,128]{2,1,0:T(8,128)S(1)} %shard_map.87.a_ref), channel_id=1, source_target_pairs={{0,4},{2,6},{4,0},{6,2},{1,5},{3,7},{5,1},{7,3},{8,12},{10,14},{12... | collective-permute-start | bytes 12296 | tf_op jit(solution)/shard_map/ppermute | solution.py:62
  83.4 1.5 %collective-permute-done.8.b_ref = f32[1,8,128]{2,1,0:T(8,128)S(1)} collective-permute-done((f32[1,8,128]{2,1,0:T(8,128)S(1)}, f32[1,8,128]{2,1,0:T(8,128)S(1)}, u32[]{:S(2)}, u32[]{:S(2)}) %collective-permute-start.8) | collective-permute-done | bytes 4128 | tf_op jit(solution)/shard_map/ppermute | solution.py:62
  84.8 4.0 %shard_map.89 = (f32[1,3,32,64,128]{4,3,2,1,0:T(8,128)}, f32[1,3,32,64,128]{4,3,2,1,0:T(8,128)}, f32[1,1,2]{2,1,0:T(1,128)}) custom-call(s32[1]{0:T(128)S(6)} %copy.12.climber_ref, f32[1,8,128]{2,1,0:T(8,128)S(1)} %shard_map.88.sums_ref, f32[1,3,32,64,128]{4,3,2,1,0:T(8,128)S(1)} %copy-done, f32[1,3,32,64,128]{4,3,2,1,0:T(8,128)S(1)} %copy-done.1, ...), custom_call_target="tpu_custom_call" | custom-call | flops 35389440 | bytes 18874368 | tf_op jit(solution)/shard_map/pallas_call | solution.py:214
  (8 shorter events, 0.0 us)
Async XLA Ops:
  0.6 70.1 %collective-permute-start = (f32[1,3,32,64,128]{4,3,2,1,0:T(8,128)}, f32[1,3,32,64,128]{4,3,2,1,0:T(8,128)S(1)}, u32[]{:S(2)}, u32[]{:S(2)}) collective-permute-start(f32[1,3,32,64,128]{4,3,2,1,0:T(8,128)} %s_ref.3), channel_id=1, source_target_pairs={{0,8},{8,0},{16,24},{24,16},{1,9},{9,1},{17,25},{25,17},{2,10},{10... | collective-permute-start | bytes 9437192 | tf_op jit(solution)/shard_map/ppermute | solution.py:183
  2.3 71.7 %collective-permute-start.1 = (f32[1,3,32,64,128]{4,3,2,1,0:T(8,128)}, f32[1,3,32,64,128]{4,3,2,1,0:T(8,128)S(1)}, u32[]{:S(2)}, u32[]{:S(2)}) collective-permute-start(f32[1,3,32,64,128]{4,3,2,1,0:T(8,128)} %s_ref.3), channel_id=1, source_target_pairs={{8,16},{16,8},{9,17},{17,9},{10,18},{18,10},{11,19},{19,11},{12,20... | collective-permute-start | bytes 9437192 | tf_op jit(solution)/shard_map/ppermute | solution.py:184
  5.2 4.1 %collective-permute-start.3 = (f32[1,3,1,64,128]{4,3,2,1,0:T(8,128)S(1)}, f32[1,3,1,64,128]{4,3,2,1,0:T(8,128)S(1)}, u32[]{:S(2)}, u32[]{:S(2)}) collective-permute-start(f32[1,3,1,64,128]{4,3,2,1,0:T(8,128)S(1)} %get-tuple-element.24), channel_id=1, source_target_pairs={{0,2},{2,4},{4,6},{6,0},{1,3},{3,5},{5,7},{7,1},{8,10},{10,12},{12... | collective-permute-start | bytes 294920 | tf_op jit(solution)/shard_map/ppermute | solution.py:24
  5.2 4.1 %collective-permute-start.2 = (f32[1,3,1,64,128]{4,3,2,1,0:T(8,128)S(1)}, f32[1,3,1,64,128]{4,3,2,1,0:T(8,128)S(1)}, u32[]{:S(2)}, u32[]{:S(2)}) collective-permute-start(f32[1,3,1,64,128]{4,3,2,1,0:T(8,128)S(1)} %get-tuple-element.23), channel_id=1, source_target_pairs={{2,0},{4,2},{6,4},{0,6},{3,1},{5,3},{7,5},{1,7},{10,8},{12,10},{14... | collective-permute-start | bytes 294920 | tf_op jit(solution)/shard_map/ppermute | solution.py:27
  9.3 10.5 %copy-start.2 = (f32[3]{0:T(128)S(1)}, f32[3]{0:T(128)}, u32[]{:S(2)}) copy-start(f32[3]{0:T(128)} %constant.6.clone) | copy-start | bytes 40
  17.7 4.2 %collective-permute-start.4 = (f32[1,3,34,1,128]{4,3,2,1,0:T(1,128)S(1)}, f32[1,3,34,1,128]{4,3,2,1,0:T(1,128)S(1)}, u32[]{:S(2)}, u32[]{:S(2)}) collective-permute-start(f32[1,3,34,1,128]{4,3,2,1,0:T(1,128)S(1)} %get-tuple-element.16), channel_id=1, source_target_pairs={{1,0},{0,1},{3,2},{2,3},{5,4},{4,5},{7,6},{6,7},{9,8},{8,9},{11,10... | collective-permute-start | bytes 156680 | tf_op jit(solution)/shard_map/ppermute | solution.py:27
  19.3 4.1 %collective-permute-start.5 = (f32[1,3,34,1,128]{4,3,2,1,0:T(1,128)S(1)}, f32[1,3,34,1,128]{4,3,2,1,0:T(1,128)S(1)}, u32[]{:S(2)}, u32[]{:S(2)}) collective-permute-start(f32[1,3,34,1,128]{4,3,2,1,0:T(1,128)S(1)} %get-tuple-element.15), channel_id=1, source_target_pairs={{0,1},{1,0},{2,3},{3,2},{4,5},{5,4},{6,7},{7,6},{8,9},{9,8},{10,11... | collective-permute-start | bytes 156680 | tf_op jit(solution)/shard_map/ppermute | solution.py:24
  24.2 1.9 %copy-start = (f32[1,3,32,64,128]{4,3,2,1,0:T(8,128)S(1)}, f32[1,3,32,64,128]{4,3,2,1,0:T(8,128)}, u32[]{:S(2)}) copy-start(f32[1,3,32,64,128]{4,3,2,1,0:T(8,128)} %s_ref.3) | copy-start | bytes 9437188
  30.2 43.7 %copy-start.1 = (f32[1,3,32,64,128]{4,3,2,1,0:T(8,128)S(1)}, f32[1,3,32,64,128]{4,3,2,1,0:T(8,128)}, u32[]{:S(2)}) copy-start(f32[1,3,32,64,128]{4,3,2,1,0:T(8,128)} %v_ref.3) | copy-start | bytes 9437188
  76.4 3.7 %collective-permute-start.6 = (f32[1,8,128]{2,1,0:T(8,128)S(1)}, f32[1,8,128]{2,1,0:T(8,128)S(1)}, u32[]{:S(2)}, u32[]{:S(2)}) collective-permute-start(f32[1,8,128]{2,1,0:T(8,128)S(1)} %get-tuple-element.8.a_ref), channel_id=1, source_target_pairs={{0,1},{1,0},{2,3},{3,2},{4,5},{5,4},{6,7},{7,6},{8,9},{9,8},{10,11... | collective-permute-start | bytes 12296 | tf_op jit(solution)/shard_map/ppermute | solution.py:62
  80.0 1.2 %collective-permute-start.7 = (f32[1,8,128]{2,1,0:T(8,128)S(1)}, f32[1,8,128]{2,1,0:T(8,128)S(1)}, u32[]{:S(2)}, u32[]{:S(2)}) collective-permute-start(f32[1,8,128]{2,1,0:T(8,128)S(1)} %shard_map.86.a_ref), channel_id=1, source_target_pairs={{0,2},{2,0},{4,6},{6,4},{1,3},{3,1},{5,7},{7,5},{8,10},{10,8},{12,... | collective-permute-start | bytes 12296 | tf_op jit(solution)/shard_map/ppermute | solution.py:62
  81.2 3.6 %collective-permute-start.8 = (f32[1,8,128]{2,1,0:T(8,128)S(1)}, f32[1,8,128]{2,1,0:T(8,128)S(1)}, u32[]{:S(2)}, u32[]{:S(2)}) collective-permute-start(f32[1,8,128]{2,1,0:T(8,128)S(1)} %shard_map.87.a_ref), channel_id=1, source_target_pairs={{0,4},{2,6},{4,0},{6,2},{1,5},{3,7},{5,1},{7,3},{8,12},{10,14},{12... | collective-permute-start | bytes 12296 | tf_op jit(solution)/shard_map/ppermute | solution.py:62

commit v9 on v8

--- a/solution.py
+++ b/solution.py
@@ -10,9 +10,9 @@
 TIME_STEP = 0.1
 SPRING = 2.0
 EPSILON = 1e-06
-ROWS = 8
+ROWS = 16
 ROWS_A = 8
-VMEM_LIMIT = 8 * 1024 * 1024
+VMEM_LIMIT = 16 * 1024 * 1024
 
 
 def extended(block, sides, width):
@@ -96,30 +96,36 @@
     image = pl.program_id(0)
     step = pl.program_id(1)
     here = pl.ds(pl.multiple_of(step * rows, rows), rows)
-    even = jnp.full((1, 1, 1), lax.axis_index("img") % 2) == 0
+    even = lax.axis_index("img") % 2 == 0
+    up = up_ref[image]
 
     @pl.when(step == 0)
     def _():
         acc_ref[...] = jnp.zeros_like(acc_ref)
 
-    up = up_ref[pl.program_id(0)]
-    ahead = jnp.where(up >= 0, 1.0, 0.0).astype(jnp.float32)
-    behind = jnp.where(up <= 0, 1.0, 0.0).astype(jnp.float32)
-    s = [s_ref[image, c, here] for c in range(3)]
-    first = [first_ref[image, c, here] for c in range(3)]
-    second = [second_ref[image, c, here] for c in range(3)]
-    fwd = [jnp.where(even, first[c], second[c]) - s[c] for c in range(3)]
-    bwd = [s[c] - jnp.where(even, second[c], first[c]) for c in range(3)]
-    raw = [ahead * fwd[c] + behind * bwd[c] for c in range(3)]
-    d = raw[0] * s[0] + raw[1] * s[1] + raw[2] * s[2]
-    tp = [raw[c] - d * s[c] for c in range(3)]
-    for c in range(3):
-        tp_ref[image, c, here] = tp[c]
-    pf = [pf_ref[image, c, here] for c in range(3)]
-    acc_ref[0] += fold(tp[0] * tp[0] + tp[1] * tp[1] + tp[2] * tp[2])
-    acc_ref[1] += fold(pf[0] * tp[0] + pf[1] * tp[1] + pf[2] * tp[2])
-    acc_ref[2] += fold(fwd[0] * fwd[0] + fwd[1] * fwd[1] + fwd[2] * fwd[2])
-    acc_ref[3] += fold(bwd[0] * bwd[0] + bwd[1] * bwd[1] + bwd[2] * bwd[2])
+    def body(nx_ref, pv_ref, mode):
+        s = [s_ref[image, c, here] for c in range(3)]
+        fwd = [nx_ref[image, c, here] - s[c] for c in range(3)]
+        bwd = [s[c] - pv_ref[image, c, here] for c in range(3)]
+        if mode > 0:
+            raw = fwd
+        elif mode < 0:
+            raw = bwd
+        else:
+            raw = [fwd[c] + bwd[c] for c in range(3)]
+        d = raw[0] * s[0] + raw[1] * s[1] + raw[2] * s[2]
+        tp = [raw[c] - d * s[c] for c in range(3)]
+        for c in range(3):
+            tp_ref[image, c, here] = tp[c]
+        pf = [pf_ref[image, c, here] for c in range(3)]
+        acc_ref[0] += fold(tp[0] * tp[0] + tp[1] * tp[1] + tp[2] * tp[2])
+        acc_ref[1] += fold(pf[0] * tp[0] + pf[1] * tp[1] + pf[2] * tp[2])
+        acc_ref[2] += fold(fwd[0] * fwd[0] + fwd[1] * fwd[1] + fwd[2] * fwd[2])
+        acc_ref[3] += fold(bwd[0] * bwd[0] + bwd[1] * bwd[1] + bwd[2] * bwd[2])
+
+    for parity, refs in ((True, (first_ref, second_ref)), (False, (second_ref, first_ref))):
+        for mode, chosen in ((1, up > 0), (-1, up < 0), (0, up == 0)):
+            pl.when((even == parity) & chosen)(functools.partial(body, *refs, mode))
 
     @pl.when(step == pl.num_programs(1) - 1)
     def _():

time: 89.1 us -> 88.5 us (level)
  no operation moved by 1% of the time
where the time goes in v9:
time: 88.5 us; the launch traced here: 88.2 us
  waiting for transfers between devices  50.9 us (58%)
  other arithmetic  15.3 us (17%)
  starting transfers between devices  10.5 us (12%)
  Pallas kernels  5.83 us (7%)
  local copies, waits for them, and re-layouts  3.63 us (4%)
  between operations  2.05 us (2%)
    ppermute x1, waiting for transfers between devices, per_device(): lax.ppermute(spins, 'img', [(i, i ^ 1) for i in range(places) if i ^ 1 <...  39.7 us
    sub x1, other arithmetic, lattice_field(): diff_z = plus_z - minus_z  8.29 us
    ppermute x3, waiting for transfers between devices, group_sum(): value = small_add(value, lax.ppermute(value, axis, pairs))  4.71 us
    reduce_sum x1, other arithmetic, cell_dot(): return jnp.sum(left * right, axis=1, keepdims=True)  4.08 us
    pallas_call x1, Pallas kernels, per_device(): pl.pallas_call(functools.partial(update_kernel, root_cells, rows, total -...  3.74 us
    ppermute x2, starting transfers between devices, extended(): lax.ppermute(lax.slice_in_dim(block, 0, width, axis=dim), axis, backward)  3.32 us
    ppermute x1, waiting for transfers between devices, per_device(): lax.ppermute(spins, 'img', [(i, i - 1 + 2 * (i % 2)) for i in range(1, pl...  3.18 us
    ppermute x3, starting transfers between devices, group_sum(): value = small_add(value, lax.ppermute(value, axis, pairs))  3.08 us
  transfers between devices with their start and end apart: 9, of which 8 were waited for; matrix products, arithmetic and copies ran while one was open for 20% of the time, Pallas kernels for 0%

profile of v9, /device:TPU:16, one launch (start us, length us, event | category | flops | bytes accessed | tf_op | source)
XLA Modules:
  0.0 88.2 jit_solution(13724377743995745845)
XLA Ops:
  0.6 1.6 %collective-permute-start = (f32[1,3,32,64,128]{4,3,2,1,0:T(8,128)}, f32[1,3,32,64,128]{4,3,2,1,0:T(8,128)S(1)}, u32[]{:S(2)}, u32[]{:S(2)}) collective-permute-start(f32[1,3,32,64,128]{4,3,2,1,0:T(8,128)} %s_ref.3), channel_id=1, source_target_pairs={{0,8},{8,0},{16,24},{24,16},{1,9},{9,1},{17,25},{25,17},{2,10},{10... | collective-permute-start | bytes 9437192 | tf_op jit(solution)/shard_map/ppermute | solution.py:189
  2.3 1.9 %collective-permute-start.1 = (f32[1,3,32,64,128]{4,3,2,1,0:T(8,128)}, f32[1,3,32,64,128]{4,3,2,1,0:T(8,128)S(1)}, u32[]{:S(2)}, u32[]{:S(2)}) collective-permute-start(f32[1,3,32,64,128]{4,3,2,1,0:T(8,128)} %s_ref.3), channel_id=1, source_target_pairs={{8,16},{16,8},{9,17},{17,9},{10,18},{18,10},{11,19},{19,11},{12,20... | collective-permute-start | bytes 9437192 | tf_op jit(solution)/shard_map/ppermute | solution.py:190
  4.2 1.0 %fusion.7 = (f32[1,3,1,64,128]{4,3,2,1,0:T(8,128)S(1)}, f32[1,3,1,64,128]{4,3,2,1,0:T(8,128)S(1)}) fusion(f32[1,3,32,64,128]{4,3,2,1,0:T(8,128)} %s_ref.3), kind=kLoop, calls=%fused_computation.22 | loop fusion | bytes 393216 | tf_op jit(solution)/shard_map/slice | solution.py:27
  5.2 0.1 collective-permute-start.3
  5.2 1.7 %collective-permute-start.2 = (f32[1,3,1,64,128]{4,3,2,1,0:T(8,128)S(1)}, f32[1,3,1,64,128]{4,3,2,1,0:T(8,128)S(1)}, u32[]{:S(2)}, u32[]{:S(2)}) collective-permute-start(f32[1,3,1,64,128]{4,3,2,1,0:T(8,128)S(1)} %get-tuple-element.23), channel_id=1, source_target_pairs={{2,0},{4,2},{6,4},{0,6},{3,1},{5,3},{7,5},{1,7},{10,8},{12,10},{14... | collective-permute-start | bytes 294920 | tf_op jit(solution)/shard_map/ppermute | solution.py:27
  7.0 1.4 %fusion.8 = (f32[1]{0:T(128)}, f32[1]{0:T(128)}, f32[1]{0:T(128)}) fusion(f32[3]{0:T(128)} %param.10), kind=kLoop, calls=%fused_computation.23 | loop fusion | bytes 24 | tf_op jit(solution)/shard_map/slice | solution.py:88
  8.3 0.9 %collective-permute-done.3 = f32[1,3,1,64,128]{4,3,2,1,0:T(8,128)S(1)} collective-permute-done((f32[1,3,1,64,128]{4,3,2,1,0:T(8,128)S(1)}, f32[1,3,1,64,128]{4,3,2,1,0:T(8,128)S(1)}, u32[]{:S(2)}, u32[]{:S(2)}) %collective-permute-start.3) | collective-permute-done | bytes 98336 | tf_op jit(solution)/shard_map/ppermute | solution.py:24
  9.3 0.0 copy-start.2
  9.3 0.0 collective-permute-done.2
  9.3 8.3 %fusion.2 = (f32[1,3,32,64,128]{4,3,2,1,0:T(8,128)S(1)}, f32[1,3,34,64,128]{4,3,2,1,0:T(8,128)S(1)}, f32[1,3,32,64,128]{4,3,2,1,0:T(8,128)S(1)}) fusion(f32[1,3,32,64,128]{4,3,2,1,0:T(8,128)} %s_ref.3, f32[1,3,34,64,128]{4,3,2,1,0:T(8,128)S(1)} %constant_dynamic-update-slice_fusion.2, f32[1,3,1,64,128]{4,3,2,1,0:T(8,128)S(1)} %collective-permute-done.3, ...), kind=kLoop, calls=%fused_computation.11 | loop fusion | flops 3145728 | bytes 12779520 | tf_op jit(solution)/shard_map/sub | solution.py:82
  17.6 0.1 fusion.6
  17.7 1.6 %collective-permute-start.4 = (f32[1,3,34,1,128]{4,3,2,1,0:T(1,128)S(1)}, f32[1,3,34,1,128]{4,3,2,1,0:T(1,128)S(1)}, u32[]{:S(2)}, u32[]{:S(2)}) collective-permute-start(f32[1,3,34,1,128]{4,3,2,1,0:T(1,128)S(1)} %get-tuple-element.16), channel_id=1, source_target_pairs={{1,0},{0,1},{3,2},{2,3},{5,4},{4,5},{7,6},{6,7},{9,8},{8,9},{11,10... | collective-permute-start | bytes 156680 | tf_op jit(solution)/shard_map/ppermute | solution.py:27
  19.3 0.5 collective-permute-start.5
  19.8 0.6 broadcast_multiply_fusion
  21.1 0.8 collective-permute-done.4
  21.9 1.5 %collective-permute-done.5 = f32[1,3,34,1,128]{4,3,2,1,0:T(1,128)S(1)} collective-permute-done((f32[1,3,34,1,128]{4,3,2,1,0:T(1,128)S(1)}, f32[1,3,34,1,128]{4,3,2,1,0:T(1,128)S(1)}, u32[]{:S(2)}, u32[]{:S(2)}) %collective-permute-start.5) | collective-permute-done | bytes 52256 | tf_op jit(solution)/shard_map/ppermute | solution.py:24
  23.4 0.8 fusion.4
  24.2 0.0 copy-start
  24.2 0.7 slice_subtract_fusion.2
  24.9 1.2 %copy-done = f32[1,3,32,64,128]{4,3,2,1,0:T(8,128)S(1)} copy-done((f32[1,3,32,64,128]{4,3,2,1,0:T(8,128)S(1)}, f32[1,3,32,64,128]{4,3,2,1,0:T(8,128)}, u32[]{:S(2)}) %copy-start) | copy-done | bytes 3145752
  26.1 4.1 %multiply_reduce_fusion = (f32[32,64,128]{2,1,0:T(8,128)S(1)}, f32[1,3,32,64,128]{4,3,2,1,0:T(8,128)S(1)}) fusion(f32[1,3,32,64,128]{4,3,2,1,0:T(8,128)S(1)} %copy-done, f32[3]{0:T(128)S(1)} %broadcast_multiply_fusion, f32[1,1,32,64,128]{4,3,2,1,0:T(8,128)S(1)} %get-tuple-element.18, f32[1,1,32,64,128]{4,3,2,1,0:T(8,128)S(1)} %get-tuple-element.19, ...), kind=kLoop, calls=%fused_computation.10 | loop fusion | flops 13107200 | bytes 14129172 | tf_op jit(solution)/shard_map/reduce_sum | solution.py:68
  30.2 0.0 copy-start.1
  30.2 0.8 multiply_subtract_fusion.pf_ref
  31.0 39.7 %collective-permute-done.first_ref = f32[1,3,32,64,128]{4,3,2,1,0:T(8,128)S(1)} collective-permute-done((f32[1,3,32,64,128]{4,3,2,1,0:T(8,128)}, f32[1,3,32,64,128]{4,3,2,1,0:T(8,128)S(1)}, u32[]{:S(2)}, u32[]{:S(2)}) %collective-permute-start) | collective-permute-done | bytes 3145760 | tf_op jit(solution)/shard_map/ppermute | solution.py:189
  70.7 3.2 %collective-permute-done.1.second_ref = f32[1,3,32,64,128]{4,3,2,1,0:T(8,128)S(1)} collective-permute-done((f32[1,3,32,64,128]{4,3,2,1,0:T(8,128)}, f32[1,3,32,64,128]{4,3,2,1,0:T(8,128)S(1)}, u32[]{:S(2)}, u32[]{:S(2)}) %collective-permute-start.1) | collective-permute-done | bytes 3145760 | tf_op jit(solution)/shard_map/ppermute | solution.py:190
  73.9 2.1 %shard_map.85 = (f32[1,3,32,64,128]{4,3,2,1,0:T(8,128)S(1)}, f32[1,8,128]{2,1,0:T(8,128)S(1)}) custom-call(s32[1]{0:T(128)S(6)} %copy.11.up_ref, f32[1,3,32,64,128]{4,3,2,1,0:T(8,128)S(1)} %copy-done, f32[1,3,32,64,128]{4,3,2,1,0:T(8,128)S(1)} %collective-permute-done.first_ref, f32[1,3,32,64,128]{4,3,2,1,0:T(8,128)S(1)} %collective-permute-done.1.second_ref, ...), custom_call_target="tpu_custom_call" | custom-call | flops 31457280 | bytes 15728640 | tf_op jit(solution)/shard_map/pallas_call | solution.py:208
  76.0 1.6 %collective-permute-start.6 = (f32[1,8,128]{2,1,0:T(8,128)S(1)}, f32[1,8,128]{2,1,0:T(8,128)S(1)}, u32[]{:S(2)}, u32[]{:S(2)}) collective-permute-start(f32[1,8,128]{2,1,0:T(8,128)S(1)} %get-tuple-element.8.a_ref), channel_id=1, source_target_pairs={{0,1},{1,0},{2,3},{3,2},{4,5},{5,4},{6,7},{7,6},{8,9},{9,8},{10,11... | collective-permute-start | bytes 12296 | tf_op jit(solution)/shard_map/ppermute | solution.py:62
  77.6 2.1 %collective-permute-done.6.b_ref = f32[1,8,128]{2,1,0:T(8,128)S(1)} collective-permute-done((f32[1,8,128]{2,1,0:T(8,128)S(1)}, f32[1,8,128]{2,1,0:T(8,128)S(1)}, u32[]{:S(2)}, u32[]{:S(2)}) %collective-permute-start.6) | collective-permute-done | bytes 4128 | tf_op jit(solution)/shard_map/ppermute | solution.py:62
  79.7 1.2 %collective-permute-done.7.b_ref = f32[1,8,128]{2,1,0:T(8,128)S(1)} collective-permute-done((f32[1,8,128]{2,1,0:T(8,128)S(1)}, f32[1,8,128]{2,1,0:T(8,128)S(1)}, u32[]{:S(2)}, u32[]{:S(2)}) %collective-permute-start.7) | collective-permute-done | bytes 4128 | tf_op jit(solution)/shard_map/ppermute | solution.py:62
  80.9 1.5 %collective-permute-start.8 = (f32[1,8,128]{2,1,0:T(8,128)S(1)}, f32[1,8,128]{2,1,0:T(8,128)S(1)}, u32[]{:S(2)}, u32[]{:S(2)}) collective-permute-start(f32[1,8,128]{2,1,0:T(8,128)S(1)} %shard_map.87.a_ref), channel_id=1, source_target_pairs={{0,4},{2,6},{4,0},{6,2},{1,5},{3,7},{5,1},{7,3},{8,12},{10,14},{12... | collective-permute-start | bytes 12296 | tf_op jit(solution)/shard_map/ppermute | solution.py:62
  83.0 1.5 %collective-permute-done.8.b_ref = f32[1,8,128]{2,1,0:T(8,128)S(1)} collective-permute-done((f32[1,8,128]{2,1,0:T(8,128)S(1)}, f32[1,8,128]{2,1,0:T(8,128)S(1)}, u32[]{:S(2)}, u32[]{:S(2)}) %collective-permute-start.8) | collective-permute-done | bytes 4128 | tf_op jit(solution)/shard_map/ppermute | solution.py:62
  84.5 3.7 %shard_map.89 = (f32[1,3,32,64,128]{4,3,2,1,0:T(8,128)}, f32[1,3,32,64,128]{4,3,2,1,0:T(8,128)}, f32[1,1,2]{2,1,0:T(1,128)}) custom-call(s32[1]{0:T(128)S(6)} %copy.12.climber_ref, f32[1,8,128]{2,1,0:T(8,128)S(1)} %shard_map.88.sums_ref, f32[1,3,32,64,128]{4,3,2,1,0:T(8,128)S(1)} %copy-done, f32[1,3,32,64,128]{4,3,2,1,0:T(8,128)S(1)} %copy-done.1, ...), custom_call_target="tpu_custom_call" | custom-call | flops 35389440 | bytes 18874368 | tf_op jit(solution)/shard_map/pallas_call | solution.py:220
  (8 shorter events, 0.0 us)
Async XLA Ops:
  0.6 70.1 %collective-permute-start = (f32[1,3,32,64,128]{4,3,2,1,0:T(8,128)}, f32[1,3,32,64,128]{4,3,2,1,0:T(8,128)S(1)}, u32[]{:S(2)}, u32[]{:S(2)}) collective-permute-start(f32[1,3,32,64,128]{4,3,2,1,0:T(8,128)} %s_ref.3), channel_id=1, source_target_pairs={{0,8},{8,0},{16,24},{24,16},{1,9},{9,1},{17,25},{25,17},{2,10},{10... | collective-permute-start | bytes 9437192 | tf_op jit(solution)/shard_map/ppermute | solution.py:189
  2.3 71.7 %collective-permute-start.1 = (f32[1,3,32,64,128]{4,3,2,1,0:T(8,128)}, f32[1,3,32,64,128]{4,3,2,1,0:T(8,128)S(1)}, u32[]{:S(2)}, u32[]{:S(2)}) collective-permute-start(f32[1,3,32,64,128]{4,3,2,1,0:T(8,128)} %s_ref.3), channel_id=1, source_target_pairs={{8,16},{16,8},{9,17},{17,9},{10,18},{18,10},{11,19},{19,11},{12,20... | collective-permute-start | bytes 9437192 | tf_op jit(solution)/shard_map/ppermute | solution.py:190
  5.2 4.1 %collective-permute-start.3 = (f32[1,3,1,64,128]{4,3,2,1,0:T(8,128)S(1)}, f32[1,3,1,64,128]{4,3,2,1,0:T(8,128)S(1)}, u32[]{:S(2)}, u32[]{:S(2)}) collective-permute-start(f32[1,3,1,64,128]{4,3,2,1,0:T(8,128)S(1)} %get-tuple-element.24), channel_id=1, source_target_pairs={{0,2},{2,4},{4,6},{6,0},{1,3},{3,5},{5,7},{7,1},{8,10},{10,12},{12... | collective-permute-start | bytes 294920 | tf_op jit(solution)/shard_map/ppermute | solution.py:24
  5.2 4.1 %collective-permute-start.2 = (f32[1,3,1,64,128]{4,3,2,1,0:T(8,128)S(1)}, f32[1,3,1,64,128]{4,3,2,1,0:T(8,128)S(1)}, u32[]{:S(2)}, u32[]{:S(2)}) collective-permute-start(f32[1,3,1,64,128]{4,3,2,1,0:T(8,128)S(1)} %get-tuple-element.23), channel_id=1, source_target_pairs={{2,0},{4,2},{6,4},{0,6},{3,1},{5,3},{7,5},{1,7},{10,8},{12,10},{14... | collective-permute-start | bytes 294920 | tf_op jit(solution)/shard_map/ppermute | solution.py:27
  9.3 10.5 %copy-start.2 = (f32[3]{0:T(128)S(1)}, f32[3]{0:T(128)}, u32[]{:S(2)}) copy-start(f32[3]{0:T(128)} %constant.6.clone) | copy-start | bytes 40
  17.7 4.2 %collective-permute-start.4 = (f32[1,3,34,1,128]{4,3,2,1,0:T(1,128)S(1)}, f32[1,3,34,1,128]{4,3,2,1,0:T(1,128)S(1)}, u32[]{:S(2)}, u32[]{:S(2)}) collective-permute-start(f32[1,3,34,1,128]{4,3,2,1,0:T(1,128)S(1)} %get-tuple-element.16), channel_id=1, source_target_pairs={{1,0},{0,1},{3,2},{2,3},{5,4},{4,5},{7,6},{6,7},{9,8},{8,9},{11,10... | collective-permute-start | bytes 156680 | tf_op jit(solution)/shard_map/ppermute | solution.py:27
  19.3 4.1 %collective-permute-start.5 = (f32[1,3,34,1,128]{4,3,2,1,0:T(1,128)S(1)}, f32[1,3,34,1,128]{4,3,2,1,0:T(1,128)S(1)}, u32[]{:S(2)}, u32[]{:S(2)}) collective-permute-start(f32[1,3,34,1,128]{4,3,2,1,0:T(1,128)S(1)} %get-tuple-element.15), channel_id=1, source_target_pairs={{0,1},{1,0},{2,3},{3,2},{4,5},{5,4},{6,7},{7,6},{8,9},{9,8},{10,11... | collective-permute-start | bytes 156680 | tf_op jit(solution)/shard_map/ppermute | solution.py:24
  24.2 1.9 %copy-start = (f32[1,3,32,64,128]{4,3,2,1,0:T(8,128)S(1)}, f32[1,3,32,64,128]{4,3,2,1,0:T(8,128)}, u32[]{:S(2)}) copy-start(f32[1,3,32,64,128]{4,3,2,1,0:T(8,128)} %s_ref.3) | copy-start | bytes 9437188
  30.2 43.7 %copy-start.1 = (f32[1,3,32,64,128]{4,3,2,1,0:T(8,128)S(1)}, f32[1,3,32,64,128]{4,3,2,1,0:T(8,128)}, u32[]{:S(2)}) copy-start(f32[1,3,32,64,128]{4,3,2,1,0:T(8,128)} %v_ref.3) | copy-start | bytes 9437188
  76.0 3.7 %collective-permute-start.6 = (f32[1,8,128]{2,1,0:T(8,128)S(1)}, f32[1,8,128]{2,1,0:T(8,128)S(1)}, u32[]{:S(2)}, u32[]{:S(2)}) collective-permute-start(f32[1,8,128]{2,1,0:T(8,128)S(1)} %get-tuple-element.8.a_ref), channel_id=1, source_target_pairs={{0,1},{1,0},{2,3},{3,2},{4,5},{5,4},{6,7},{7,6},{8,9},{9,8},{10,11... | collective-permute-start | bytes 12296 | tf_op jit(solution)/shard_map/ppermute | solution.py:62
  79.7 1.2 %collective-permute-start.7 = (f32[1,8,128]{2,1,0:T(8,128)S(1)}, f32[1,8,128]{2,1,0:T(8,128)S(1)}, u32[]{:S(2)}, u32[]{:S(2)}) collective-permute-start(f32[1,8,128]{2,1,0:T(8,128)S(1)} %shard_map.86.a_ref), channel_id=1, source_target_pairs={{0,2},{2,0},{4,6},{6,4},{1,3},{3,1},{5,7},{7,5},{8,10},{10,8},{12,... | collective-permute-start | bytes 12296 | tf_op jit(solution)/shard_map/ppermute | solution.py:62
  80.9 3.6 %collective-permute-start.8 = (f32[1,8,128]{2,1,0:T(8,128)S(1)}, f32[1,8,128]{2,1,0:T(8,128)S(1)}, u32[]{:S(2)}, u32[]{:S(2)}) collective-permute-start(f32[1,8,128]{2,1,0:T(8,128)S(1)} %shard_map.87.a_ref), channel_id=1, source_target_pairs={{0,4},{2,6},{4,0},{6,2},{1,5},{3,7},{5,1},{7,3},{8,12},{10,14},{12... | collective-permute-start | bytes 12296 | tf_op jit(solution)/shard_map/ppermute | solution.py:62
